TPU v7x, 128 devices: a whole 4x4x4 slice. The times are simulated.
128 devices in a mesh: req: 32 (over x, y_hi, z), exp: 4 (over y_lo, core).
Axes of the slice: x: 4, y: 4 (y_hi: 2, y_lo: 2; y = y_hi * 2 + y_lo), z: 4, core: 2. Of those that a mesh axis runs over, the one named last changes fastest.
Arguments:
- tokens: bfloat16 [8192, 1024], P('req', 'exp'), may hold values from -7.2 to 7.2
- lengths: int32 [32, 4], P('req'), may hold values from 1 to 128, 256 in all within a row
- groups: int32 [32, 4], P('req'), may hold values from 0 to 3
- owners: int32 [4], replicated, may hold values from 0 to 31, as said below
- prefix_cache: bfloat16 [32, 2048, 2, 1024], P('req', None, None, 'exp'), may hold values from -102 to 102
- attn_gain: float32 [1024], replicated, may hold values from 0.1 to 1.9
- w_qkv: bfloat16 [1024, 3, 1024], P(None, None, 'exp'), may hold values from -0.3125 to 0.3125
- w_out: bfloat16 [1024, 1024], P('exp'), may hold values from -0.1875 to 0.1875
- moe_gain: float32 [1024], replicated, may hold values from 0.1 to 1.9
- w_router: bfloat16 [1024, 16], replicated, may hold values from -0.375 to 0.375
- expert_ids: int32 [8192, 2], P('req'), may hold values from 0 to 15, all different within a row; in each aligned block of 256 rows (0 to 255, 256 to 511, ...) at most 80 rows name the same one
- w_in: bfloat16 [32, 1024, 2, 1408], P('req', None, None, 'exp'), may hold values from -0.1875 to 0.1875
- w_down: bfloat16 [32, 1408, 1024], P('req', 'exp'), may hold values from -0.109375 to 0.109375
Outputs:
- hidden_out: bfloat16 [8192, 1024], P('req', 'exp')
- suffix_kv: bfloat16 [8192, 2, 1024], P('req', None, 'exp')
Inputs may be any that keep to these rules, and one draw needn't show every extreme that they name: The 4 lengths of each row sum to 256. `owners`: distinct slots. `expert_ids`: the two experts of a token differ; among the rows of one index of req no expert is named more than 80 times, and some expert exactly that often in some blocks.
All inputs are finite; a program needn't handle non-finite values.
Results may differ from a plain program's by a relative error of at most 0.014.
The roundings to bfloat16 on the way count: a program that leaves them out, or rounds other values in their place, can miss the bound.
Values may be sent and summed in bfloat16 or wider, within the bound.
No kernel may reach another device: no remote copies, remote signals or barrier semaphores. Data moves between devices by JAX's collectives and lax.ppermute only.
A program may use at most 128 MiB of HBM per device.

v0:
```python
import math

import jax
import jax.numpy as jnp
from jax import lax
from jax.sharding import PartitionSpec as P

HEAD_DIM = 64
EXPERTS = 16
TOP = 2
SPLIT = 2
GROUPS = 4
PREFIX = 2048
REQ_DEV = 4
SUF_MOST = 128
CAP = 40


epsilon = 1e-06


def spread(shard, axis, root):
    mine = lax.axis_index(axis) == root
    return lax.psum(jnp.where(mine, shard, jnp.zeros_like(shard)), axis)


def norm_rows(values, gain):
    squares = jnp.sum(values * values, axis=1)
    return values * lax.rsqrt(squares / values.shape[1] + epsilon)[:, None] * gain


def request_context(query_all, key_all, value_all, prefix_kv, start, length, window):
    row_count = query_all.shape[0]
    first = jnp.minimum(start, row_count - window)
    query_win = lax.dynamic_slice_in_dim(query_all, first, window, 0)
    key_win = lax.dynamic_slice_in_dim(key_all, first, window, 0)
    value_win = lax.dynamic_slice_in_dim(value_all, first, window, 0)
    keys = jnp.concatenate([prefix_kv[:, 0], key_win], axis=0)
    values = jnp.concatenate([prefix_kv[:, 1], value_win], axis=0)
    scores = jnp.einsum(
        "qhd,khd->hqk", query_win, keys, preferred_element_type=jnp.float32
    ) / math.sqrt(query_all.shape[2])
    positions = first + jnp.arange(window, dtype=jnp.int32)
    suffix_ok = (positions[None, :] <= positions[:, None]) & (positions[None, :] >= start)
    allowed = jnp.concatenate([jnp.ones((window, prefix_kv.shape[0]), bool), suffix_ok], axis=1)
    scores = jnp.where(allowed[None], scores, -1e30)
    highest = jnp.max(scores, axis=-1, keepdims=True)
    weight = jnp.exp(scores - highest)
    totals = jnp.sum(weight, axis=-1)
    context = jnp.einsum(
        "hqk,khd->qhd", weight.astype(jnp.bfloat16), values, preferred_element_type=jnp.float32
    )
    context = context / jnp.transpose(totals)[:, :, None]
    inside = (positions >= start) & (positions < start + length)
    context = context * inside[:, None, None].astype(jnp.float32)
    placed = jnp.zeros((row_count,) + context.shape[1:], jnp.float32)
    return lax.dynamic_update_slice_in_dim(placed, context, first, 0)


def slot_ranks(identity, experts):
    flat_ids = identity.reshape(-1)
    hits = (flat_ids[:, None] == jnp.arange(experts, dtype=jnp.int32)[None, :]).astype(jnp.int32)
    before = jnp.cumsum(hits, axis=0) - hits
    return (flat_ids, jnp.sum(before * hits, axis=1))


def slot_table(flat_ids, ranks, capacity, experts, row_count, topk):
    kept = ranks < capacity
    target = jnp.where(kept, flat_ids * capacity + ranks, experts * capacity)
    source = jnp.arange(flat_ids.shape[0], dtype=jnp.int32) // topk
    table = (
        jnp.full((experts * capacity,), row_count, jnp.int32).at[target].set(source, mode="drop")
    )
    return (kept, table)


def expert_apply(slots, weight_in, weight_down):
    joined = jnp.einsum("slcd,ldgh->slcgh", slots, weight_in, preferred_element_type=jnp.float32)
    units = (jax.nn.gelu(joined[:, :, :, 0], approximate=True) * joined[:, :, :, 1]).astype(
        jnp.bfloat16
    )
    return jnp.einsum("slch,lhd->slcd", units, weight_down, preferred_element_type=jnp.float32)


def shards(
    tokens,
    lengths,
    groups,
    owners,
    prefix_cache,
    attn_gain,
    w_qkv,
    w_out,
    moe_gain,
    w_router,
    expert_ids,
    w_in,
    w_down,
):
    rows_whole = lax.all_gather(tokens, "exp", axis=1, tiled=True)
    row_count = rows_whole.shape[0]
    full_width = rows_whole.shape[1]
    quarter = tokens.shape[1]
    local_heads = quarter // HEAD_DIM
    x_attn = norm_rows(rows_whole.astype(jnp.float32), attn_gain).astype(jnp.bfloat16)
    qkv = jnp.dot(
        x_attn, w_qkv.reshape(full_width, 3 * quarter), preferred_element_type=jnp.float32
    )
    qkv = qkv.astype(jnp.bfloat16).reshape(row_count, 3, quarter)
    suffix_kv = jnp.stack([qkv[:, 1], qkv[:, 2]], axis=1)
    query_all = qkv[:, 0].reshape(row_count, local_heads, HEAD_DIM)
    key_all = qkv[:, 1].reshape(row_count, local_heads, HEAD_DIM)
    value_all = qkv[:, 2].reshape(row_count, local_heads, HEAD_DIM)
    own_slot = prefix_cache[0]
    block_lengths = lengths[0]
    block_groups = groups[0]
    starts = jnp.cumsum(block_lengths) - block_lengths
    context = jnp.zeros((row_count, local_heads, HEAD_DIM), jnp.float32)
    arrived = []
    for prefix_group in range(GROUPS):
        arrived.append(spread(own_slot, "req", owners[prefix_group]))
    cached = jnp.stack(arrived, axis=0)
    for request in range(REQ_DEV):
        prefix_kv = cached[block_groups[request]].reshape(PREFIX, 2, local_heads, HEAD_DIM)
        context = context + request_context(
            query_all,
            key_all,
            value_all,
            prefix_kv,
            starts[request],
            block_lengths[request],
            SUF_MOST,
        )
    context = context.reshape(row_count, quarter).astype(jnp.bfloat16)
    partial_attn = jnp.dot(context, w_out, preferred_element_type=jnp.float32)
    resid = tokens.astype(jnp.float32) + lax.psum_scatter(
        partial_attn.astype(jnp.bfloat16), "exp", scatter_dimension=1, tiled=True
    ).astype(jnp.float32)
    squares = lax.psum(jnp.sum(resid * resid, axis=1), "exp")
    column_start = lax.axis_index("exp") * quarter
    gain_part = lax.dynamic_slice_in_dim(moe_gain, column_start, quarter, 0)
    x_part = (resid * lax.rsqrt(squares / full_width + epsilon)[:, None] * gain_part).astype(
        jnp.bfloat16
    )
    x_source = lax.all_gather(x_part, "exp", axis=1, tiled=True)
    logits = jnp.dot(x_source, w_router, preferred_element_type=jnp.float32)
    gates = jax.nn.sigmoid(jnp.take_along_axis(logits, expert_ids, axis=1)).reshape(-1)
    flat_ids, ranks = slot_ranks(expert_ids, EXPERTS)
    kept, table = slot_table(flat_ids, ranks, CAP, EXPERTS, row_count, TOP)
    columns = x_source.shape[1]
    padded = jnp.concatenate([x_source, jnp.zeros((1, columns), x_source.dtype)], axis=0)
    picked = padded[table].reshape(EXPERTS, 1, CAP, columns)
    req_total = lax.axis_size("req")
    local_rows = EXPERTS * SPLIT // req_total
    outgoing_rows = jnp.broadcast_to(picked, (EXPERTS, SPLIT, CAP, columns)).reshape(
        req_total, local_rows, CAP, columns
    )
    partial_out = expert_apply(
        lax.all_to_all(outgoing_rows, "req", split_axis=0, concat_axis=0, tiled=True), w_in, w_down
    )
    returned = lax.all_to_all(
        partial_out.astype(jnp.bfloat16), "req", split_axis=0, concat_axis=0, tiled=True
    ).astype(partial_out.dtype)
    out_columns = returned.shape[3]
    summed = jnp.sum(returned.reshape(EXPERTS, SPLIT, CAP, out_columns), axis=1).reshape(
        EXPERTS * CAP, out_columns
    )
    source = flat_ids * CAP + jnp.minimum(ranks, CAP - 1)
    chosen = summed[source].reshape(row_count, TOP, out_columns)
    scale = jnp.where(kept, gates, 0.0).reshape(row_count, TOP)
    mixture = jnp.sum(chosen * scale[:, :, None], axis=1)
    moe_part = lax.psum_scatter(
        mixture.astype(jnp.bfloat16), "exp", scatter_dimension=1, tiled=True
    ).astype(jnp.float32)
    hidden_out = (resid + moe_part).astype(jnp.bfloat16)
    return (hidden_out, suffix_kv)


def solution(mesh):
    return jax.shard_map(
        shards,
        mesh=mesh,
        in_specs=(
            P("req", "exp"),
            P("req", None),
            P("req", None),
            P(),
            P("req", None, None, "exp"),
            P(),
            P(None, None, "exp"),
            P("exp", None),
            P(),
            P(),
            P("req", None),
            P("req", None, None, "exp"),
            P("req", "exp", None),
        ),
        out_specs=(P("req", "exp"), P("req", None, "exp")),
        check_vma=False,
    )
```

profile of v0, /device:TPU:1, one launch (start us, length us, event | category | flops | bytes accessed | tf_op | source)
XLA Modules:
  0.0 647.7 jit_solution(16617910004213075310)
XLA Ops:
  7.2 1.5 fusion.154
  11.3 8.2 %broadcast_select_fusion = (bf16[1,2048,2,256]{3,2,1,0:T(2,128)(2,1)}, bf16[1,2048,2,256]{3,2,1,0:T(2,128)(2,1)}, bf16[1,2048,2,256]{3,2,1,0:T(2,128)(2,1)}, bf16[1,2048,2,256]{3,2,1,0:T(2,128)(2,1)}) fusion(bf16[1,2048,2,256]{3,2,1,0:T(2,128)(2,1)} %param.17, pred[]{:T(512)S(6)} %eq.40, pred[]{:T(512)S(6)} %eq.38, pred[]{:T(512)S(6)} %eq.37, pred[]{:T(512)S(6)} %eq.39), kind=kLoop, calls=%fused_computation.17 | loop fusion | flops 4194304 | bytes 10485764 | tf_op jit(solution)/shard_map/jit(_where)/select_n | solution.py:24
  29.3 1.7 copy.57
  31.1 10.1 %all_gather.6 = bf16[256,1024]{1,0:T(8,128)(2,1)S(1)} all-gather(bf16[256,256]{1,0:T(8,128)(2,1)S(1)} %copy-done.9), channel_id=1, replica_groups=mesh['req'=32,'exp'=4] {'exp'}, dimensions={1}, use_global_device_ids=true | all-gather | bytes 655360 | tf_op jit(solution)/shard_map/all_gather | solution.py:100
  41.4 2.1 convolution_convert_fusion.1
  47.7 0.8 concatenate.49
  49.3 0.8 concatenate.46
  52.1 0.8 concatenate.43
  54.3 1.2 and_convert_fusion.3
  55.6 0.8 concatenate.40
  56.7 2.2 reduce-window.20
  62.1 1.1 constant_dynamic-slice_fusion
  63.2 327.3 %all-reduce.8.cloned.1.call-done = (bf16[1,2048,2,256]{3,2,1,0:T(2,128)(2,1)}, bf16[1,2048,2,256]{3,2,1,0:T(2,128)(2,1)}, bf16[1,2048,2,256]{3,2,1,0:T(2,128)(2,1)}, bf16[1,2048,2,256]{3,2,1,0:T(2,128)(2,1)}) async-done(((bf16[1,2048,2,256]{3,2,1,0:T(2,128)(2,1)}, bf16[1,2048,2,256]{3,2,1,0:T(2,128)(2,1)}, bf16[1,2048,2,256]{3,2,1,0:T(2,128)(2,1)}, bf16[1,2048,2,256]{3,2,1,0:T(2,128)(2,1)}), ...) | async-done | bytes 8388624 | tf_op jit(solution)/shard_map/psum | solution.py:24
  390.5 3.4 constant_dynamic-update-slice_fusion.3
  393.9 1.6 constant_dynamic-update-slice_fusion.2
  395.6 1.6 constant_dynamic-update-slice_fusion.1
  397.3 1.6 constant_dynamic-update-slice_fusion
  398.9 6.8 %constant_dynamic-slice_fusion.2 = (bf16[1,2048,2,256]{3,2,1,0:T(2,128)(2,1)}, bf16[1,2048,2,256]{3,2,1,0:T(2,128)(2,1)}, bf16[1,2048,2,256]{3,2,1,0:T(2,128)(2,1)}, bf16[1,2048,2,256]{3,2,1,0:T(2,128)(2,1)S(1)}) fusion(bf16[4,2048,2,256]{3,2,1,0:T(2,128)(2,1)S(1)} %constant_dynamic-update-slice_fusion, s32[]{:T(128)S(6)} %select_n.168, s32[]{:T(128)S(6)} %select_n.165, ...), kind=kLoop, calls=%fused_computation.147 | loop fusion | bytes 16777232 | tf_op jit(solution)/shard_map/dynamic_slice | solution.py:124
  405.7 6.2 copy.61
  411.9 3.1 slice_bitcast_fusion.1
  415.1 6.2 copy.60
  421.3 3.1 slice_bitcast_fusion.3
  424.4 6.2 copy.59
  430.6 3.1 slice_bitcast_fusion.5
  433.7 4.7 copy.56
  438.4 1.8 slice_bitcast_fusion.7
  440.3 1.2 fusion.156
  441.6 0.7 fusion.6
  442.3 1.3 copy-done.2
  443.6 1.2 fusion.155
  444.8 0.7 fusion.4
  445.6 1.0 fusion.45
  447.2 3.3 fusion.57
  450.6 1.3 add.272
  451.9 2.4 fusion.157
  454.4 0.7 fusion.8
  455.6 1.0 fusion.69
  457.0 1.2 fusion.158
  459.4 1.0 fusion.81
  460.9 1.1 convolution_convert_fusion
  462.8 0.8 dynamic_slice.67
  463.6 2.4 scatter_custom_fusion
  466.1 34.6 %reduce-scatter.3.cloned.1.call-done = bf16[256,256]{1,0:T(8,128)(2,1)} async-done(((bf16[256,1024]{1,0:T(8,128)(2,1)}), bf16[256,256]{1,0:T(8,128)(2,1)}) %reduce-scatter.3.cloned.1.call-update) | async-done | bytes 131088 | tf_op jit(solution)/shard_map/reduce_scatter | solution.py:136
  500.7 1.0 multiply_reduce_fusion.1
  501.7 5.1 psum.39
  506.8 1.0 multiply_convert_fusion
  507.9 8.2 %all_gather.7 = bf16[256,1024]{1,0:T(8,128)(2,1)S(1)} all-gather(bf16[256,256]{1,0:T(8,128)(2,1)S(1)} %multiply_convert_fusion), channel_id=1, replica_groups=mesh['req'=32,'exp'=4] {'exp'}, dimensions={1}, use_global_device_ids=true | all-gather | bytes 655360 | tf_op jit(solution)/shard_map/all_gather | solution.py:145
  516.1 0.8 copy-done.3
  516.9 2.8 gather_fusion
  520.2 43.0 %all_to_all.10 = bf16[32,1,40,1024]{3,2,1,0:T(8,128)(2,1)S(1)} all-to-all(bf16[32,1,40,1024]{3,2,1,0:T(8,128)(2,1)S(1)} %bitcast.153), channel_id=1, replica_groups=mesh['req'=32,'exp'=4] {'req'}, dimensions={0} | all-to-all | bytes 5242880 | tf_op jit(solution)/shard_map/all_to_all | solution.py:159
  563.1 2.3 fusion.26
  565.4 3.3 convert_bitcast_fusion
  568.7 5.4 all-to-all-start.1
  575.1 4.6 gather_fusion.2
  579.9 0.8 copy.70
  580.7 25.9 %all-to-all-done.1 = bf16[32,1,40,1024]{3,2,1,0:T(8,128)(2,1)} async-done(((bf16[32,1,40,1024]{3,2,1,0:T(8,128)(2,1)}), bf16[32,1,40,1024]{3,2,1,0:T(8,128)(2,1)}, u32[]{:S(2)}, u32[]{:S(2)}) %all-to-all-start.1) | async-done | bytes 2621472 | tf_op jit(solution)/shard_map/all_to_all | solution.py:161
  606.6 2.6 convert_reduce_fusion
  609.2 2.7 gather_fusion.1
  611.9 2.6 reshape.339
  614.6 4.4 multiply_reduce_fusion
  619.0 1.0 stack.24
  620.0 0.9 copy.71
  620.9 18.5 %reduce-scatter.5.cloned.1.call-done = bf16[256,256]{1,0:T(8,128)(2,1)} async-done(((bf16[256,1024]{1,0:T(8,128)(2,1)}), bf16[256,256]{1,0:T(8,128)(2,1)}) %reduce-scatter.5.cloned.1.call-update) | async-done | bytes 131088 | tf_op jit(solution)/shard_map/reduce_scatter | solution.py:172
  639.4 1.7 add_convert_fusion
  (141 shorter events, 12.2 us)
Async XLA Ops:
  7.2 555.9 %copy-start = (bf16[1,1024,2,352]{1,3,2,0:T(8,128)(2,1)S(1)}, bf16[1,1024,2,352]{1,3,2,0:T(8,128)(2,1)}, u32[]{:S(2)}) copy-start(bf16[1,1024,2,352]{1,3,2,0:T(8,128)(2,1)} %param.24) | copy-start | bytes 4325380
  7.2 383.3 %all-reduce.8.cloned.1.call-start = ((), (), s32[]{:S(2)}) async-start(), calls=%async_computation.6 | async-start | bytes 16777216 | tf_op jit(solution)/shard_map/psum | solution.py:24
  19.4 0.7 copy-start.36
  19.4 6.3 copy-start.37
  19.4 9.9 %copy-start.14 = (bf16[1024,3,256]{2,0,1:T(8,128)(2,1)S(1)}, bf16[1024,3,256]{2,0,1:T(8,128)(2,1)}, u32[]{:S(2)}) copy-start(bf16[1024,3,256]{2,0,1:T(8,128)(2,1)} %param.19) | copy-start | bytes 4718596
  19.5 11.6 %copy-start.9 = (bf16[256,256]{1,0:T(8,128)(2,1)S(1)}, bf16[256,256]{1,0:T(8,128)(2,1)}, u32[]{:S(2)}) copy-start(bf16[256,256]{1,0:T(8,128)(2,1)} %param.13) | copy-start | bytes 393220
  19.5 21.9 %copy-start.40 = (f32[1024]{0:T(1024)S(1)}, f32[1024]{0:T(1024)}, u32[]{:S(2)}) copy-start(f32[1024]{0:T(1024)} %param.18) | copy-start | bytes 12292
  19.5 481.2 %reduce-scatter.3.cloned.1.call-start = ((), (), s32[]{:S(2)}) async-start(), calls=%async_computation.4 | async-start | bytes 655360 | tf_op jit(solution)/shard_map/reduce_scatter | solution.py:136
  41.4 15.0 %copy-start.34 = (s32[256,2]{0,1:T(2,128)S(1)}, s32[256,2]{0,1:T(2,128)}, u32[]{:S(2)}) copy-start(s32[256,2]{0,1:T(2,128)} %param.23) | copy-start | bytes 6148
  43.7 350.2 %copy-start.8 = (bf16[256,768]{0,1:T(8,128)(2,1)}, bf16[256,768]{0,1:T(8,128)(2,1)S(1)}, u32[]{:S(2)}) copy-start(bf16[256,768]{0,1:T(8,128)(2,1)S(1)} %copy.58) | copy-start | bytes 1179652
  56.5 337.4 %copy-start.15 = (s32[256,2]{1,0:T(8,128)}, s32[256,2]{1,0:T(8,128)S(1)}, u32[]{:S(2)}) copy-start(s32[256,2]{1,0:T(8,128)S(1)} %copy.62) | copy-start | bytes 6148
  390.5 3.4 copy-start.13
  393.9 1.7 copy-start.12
  395.6 1.7 copy-start.11
  438.4 1.9 copy-start.18
  438.4 1.9 copy-start.23
  438.4 1.9 copy-start.29
  438.4 1.9 copy-start.33
  441.5 2.0 copy-start.2
  441.5 2.0 copy-start.24
  441.6 2.0 copy-start.32
  444.8 0.8 copy-start.28
  444.8 0.8 copy-start.38
  445.6 1.6 copy-start.7
  445.6 1.6 copy-start.27
  447.2 4.7 copy-start.22
  447.2 4.7 copy-start.31
  454.3 1.2 copy-start.6
  454.3 1.2 copy-start.26
  455.6 1.4 copy-start.17
  455.6 1.4 copy-start.21
  455.6 1.4 copy-start.30
  458.2 1.2 copy-start.5
  458.2 1.2 copy-start.25
  459.4 1.5 copy-start.19
  460.5 1.6 copy-start.20
  460.5 1.8 copy-start.16
  460.5 40.2 %copy-start.10 = (bf16[256,256]{1,0:T(8,128)(2,1)S(1)}, bf16[256,256]{1,0:T(8,128)(2,1)}, u32[]{:S(2)}) copy-start(bf16[256,256]{1,0:T(8,128)(2,1)} %param.13) | copy-start | bytes 393220
  516.1 0.8 copy-start.3
  563.1 2.3 copy-start.39
  568.7 6.1 copy-start.4
  568.7 6.1 copy-start.35
  568.7 37.9 %all-to-all-start.1 = ((bf16[32,1,40,1024]{3,2,1,0:T(8,128)(2,1)}), bf16[32,1,40,1024]{3,2,1,0:T(8,128)(2,1)}, u32[]{:S(2)}, u32[]{:S(2)}) async-start(bf16[32,1,40,1024]{3,2,1,0:T(8,128)(2,1)} %convert_bitcast_fusion), calls=%async_computation.2 | async-start | bytes 5242880 | tf_op jit(solution)/shard_map/all_to_all | solution.py:161
  574.2 65.3 %reduce-scatter.5.cloned.1.call-start = ((), (), s32[]{:S(2)}) async-start(), calls=%async_computation.5 | async-start | bytes 655360 | tf_op jit(solution)/shard_map/reduce_scatter | solution.py:172
  611.9 29.2 %copy-start.1 = (bf16[1,1024,2,352]{1,3,2,0:T(8,128)(2,1)S(1)}, bf16[1,1024,2,352]{1,3,2,0:T(8,128)(2,1)}, u32[]{:S(2)}) copy-start(bf16[1,1024,2,352]{1,3,2,0:T(8,128)(2,1)} %param.24) | copy-start | bytes 4325380
Sparse Core Ops, SparseCore 0:
  19.6 370.8 all-reduce.7
  462.2 38.4 reduce-scatter.2
  619.1 20.2 reduce-scatter.4
where the time goes:
time: 649 us; the launch traced here: 648 us
  waiting for transfers between devices  406 us (63%)
  local copies, waits for them, and re-layouts  87 us (13%)
  blocking collectives  66.4 us (10%)
  between operations  32.5 us (5%)
  other arithmetic  28.4 us (4%)
  matrix products  21.4 us (3%)
    psum x1, waiting for transfers between devices, spread(): return lax.psum(jnp.where(mine, shard, jnp.zeros_like(shard)), axis)  327 us
    all_to_all x1, blocking collectives, shards(): lax.all_to_all(outgoing_rows, 'req', split_axis=0, concat_axis=0, tiled=T...  43 us
    reduce_scatter x1, waiting for transfers between devices, shards(): lax.psum_scatter(partial_attn.astype(jnp.bfloat16), 'exp', scatter_dimens...  34.6 us
    dynamic_slice x5, local copies, waits for them, and re-layouts, shards(): cached[block_groups[request]].reshape(PREFIX, 2, local_heads, HEAD_DIM)  30 us
    all_to_all x1, waiting for transfers between devices, shards(): lax.all_to_all(partial_out.astype(jnp.bfloat16), 'req', split_axis=0, con...  25.9 us
    reduce_scatter x1, waiting for transfers between devices, shards(): lax.psum_scatter(mixture.astype(jnp.bfloat16), 'exp', scatter_dimension=1...  18.5 us
    unnamed x88, local copies, waits for them, and re-layouts  13.4 us
  transfers between devices with their start and end apart: 4, of which 4 were waited for; matrix products, arithmetic and copies ran while one was open for 5% of the time, Pallas kernels for 0%

commit v1 on v0

--- a/solution.py
+++ b/solution.py
@@ -116,10 +116,11 @@
     block_groups = groups[0]
     starts = jnp.cumsum(block_lengths) - block_lengths
     context = jnp.zeros((row_count, local_heads, HEAD_DIM), jnp.float32)
-    arrived = []
-    for prefix_group in range(GROUPS):
-        arrived.append(spread(own_slot, "req", owners[prefix_group]))
-    cached = jnp.stack(arrived, axis=0)
+    req_total = lax.axis_size("req")
+    pieces = own_slot.reshape(req_total, PREFIX // req_total, 2, quarter)
+    pieces = lax.all_to_all(pieces, "req", split_axis=0, concat_axis=0, tiled=True)
+    owned = jnp.take(pieces, owners, axis=0)
+    cached = lax.all_gather(owned, "req", axis=1, tiled=True)
     for request in range(REQ_DEV):
         prefix_kv = cached[block_groups[request]].reshape(PREFIX, 2, local_heads, HEAD_DIM)
         context = context + request_context(
@@ -150,7 +151,6 @@
     columns = x_source.shape[1]
     padded = jnp.concatenate([x_source, jnp.zeros((1, columns), x_source.dtype)], axis=0)
     picked = padded[table].reshape(EXPERTS, 1, CAP, columns)
-    req_total = lax.axis_size("req")
     local_rows = EXPERTS * SPLIT // req_total
     outgoing_rows = jnp.broadcast_to(picked, (EXPERTS, SPLIT, CAP, columns)).reshape(
         req_total, local_rows, CAP, columns

time: 649 us -> 376 us (0.58)
  waiting for transfers between devices: 406 us -> 145 us
  local copies, waits for them, and re-layouts: 87 us -> 74.8 us
  starting transfers between devices: 5.56 us -> 17 us
    psum x1 -> x0, waiting for transfers between devices: 327 us -> none  [spread(): return lax.psum(jnp.where(mine, shard, jnp.zeros_like(shard)), axis)]
    all_gather x0 -> x1, waiting for transfers between devices: none -> 61.2 us  [shards(): cached = lax.all_gather(owned, 'req', axis=1, tiled=True)]
    all_to_all x0 -> x1, waiting for transfers between devices: none -> 26.7 us  [shards(): lax.all_to_all(pieces, 'req', split_axis=0, concat_axis=0, tiled=True)]
    reduce_scatter x1, waiting for transfers between devices: 34.6 us -> 12.7 us  [shards(): lax.psum_scatter(partial_attn.astype(jnp.bfloat16), 'exp', scatter_dimens...]
    all_to_all x0 -> x1, starting transfers between devices: none -> 11.5 us  [shards(): lax.all_to_all(pieces, 'req', split_axis=0, concat_axis=0, tiled=True)]
    dynamic_slice x5, local copies, waits for them, and re-layouts: 30 us -> 20.7 us  [shards(): cached[block_groups[request]].reshape(PREFIX, 2, local_heads, HEAD_DIM)]
    unnamed x88 -> x77, local copies, waits for them, and re-layouts: 13.4 us -> 5.01 us
  transfers between devices with their start and end apart: 4 -> 5, of which waited for: 4 -> 5; matrix products, arithmetic and copies ran while one was open for 5% -> 8% of each run, Pallas kernels for 0% -> 0%
where the time goes in v1:
time: 376 us; the launch traced here: 375 us
  waiting for transfers between devices  145 us (39%)
  local copies, waits for them, and re-layouts  74.8 us (20%)
  blocking collectives  64.8 us (17%)
  between operations  29.5 us (8%)
  other arithmetic  23.5 us (6%)
  matrix products  20.6 us (5%)
  starting transfers between devices  17 us (5%)
    all_gather x1, waiting for transfers between devices, shards(): cached = lax.all_gather(owned, 'req', axis=1, tiled=True)  61.2 us
    all_to_all x1, blocking collectives, shards(): lax.all_to_all(outgoing_rows, 'req', split_axis=0, concat_axis=0, tiled=T...  43 us
    all_to_all x1, waiting for transfers between devices, shards(): lax.all_to_all(partial_out.astype(jnp.bfloat16), 'req', split_axis=0, con...  27.1 us
    all_to_all x1, waiting for transfers between devices, shards(): lax.all_to_all(pieces, 'req', split_axis=0, concat_axis=0, tiled=True)  26.7 us
    dynamic_slice x5, local copies, waits for them, and re-layouts, shards(): cached[block_groups[request]].reshape(PREFIX, 2, local_heads, HEAD_DIM)  20.7 us
    reduce_scatter x1, waiting for transfers between devices, shards(): lax.psum_scatter(mixture.astype(jnp.bfloat16), 'exp', scatter_dimension=1...  17.3 us
    reduce_scatter x1, waiting for transfers between devices, shards(): lax.psum_scatter(partial_attn.astype(jnp.bfloat16), 'exp', scatter_dimens...  12.7 us
    all_to_all x1, starting transfers between devices, shards(): lax.all_to_all(pieces, 'req', split_axis=0, concat_axis=0, tiled=True)  11.5 us
  transfers between devices with their start and end apart: 5, of which 5 were waited for; matrix products, arithmetic and copies ran while one was open for 8% of the time, Pallas kernels for 0%

profile of v1, /device:TPU:1, one launch (start us, length us, event | category | flops | bytes accessed | tf_op | source)
XLA Modules:
  0.0 375.4 jit_solution(5004011562443710607)
XLA Ops:
  7.2 3.5 copy.73
  10.7 11.5 %all-to-all-start = ((bf16[32,64,2,256]{3,1,2,0:T(8,128)(2,1)}), bf16[32,64,2,256]{3,1,2,0:T(8,128)(2,1)S(1)}, u32[]{:S(2)}, u32[]{:S(2)}) async-start(bf16[32,64,2,256]{3,1,2,0:T(8,128)(2,1)} %copy.73), calls=%async_computation | async-start | bytes 4194304 | tf_op jit(solution)/shard_map/all_to_all | solution.py:121
  22.2 1.2 compare_and_fusion.4
  23.4 26.7 %all-to-all-done = bf16[32,64,2,256]{3,1,2,0:T(8,128)(2,1)S(1)} async-done(((bf16[32,64,2,256]{3,1,2,0:T(8,128)(2,1)}), bf16[32,64,2,256]{3,1,2,0:T(8,128)(2,1)S(1)}, u32[]{:S(2)}, u32[]{:S(2)}) %all-to-all-start) | async-done | bytes 2097184 | tf_op jit(solution)/shard_map/all_to_all | solution.py:121
  50.1 1.3 gather_fusion
  51.4 1.8 broadcast_select_fusion
  62.7 1.7 copy.75
  64.5 8.5 %all_gather.10 = bf16[256,1024]{1,0:T(8,128)(2,1)S(1)} all-gather(bf16[256,256]{1,0:T(8,128)(2,1)S(1)} %copy-done.10), channel_id=1, replica_groups=mesh['req'=32,'exp'=4] {'exp'}, dimensions={1}, use_global_device_ids=true | all-gather | bytes 655360 | tf_op jit(solution)/shard_map/all_gather | solution.py:100
  73.1 1.3 convolution_convert_fusion.1
  77.9 1.1 and_convert_fusion.3
  79.1 0.8 concatenate.40
  79.9 1.2 and_convert_fusion.2
  81.2 0.8 concatenate.43
  83.3 1.2 and_convert_fusion.1
  84.6 0.8 concatenate.46
  86.7 1.2 and_convert_fusion
  88.0 0.8 concatenate.49
  92.3 1.1 constant_dynamic-slice_fusion
  93.3 61.2 %all-gather.2.cloned.1.call-done = bf16[4,2048,2,256]{3,1,2,0:T(8,128)(2,1)} async-done(((bf16[4,64,2,256]{3,1,2,0:T(8,128)(2,1)}), bf16[4,2048,2,256]{3,1,2,0:T(8,128)(2,1)}) %all-gather.2.cloned.1.call-update) | async-done | bytes 8388624 | tf_op jit(solution)/shard_map/all_gather | solution.py:123
  154.6 6.2 %constant_dynamic-slice_fusion.2 = (bf16[1,2048,2,256]{3,1,2,0:T(8,128)(2,1)S(1)}, bf16[1,2048,2,256]{3,1,2,0:T(8,128)(2,1)}, bf16[1,2048,2,256]{3,1,2,0:T(8,128)(2,1)}, bf16[1,2048,2,256]{3,1,2,0:T(8,128)(2,1)}) fusion(bf16[4,2048,2,256]{3,1,2,0:T(8,128)(2,1)} %all-gather.2.cloned.1.call-done, s32[]{:T(128)S(6)} %select_n.129, s32[]{:T(128)S(6)} %select_n.126, ...), kind=kLoop, calls=%fused_computation.141 | loop fusion | bytes 16777232 | tf_op jit(solution)/shard_map/dynamic_slice | solution.py:125
  160.7 4.0 %copy.74 = bf16[1,2048,2,256]{1,3,2,0:T(8,128)(2,1)} copy(bf16[1,2048,2,256]{3,1,2,0:T(8,128)(2,1)} %get-tuple-element.13) | data formatting | bytes 4194304 | tf_op jit(solution)/shard_map/dynamic_slice | solution.py:125
  164.8 3.1 slice_bitcast_fusion.7
  167.9 4.0 %copy.77 = bf16[1,2048,2,256]{1,3,2,0:T(8,128)(2,1)} copy(bf16[1,2048,2,256]{3,1,2,0:T(8,128)(2,1)} %get-tuple-element.12) | data formatting | bytes 4194304 | tf_op jit(solution)/shard_map/dynamic_slice | solution.py:125
  171.9 3.2 slice_bitcast_fusion.5
  175.1 1.2 fusion.154
  177.6 1.7 fusion.45
  180.0 1.8 dynamic_update_slice.14
  181.8 2.5 fusion.155
  185.6 1.7 fusion.57
  187.3 2.3 add.269
  189.6 4.0 %copy.78 = bf16[1,2048,2,256]{1,3,2,0:T(8,128)(2,1)} copy(bf16[1,2048,2,256]{3,1,2,0:T(8,128)(2,1)} %get-tuple-element.11) | data formatting | bytes 4194304 | tf_op jit(solution)/shard_map/dynamic_slice | solution.py:125
  193.7 1.7 slice_bitcast_fusion.3
  195.4 1.2 fusion.156
  197.6 1.7 fusion.69
  199.3 2.3 add.276
  201.7 2.5 copy.79
  204.2 1.7 slice_bitcast_fusion.1
  205.9 1.2 fusion.157
  208.1 1.0 fusion.81
  209.6 1.1 convolution_convert_fusion
  210.7 1.2 reduce-window.20
  213.0 2.4 scatter_custom_fusion
  215.5 12.7 %reduce-scatter.3.cloned.1.call-done = bf16[256,256]{1,0:T(8,128)(2,1)} async-done(((bf16[256,1024]{1,0:T(8,128)(2,1)}), bf16[256,256]{1,0:T(8,128)(2,1)}) %reduce-scatter.3.cloned.1.call-update) | async-done | bytes 131088 | tf_op jit(solution)/shard_map/reduce_scatter | solution.py:137
  228.2 1.0 multiply_reduce_fusion.1
  229.3 5.1 %psum.7 = f32[256]{0:T(256)S(1)} all-reduce(f32[256]{0:T(256)S(1)} %multiply_reduce_fusion.1), channel_id=1, replica_groups=mesh['req'=32,'exp'=4] {'exp'}, use_global_device_ids=true, to_apply=%region_12.13 | all-reduce | flops 256 | bytes 2048 | tf_op jit(solution)/shard_map/psum | solution.py:140
  234.4 1.0 multiply_convert_fusion
  235.4 8.2 %all_gather.11 = bf16[256,1024]{1,0:T(8,128)(2,1)S(1)} all-gather(bf16[256,256]{1,0:T(8,128)(2,1)S(1)} %multiply_convert_fusion), channel_id=1, replica_groups=mesh['req'=32,'exp'=4] {'exp'}, dimensions={1}, use_global_device_ids=true | all-gather | bytes 655360 | tf_op jit(solution)/shard_map/all_gather | solution.py:146
  243.6 0.8 copy-done.2
  244.5 2.8 gather_fusion.1
  247.7 43.0 %all_to_all.15 = bf16[32,1,40,1024]{3,2,1,0:T(8,128)(2,1)S(1)} all-to-all(bf16[32,1,40,1024]{3,2,1,0:T(8,128)(2,1)S(1)} %bitcast.150), channel_id=1, replica_groups=mesh['req'=32,'exp'=4] {'req'}, dimensions={0} | all-to-all | bytes 5242880 | tf_op jit(solution)/shard_map/all_to_all | solution.py:159
  290.7 2.3 fusion.26
  293.0 3.3 convert_bitcast_fusion
  296.3 5.4 %all-to-all-start.2 = ((bf16[32,1,40,1024]{3,2,1,0:T(8,128)(2,1)}), bf16[32,1,40,1024]{3,2,1,0:T(8,128)(2,1)}, u32[]{:S(2)}, u32[]{:S(2)}) async-start(bf16[32,1,40,1024]{3,2,1,0:T(8,128)(2,1)} %convert_bitcast_fusion), calls=%async_computation.3 | async-start | bytes 5242880 | tf_op jit(solution)/shard_map/all_to_all | solution.py:161
  302.7 4.7 %gather_fusion.3 = f32[512]{0:T(512)S(1)} fusion(f32[256,16]{0,1:T(8,128)S(1)} %fusion.158, s32[512]{0:T(512)S(1)} %reshape.360), kind=kCustom, calls=%fused_computation.3 | custom fusion | bytes 8192 | tf_op jit(solution)/shard_map/jit(take_along_axis)/gather | solution.py:148
  307.6 0.8 copy.88
  308.4 27.1 %all-to-all-done.2 = bf16[32,1,40,1024]{3,2,1,0:T(8,128)(2,1)} async-done(((bf16[32,1,40,1024]{3,2,1,0:T(8,128)(2,1)}), bf16[32,1,40,1024]{3,2,1,0:T(8,128)(2,1)}, u32[]{:S(2)}, u32[]{:S(2)}) %all-to-all-start.2) | async-done | bytes 2621472 | tf_op jit(solution)/shard_map/all_to_all | solution.py:161
  335.5 2.6 convert_reduce_fusion
  338.1 2.7 gather_fusion.2
  340.8 2.6 reshape.332
  343.4 4.4 %multiply_reduce_fusion = bf16[256,1024]{1,0:T(8,128)(2,1)} fusion(f32[256,2,1024]{2,1,0:T(2,128)S(1)} %reshape.332, f32[256,2]{1,0:T(8,128)} %copy.88), kind=kLoop, calls=%fused_computation.38 | loop fusion | flops 786432 | bytes 2623488 | tf_op jit(solution)/shard_map/reduce_sum | solution.py:171
  347.9 1.0 stack.4
  348.9 0.9 copy.89
  349.7 17.3 %reduce-scatter.5.cloned.1.call-done = bf16[256,256]{1,0:T(8,128)(2,1)} async-done(((bf16[256,1024]{1,0:T(8,128)(2,1)}), bf16[256,256]{1,0:T(8,128)(2,1)}) %reduce-scatter.5.cloned.1.call-update) | async-done | bytes 131088 | tf_op jit(solution)/shard_map/reduce_scatter | solution.py:172
  367.1 1.7 add_convert_fusion
  (135 shorter events, 12.7 us)
Async XLA Ops:
  7.2 283.5 %copy-start = (bf16[1,1024,2,352]{1,3,2,0:T(8,128)(2,1)S(1)}, bf16[1,1024,2,352]{1,3,2,0:T(8,128)(2,1)}, u32[]{:S(2)}) copy-start(bf16[1,1024,2,352]{1,3,2,0:T(8,128)(2,1)} %param.24) | copy-start | bytes 4325380
  10.7 11.5 %copy-start.36 = (s32[4]{0:T(128)S(1)}, s32[4]{0:T(128)}, u32[]{:S(2)}) copy-start(s32[4]{0:T(128)} %param.16) | copy-start | bytes 52
  10.7 42.5 %copy-start.30 = (s32[1,4]{1,0:T(1,128)S(1)}, s32[1,4]{1,0:T(1,128)}, u32[]{:S(2)}) copy-start(s32[1,4]{1,0:T(1,128)} %param.14) | copy-start | bytes 52
  10.7 45.9 %copy-start.29 = (s32[1,4]{1,0:T(1,128)S(1)}, s32[1,4]{1,0:T(1,128)}, u32[]{:S(2)}) copy-start(s32[1,4]{1,0:T(1,128)} %param.15) | copy-start | bytes 52
  10.7 51.6 %copy-start.27 = (s32[256,2]{0,1:T(2,128)S(1)}, s32[256,2]{0,1:T(2,128)}, u32[]{:S(2)}) copy-start(s32[256,2]{0,1:T(2,128)} %param.23) | copy-start | bytes 6148
  10.7 39.4 %all-to-all-start = ((bf16[32,64,2,256]{3,1,2,0:T(8,128)(2,1)}), bf16[32,64,2,256]{3,1,2,0:T(8,128)(2,1)S(1)}, u32[]{:S(2)}, u32[]{:S(2)}) async-start(bf16[32,64,2,256]{3,1,2,0:T(8,128)(2,1)} %copy.73), calls=%async_computation | async-start | bytes 4194304 | tf_op jit(solution)/shard_map/all_to_all | solution.py:121
  22.2 132.4 %all-gather.2.cloned.1.call-start = ((), (), s32[]{:S(2)}) async-start(), calls=%async_computation.5 | async-start | bytes 8650752 | tf_op jit(solution)/shard_map/all_gather | solution.py:123
  51.4 13.1 %copy-start.10 = (bf16[256,256]{1,0:T(8,128)(2,1)S(1)}, bf16[256,256]{1,0:T(8,128)(2,1)}, u32[]{:S(2)}) copy-start(bf16[256,256]{1,0:T(8,128)(2,1)} %param.13) | copy-start | bytes 393220
  53.2 175.1 %reduce-scatter.3.cloned.1.call-start = ((), (), s32[]{:S(2)}) async-start(), calls=%async_computation.6 | async-start | bytes 655360 | tf_op jit(solution)/shard_map/reduce_scatter | solution.py:137
  74.7 18.7 %copy-start.9 = (bf16[256,768]{0,1:T(8,128)(2,1)}, bf16[256,768]{0,1:T(8,128)(2,1)S(1)}, u32[]{:S(2)}) copy-start(bf16[256,768]{0,1:T(8,128)(2,1)S(1)} %copy.76) | copy-start | bytes 1179652
  171.9 3.2 copy-start.12
  171.9 3.2 copy-start.16
  171.9 3.2 copy-start.21
  171.9 3.2 copy-start.26
  176.4 1.2 copy-start.4
  176.4 1.2 copy-start.20
  176.4 1.2 copy-start.34
  184.3 1.2 copy-start.5
  184.3 1.3 copy-start.6
  184.4 1.3 copy-start.19
  184.4 1.2 copy-start.33
  193.7 1.7 copy-start.15
  193.7 1.8 copy-start.22
  193.7 1.8 copy-start.25
  196.7 1.0 copy-start.7
  196.7 1.0 copy-start.18
  196.7 0.9 copy-start.32
  204.2 1.7 copy-start.14
  204.2 1.8 copy-start.23
  204.2 1.8 copy-start.24
  207.2 1.0 copy-start.8
  207.2 1.0 copy-start.17
  207.2 0.9 copy-start.31
  208.1 1.4 copy-start.13
  209.2 19.1 %copy-start.11 = (bf16[256,256]{1,0:T(8,128)(2,1)S(1)}, bf16[256,256]{1,0:T(8,128)(2,1)}, u32[]{:S(2)}) copy-start(bf16[256,256]{1,0:T(8,128)(2,1)} %param.13) | copy-start | bytes 393220
  243.6 0.8 copy-start.2
  290.7 2.3 copy-start.35
  296.3 6.1 %copy-start.3 = (bf16[256,1024]{1,0:T(8,128)(2,1)S(1)}, bf16[256,1024]{1,0:T(8,128)(2,1)}, u32[]{:S(2)}) copy-start(bf16[256,1024]{1,0:T(8,128)(2,1)} %copy-done.2) | copy-start | bytes 1572868
  296.3 6.1 %copy-start.28 = (bf16[1024,16]{0,1:T(8,128)(2,1)S(1)}, bf16[1024,16]{0,1:T(8,128)(2,1)}, u32[]{:S(2)}) copy-start(bf16[1024,16]{0,1:T(8,128)(2,1)} %param.22) | copy-start | bytes 98308
  296.3 39.2 %all-to-all-start.2 = ((bf16[32,1,40,1024]{3,2,1,0:T(8,128)(2,1)}), bf16[32,1,40,1024]{3,2,1,0:T(8,128)(2,1)}, u32[]{:S(2)}, u32[]{:S(2)}) async-start(bf16[32,1,40,1024]{3,2,1,0:T(8,128)(2,1)} %convert_bitcast_fusion), calls=%async_computation.3 | async-start | bytes 5242880 | tf_op jit(solution)/shard_map/all_to_all | solution.py:161
  301.7 65.3 %reduce-scatter.5.cloned.1.call-start = ((), (), s32[]{:S(2)}) async-start(), calls=%async_computation.7 | async-start | bytes 655360 | tf_op jit(solution)/shard_map/reduce_scatter | solution.py:172
  340.8 28.0 %copy-start.1 = (bf16[1,1024,2,352]{1,3,2,0:T(8,128)(2,1)S(1)}, bf16[1,1024,2,352]{1,3,2,0:T(8,128)(2,1)}, u32[]{:S(2)}) copy-start(bf16[1,1024,2,352]{1,3,2,0:T(8,128)(2,1)} %param.24) | copy-start | bytes 4325380
Sparse Core Ops, SparseCore 0:
  53.3 101.2 all-gather.1
  210.8 17.3 reduce-scatter.2
  348.0 19.0 reduce-scatter.4

commit v2 on v1

--- a/solution.py
+++ b/solution.py
@@ -134,45 +134,39 @@
         )
     context = context.reshape(row_count, quarter).astype(jnp.bfloat16)
     partial_attn = jnp.dot(context, w_out, preferred_element_type=jnp.float32)
-    resid = tokens.astype(jnp.float32) + lax.psum_scatter(
-        partial_attn.astype(jnp.bfloat16), "exp", scatter_dimension=1, tiled=True
-    ).astype(jnp.float32)
-    squares = lax.psum(jnp.sum(resid * resid, axis=1), "exp")
+    attn_full = lax.psum(partial_attn.astype(jnp.bfloat16), "exp").astype(jnp.float32)
+    resid_full = rows_whole.astype(jnp.float32) + attn_full
+    x_full = norm_rows(resid_full, moe_gain).astype(jnp.bfloat16)
     column_start = lax.axis_index("exp") * quarter
-    gain_part = lax.dynamic_slice_in_dim(moe_gain, column_start, quarter, 0)
-    x_part = (resid * lax.rsqrt(squares / full_width + epsilon)[:, None] * gain_part).astype(
-        jnp.bfloat16
-    )
-    x_source = lax.all_gather(x_part, "exp", axis=1, tiled=True)
-    logits = jnp.dot(x_source, w_router, preferred_element_type=jnp.float32)
+    resid = lax.dynamic_slice_in_dim(resid_full, column_start, quarter, 1)
+    x_part = lax.dynamic_slice_in_dim(x_full, column_start, quarter, 1)
+    logits = jnp.dot(x_full, w_router, preferred_element_type=jnp.float32)
     gates = jax.nn.sigmoid(jnp.take_along_axis(logits, expert_ids, axis=1)).reshape(-1)
     flat_ids, ranks = slot_ranks(expert_ids, EXPERTS)
     kept, table = slot_table(flat_ids, ranks, CAP, EXPERTS, row_count, TOP)
-    columns = x_source.shape[1]
-    padded = jnp.concatenate([x_source, jnp.zeros((1, columns), x_source.dtype)], axis=0)
-    picked = padded[table].reshape(EXPERTS, 1, CAP, columns)
+    padded = jnp.concatenate([x_part, jnp.zeros((1, quarter), x_part.dtype)], axis=0)
+    picked = padded[table].reshape(EXPERTS, 1, CAP, quarter)
     local_rows = EXPERTS * SPLIT // req_total
-    outgoing_rows = jnp.broadcast_to(picked, (EXPERTS, SPLIT, CAP, columns)).reshape(
-        req_total, local_rows, CAP, columns
+    outgoing_rows = jnp.broadcast_to(picked, (EXPERTS, SPLIT, CAP, quarter)).reshape(
+        req_total, local_rows, CAP, quarter
     )
-    partial_out = expert_apply(
-        lax.all_to_all(outgoing_rows, "req", split_axis=0, concat_axis=0, tiled=True), w_in, w_down
+    arrived = lax.all_to_all(outgoing_rows, "req", split_axis=0, concat_axis=0, tiled=True)
+    arrived = lax.all_gather(arrived, "exp", axis=3, tiled=True)
+    partial_out = expert_apply(arrived, w_in, w_down)
+    reduced = lax.psum_scatter(
+        partial_out.astype(jnp.bfloat16), "exp", scatter_dimension=3, tiled=True
     )
-    returned = lax.all_to_all(
-        partial_out.astype(jnp.bfloat16), "req", split_axis=0, concat_axis=0, tiled=True
-    ).astype(partial_out.dtype)
-    out_columns = returned.shape[3]
-    summed = jnp.sum(returned.reshape(EXPERTS, SPLIT, CAP, out_columns), axis=1).reshape(
-        EXPERTS * CAP, out_columns
+    returned = lax.all_to_all(reduced, "req", split_axis=0, concat_axis=0, tiled=True).astype(
+        jnp.float32
+    )
+    summed = jnp.sum(returned.reshape(EXPERTS, SPLIT, CAP, quarter), axis=1).reshape(
+        EXPERTS * CAP, quarter
     )
     source = flat_ids * CAP + jnp.minimum(ranks, CAP - 1)
-    chosen = summed[source].reshape(row_count, TOP, out_columns)
+    chosen = summed[source].reshape(row_count, TOP, quarter)
     scale = jnp.where(kept, gates, 0.0).reshape(row_count, TOP)
     mixture = jnp.sum(chosen * scale[:, :, None], axis=1)
-    moe_part = lax.psum_scatter(
-        mixture.astype(jnp.bfloat16), "exp", scatter_dimension=1, tiled=True
-    ).astype(jnp.float32)
-    hidden_out = (resid + moe_part).astype(jnp.bfloat16)
+    hidden_out = (resid + mixture).astype(jnp.bfloat16)
     return (hidden_out, suffix_kv)
 
 

time: 376 us -> 382 us (1.016)
  waiting for transfers between devices: 145 us -> 191 us
  blocking collectives: 64.8 us -> 30.4 us
  local copies, waits for them, and re-layouts: 74.8 us -> 68.2 us
  other arithmetic: 23.5 us -> 17.7 us
  starting transfers between devices: 17 us -> 21 us
    psum x0 -> x1, waiting for transfers between devices: none -> 34 us  [shards(): lax.psum(partial_attn.astype(jnp.bfloat16), 'exp').astype(jnp.float32)]
    all_gather x0 -> x1, waiting for transfers between devices: none -> 31.3 us  [shards(): arrived = lax.all_gather(arrived, 'exp', axis=3, tiled=True)]
    all_to_all x1, waiting for transfers between devices: 27.1 us -> 5.53 us  [shards(): lax.all_to_all(reduced, 'req', split_axis=0, concat_axis=0, tiled=True)]
    all_to_all x1, blocking collectives: 43 us -> 21.9 us  [shards(): lax.all_to_all(outgoing_rows, 'req', split_axis=0, concat_axis=0, tiled=T...]
    all_gather x1 -> x0, blocking collectives: 8.19 us -> none  [shards(): x_source = lax.all_gather(x_part, 'exp', axis=1, tiled=True)]
    psum x1 -> x0, blocking collectives: 5.12 us -> none  [shards(): squares = lax.psum(jnp.sum(resid * resid, axis=1), 'exp')]
    all_to_all x1, starting transfers between devices: 5.44 us -> 9.37 us  [shards(): lax.all_to_all(reduced, 'req', split_axis=0, concat_axis=0, tiled=True)]
    reduce_scatter x2 -> x1, waiting for transfers between devices: 30.1 us -> 33.3 us  [shards(): lax.psum_scatter(partial_out.astype(jnp.bfloat16), 'exp', scatter_dimensi...]
  transfers between devices with their start and end apart: 5 -> 6, of which waited for: 5 -> 6; matrix products, arithmetic and copies ran while one was open for 8% -> 7% of each run, Pallas kernels for 0% -> 0%
where the time goes in v2:
time: 382 us; the launch traced here: 379 us
  waiting for transfers between devices  191 us (50%)
  local copies, waits for them, and re-layouts  68.2 us (18%)
  blocking collectives  30.4 us (8%)
  between operations  29.2 us (8%)
  matrix products  21.6 us (6%)
  starting transfers between devices  21 us (5%)
  other arithmetic  17.7 us (5%)
    all_gather x1, waiting for transfers between devices, shards(): cached = lax.all_gather(owned, 'req', axis=1, tiled=True)  60.2 us
    psum x1, waiting for transfers between devices, shards(): lax.psum(partial_attn.astype(jnp.bfloat16), 'exp').astype(jnp.float32)  34 us
    reduce_scatter x1, waiting for transfers between devices, shards(): lax.psum_scatter(partial_out.astype(jnp.bfloat16), 'exp', scatter_dimensi...  33.3 us
    all_gather x1, waiting for transfers between devices, shards(): arrived = lax.all_gather(arrived, 'exp', axis=3, tiled=True)  31.3 us
    all_to_all x1, waiting for transfers between devices, shards(): lax.all_to_all(pieces, 'req', split_axis=0, concat_axis=0, tiled=True)  26.7 us
    all_to_all x1, blocking collectives, shards(): lax.all_to_all(outgoing_rows, 'req', split_axis=0, concat_axis=0, tiled=T...  21.9 us
    dynamic_slice x5, local copies, waits for them, and re-layouts, shards(): cached[block_groups[request]].reshape(PREFIX, 2, local_heads, HEAD_DIM)  20.6 us
    all_to_all x1, starting transfers between devices, shards(): lax.all_to_all(pieces, 'req', split_axis=0, concat_axis=0, tiled=True)  11.5 us
  transfers between devices with their start and end apart: 6, of which 6 were waited for; matrix products, arithmetic and copies ran while one was open for 7% of the time, Pallas kernels for 0%

profile of v2, /device:TPU:1, one launch (start us, length us, event | category | flops | bytes accessed | tf_op | source)
XLA Modules:
  0.0 379.2 jit_solution(11752117033574564083)
XLA Ops:
  7.2 3.5 copy.74
  10.7 11.5 %all-to-all-start = ((bf16[32,64,2,256]{3,1,2,0:T(8,128)(2,1)}), bf16[32,64,2,256]{3,1,2,0:T(8,128)(2,1)S(1)}, u32[]{:S(2)}, u32[]{:S(2)}) async-start(bf16[32,64,2,256]{3,1,2,0:T(8,128)(2,1)} %copy.74), calls=%async_computation | async-start | bytes 4194304 | tf_op jit(solution)/shard_map/all_to_all | solution.py:121
  22.2 1.2 compare_and_fusion.4
  23.4 26.7 %all-to-all-done = bf16[32,64,2,256]{3,1,2,0:T(8,128)(2,1)S(1)} async-done(((bf16[32,64,2,256]{3,1,2,0:T(8,128)(2,1)}), bf16[32,64,2,256]{3,1,2,0:T(8,128)(2,1)S(1)}, u32[]{:S(2)}, u32[]{:S(2)}) %all-to-all-start) | async-done | bytes 2097184 | tf_op jit(solution)/shard_map/all_to_all | solution.py:121
  50.1 1.3 gather_fusion
  51.3 1.8 broadcast_select_fusion
  53.4 0.7 fusion.153
  56.6 0.7 fusion.152
  62.6 1.7 copy.76
  64.3 8.5 %all_gather.9 = bf16[256,1024]{1,0:T(8,128)(2,1)S(1)} all-gather(bf16[256,256]{1,0:T(8,128)(2,1)S(1)} %copy-done.21), channel_id=1, replica_groups=mesh['req'=32,'exp'=4] {'exp'}, dimensions={1}, use_global_device_ids=true | all-gather | bytes 655360 | tf_op jit(solution)/shard_map/all_gather | solution.py:100
  74.4 0.7 fusion.151
  77.5 1.0 and_convert_fusion.3
  78.7 0.8 concatenate.40
  79.5 1.3 and_convert_fusion.2
  80.8 0.8 concatenate.43
  82.8 1.1 and_convert_fusion.1
  84.0 0.8 concatenate.46
  86.8 0.8 concatenate.49
  87.9 1.3 reduce-window.20
  92.6 0.7 fusion.150
  93.3 1.1 constant_dynamic-slice_fusion.1
  94.4 60.2 %all-gather.3.cloned.1.call-done = bf16[4,2048,2,256]{3,1,2,0:T(8,128)(2,1)} async-done(((bf16[4,64,2,256]{3,1,2,0:T(8,128)(2,1)}), bf16[4,2048,2,256]{3,1,2,0:T(8,128)(2,1)}) %all-gather.3.cloned.1.call-update) | async-done | bytes 8388624 | tf_op jit(solution)/shard_map/all_gather | solution.py:123
  154.6 6.2 %constant_dynamic-slice_fusion.3 = (bf16[1,2048,2,256]{3,1,2,0:T(8,128)(2,1)S(1)}, bf16[1,2048,2,256]{3,1,2,0:T(8,128)(2,1)}, bf16[1,2048,2,256]{3,1,2,0:T(8,128)(2,1)}, bf16[1,2048,2,256]{3,1,2,0:T(8,128)(2,1)}) fusion(bf16[4,2048,2,256]{3,1,2,0:T(8,128)(2,1)} %all-gather.3.cloned.1.call-done, s32[]{:T(128)S(6)} %select_n.130, s32[]{:T(128)S(6)} %select_n.127, ...), kind=kLoop, calls=%fused_computation.142 | loop fusion | bytes 16777232 | tf_op jit(solution)/shard_map/dynamic_slice | solution.py:125
  160.8 4.0 %copy.75 = bf16[1,2048,2,256]{1,3,2,0:T(8,128)(2,1)} copy(bf16[1,2048,2,256]{3,1,2,0:T(8,128)(2,1)} %get-tuple-element.13) | data formatting | bytes 4194304 | tf_op jit(solution)/shard_map/dynamic_slice | solution.py:125
  164.8 3.1 slice_bitcast_fusion.7
  168.0 4.0 %copy.78 = bf16[1,2048,2,256]{1,3,2,0:T(8,128)(2,1)} copy(bf16[1,2048,2,256]{3,1,2,0:T(8,128)(2,1)} %get-tuple-element.12) | data formatting | bytes 4194304 | tf_op jit(solution)/shard_map/dynamic_slice | solution.py:125
  171.9 3.2 slice_bitcast_fusion.5
  175.2 1.2 fusion.154
  176.5 0.7 fusion.4
  177.7 1.7 fusion.45
  179.4 0.7 broadcast.315
  180.1 1.8 dynamic_update_slice.14
  181.9 2.5 fusion.155
  184.4 0.7 fusion.6
  185.7 1.7 fusion.57
  187.4 2.3 add.272
  189.7 4.0 %copy.79 = bf16[1,2048,2,256]{1,3,2,0:T(8,128)(2,1)} copy(bf16[1,2048,2,256]{3,1,2,0:T(8,128)(2,1)} %get-tuple-element.11) | data formatting | bytes 4194304 | tf_op jit(solution)/shard_map/dynamic_slice | solution.py:125
  193.7 1.7 slice_bitcast_fusion.3
  195.5 1.2 fusion.156
  196.7 0.7 fusion.8
  197.7 1.7 fusion.69
  199.4 2.3 add.279
  201.7 2.4 copy.80
  204.2 1.7 slice_bitcast_fusion.1
  205.9 1.2 fusion.157
  207.2 0.7 fusion.10
  208.1 1.0 fusion.81
  209.6 1.1 convolution_convert_fusion
  210.8 2.6 scatter_custom_fusion
  213.4 34.0 %all-reduce.7.cloned.1.call-done = bf16[256,1024]{1,0:T(8,128)(2,1)} async-done(((bf16[256,1024]{1,0:T(8,128)(2,1)}), bf16[256,1024]{1,0:T(8,128)(2,1)}) %all-reduce.7.cloned.1.call-update) | async-done | bytes 524304 | tf_op jit(solution)/shard_map/psum | solution.py:137
  247.5 2.3 convert_add_fusion
  250.0 2.8 gather_fusion.1
  252.8 21.9 %all_to_all.15 = bf16[32,1,40,256]{3,2,1,0:T(8,128)(2,1)} all-to-all(bf16[32,1,40,256]{3,2,1,0:T(8,128)(2,1)S(1)} %bitcast.158), channel_id=1, replica_groups=mesh['req'=32,'exp'=4] {'req'}, dimensions={0} | all-to-all | bytes 1310720 | tf_op jit(solution)/shard_map/all_to_all | solution.py:153
  274.8 31.3 %all-gather.5.cloned.1.call-done = bf16[32,1,40,1024]{3,2,0,1:T(8,128)(2,1)} async-done(((bf16[32,1,40,256]{3,2,0,1:T(8,128)(2,1)}), bf16[32,1,40,1024]{3,2,0,1:T(8,128)(2,1)}) %all-gather.5.cloned.1.call-update) | async-done | bytes 2621456 | tf_op jit(solution)/shard_map/all_gather | solution.py:154
  306.1 4.0 %fusion.26 = f32[32,1,40,2,352]{4,2,3,0,1:T(8,128)S(1)} fusion(bf16[32,1,40,1024]{3,2,0,1:T(8,128)(2,1)} %all-gather.5.cloned.1.call-done, bf16[1,1024,2,352]{1,3,2,0:T(8,128)(2,1)S(1)} %copy-done), kind=kOutput, calls=%fused_computation.37 | convolution fusion | flops 1845493760 | bytes 7667712 | tf_op jit(solution)/shard_map/slcd,ldgh->slcgh/dot_general | solution.py:78
  310.1 3.2 convert_bitcast_fusion
  313.4 33.3 %reduce-scatter.2.cloned.1.call-done = bf16[32,1,40,256]{3,2,0,1:T(8,128)(2,1)} async-done(((bf16[32,1,40,1024]{3,2,0,1:T(8,128)(2,1)}), bf16[32,1,40,256]{3,2,0,1:T(8,128)(2,1)}) %reduce-scatter.2.cloned.1.call-update) | async-done | bytes 655376 | tf_op jit(solution)/shard_map/reduce_scatter | solution.py:156
  346.7 9.4 %all-to-all-start.2 = ((bf16[32,1,40,256]{3,2,1,0:T(8,128)(2,1)}), bf16[32,1,40,256]{3,2,1,0:T(8,128)(2,1)S(1)}, u32[]{:S(2)}, u32[]{:S(2)}) async-start(bf16[32,1,40,256]{3,2,1,0:T(8,128)(2,1)} %bitcast.164), calls=%async_computation.3 | async-start | bytes 1310720 | tf_op jit(solution)/shard_map/all_to_all | solution.py:159
  356.7 0.9 copy.91
  357.8 4.6 %gather_fusion.3 = f32[512]{0:T(512)S(1)} fusion(f32[256,16]{0,1:T(8,128)S(1)} %fusion.158, s32[512]{0:T(512)S(1)} %reshape.364), kind=kCustom, calls=%fused_computation.3 | custom fusion | bytes 8192 | tf_op jit(solution)/shard_map/jit(take_along_axis)/gather | solution.py:144
  362.8 5.5 %all-to-all-done.2 = bf16[32,1,40,256]{3,2,1,0:T(8,128)(2,1)S(1)} async-done(((bf16[32,1,40,256]{3,2,1,0:T(8,128)(2,1)}), bf16[32,1,40,256]{3,2,1,0:T(8,128)(2,1)S(1)}, u32[]{:S(2)}, u32[]{:S(2)}) %all-to-all-start.2) | async-done | bytes 655392 | tf_op jit(solution)/shard_map/all_to_all | solution.py:159
  368.4 1.6 gather_fusion.2
  370.3 0.7 multiply_reduce_fusion.1
  371.0 1.7 add_convert_fusion
  (140 shorter events, 8.4 us)
Async XLA Ops:
  7.2 298.9 %copy-start = (bf16[1,1024,2,352]{1,3,2,0:T(8,128)(2,1)S(1)}, bf16[1,1024,2,352]{1,3,2,0:T(8,128)(2,1)}, u32[]{:S(2)}) copy-start(bf16[1,1024,2,352]{1,3,2,0:T(8,128)(2,1)} %param.24) | copy-start | bytes 4325380
  10.6 11.5 %copy-start.38 = (s32[4]{0:T(128)S(1)}, s32[4]{0:T(128)}, u32[]{:S(2)}) copy-start(s32[4]{0:T(128)} %param.16) | copy-start | bytes 52
  10.6 42.5 %copy-start.31 = (s32[1,4]{1,0:T(1,128)S(1)}, s32[1,4]{1,0:T(1,128)}, u32[]{:S(2)}) copy-start(s32[1,4]{1,0:T(1,128)} %param.14) | copy-start | bytes 52
  10.7 45.9 %copy-start.30 = (s32[1,4]{1,0:T(1,128)S(1)}, s32[1,4]{1,0:T(1,128)}, u32[]{:S(2)}) copy-start(s32[1,4]{1,0:T(1,128)} %param.15) | copy-start | bytes 52
  10.7 51.5 %copy-start.28 = (s32[256,2]{0,1:T(2,128)S(1)}, s32[256,2]{0,1:T(2,128)}, u32[]{:S(2)}) copy-start(s32[256,2]{0,1:T(2,128)} %param.23) | copy-start | bytes 6148
  10.7 39.4 %all-to-all-start = ((bf16[32,64,2,256]{3,1,2,0:T(8,128)(2,1)}), bf16[32,64,2,256]{3,1,2,0:T(8,128)(2,1)S(1)}, u32[]{:S(2)}, u32[]{:S(2)}) async-start(bf16[32,64,2,256]{3,1,2,0:T(8,128)(2,1)} %copy.74), calls=%async_computation | async-start | bytes 4194304 | tf_op jit(solution)/shard_map/all_to_all | solution.py:121
  22.1 132.5 %all-gather.3.cloned.1.call-start = ((), (), s32[]{:S(2)}) async-start(), calls=%async_computation.4 | async-start | bytes 8650752 | tf_op jit(solution)/shard_map/all_gather | solution.py:123
  51.3 13.0 %copy-start.21 = (bf16[256,256]{1,0:T(8,128)(2,1)S(1)}, bf16[256,256]{1,0:T(8,128)(2,1)}, u32[]{:S(2)}) copy-start(bf16[256,256]{1,0:T(8,128)(2,1)} %param.13) | copy-start | bytes 393220
  53.1 194.3 %all-reduce.7.cloned.1.call-start = ((), (), s32[]{:S(2)}) async-start(), calls=%async_computation.5 | async-start | bytes 1048576 | tf_op jit(solution)/shard_map/psum | solution.py:137
  62.4 11.2 %copy-start.37 = (f32[1024]{0:T(1024)S(1)}, f32[1024]{0:T(1024)}, u32[]{:S(2)}) copy-start(f32[1024]{0:T(1024)} %param.18) | copy-start | bytes 12292
  72.8 0.8 copy-start.2
  74.4 20.0 %copy-start.9 = (bf16[256,768]{0,1:T(8,128)(2,1)}, bf16[256,768]{0,1:T(8,128)(2,1)S(1)}, u32[]{:S(2)}) copy-start(bf16[256,768]{0,1:T(8,128)(2,1)S(1)} %copy.77) | copy-start | bytes 1179652
  171.9 3.2 copy-start.12
  171.9 3.3 copy-start.16
  171.9 3.3 copy-start.22
  171.9 3.3 copy-start.27
  176.4 1.2 copy-start.4
  176.4 1.2 copy-start.20
  176.5 1.2 copy-start.35
  184.4 1.2 copy-start.5
  184.4 1.3 copy-start.6
  184.4 1.3 copy-start.19
  184.4 1.2 copy-start.34
  193.7 1.7 copy-start.15
  193.7 1.8 copy-start.23
  193.7 1.8 copy-start.26
  196.7 1.0 copy-start.7
  196.7 1.0 copy-start.18
  196.7 0.9 copy-start.33
  204.1 1.7 copy-start.14
  204.1 1.8 copy-start.24
  204.1 1.8 copy-start.25
  207.2 1.0 copy-start.8
  207.2 1.0 copy-start.17
  208.1 1.4 copy-start.13
  209.1 38.3 %copy-start.3 = (bf16[256,1024]{1,0:T(8,128)(2,1)S(1)}, bf16[256,1024]{1,0:T(8,128)(2,1)}, u32[]{:S(2)}) copy-start(bf16[256,1024]{1,0:T(8,128)(2,1)} %copy-done.2) | copy-start | bytes 1572868
  209.2 40.6 %copy-start.32 = (f32[1024]{0:T(1024)S(1)}, f32[1024]{0:T(1024)}, u32[]{:S(2)}) copy-start(f32[1024]{0:T(1024)} %param.21) | copy-start | bytes 12292
  210.7 95.3 %all-gather.5.cloned.1.call-start = ((), (), s32[]{:S(2)}) async-start(), calls=%async_computation.6 | async-start | bytes 3276800 | tf_op jit(solution)/shard_map/all_gather | solution.py:154
  247.5 2.3 copy-start.11
  274.7 35.4 %copy-start.36 = (bf16[1,352,1024]{2,1,0:T(8,128)(2,1)S(1)}, bf16[1,352,1024]{2,1,0:T(8,128)(2,1)}, u32[]{:S(2)}) copy-start(bf16[1,352,1024]{2,1,0:T(8,128)(2,1)} %param.25) | copy-start | bytes 2162692
  274.7 72.0 %reduce-scatter.2.cloned.1.call-start = ((), (), s32[]{:S(2)}) async-start(), calls=%async_computation.7 | async-start | bytes 3276800 | tf_op jit(solution)/shard_map/reduce_scatter | solution.py:156
  313.3 42.8 %copy-start.10 = (bf16[256,768]{0,1:T(8,128)(2,1)S(1)}, bf16[256,768]{0,1:T(8,128)(2,1)}, u32[]{:S(2)}) copy-start(bf16[256,768]{0,1:T(8,128)(2,1)} %copy-done.9) | copy-start | bytes 1179652
  313.3 44.2 %copy-start.29 = (bf16[1024,16]{0,1:T(8,128)(2,1)S(1)}, bf16[1024,16]{0,1:T(8,128)(2,1)}, u32[]{:S(2)}) copy-start(bf16[1024,16]{0,1:T(8,128)(2,1)} %param.22) | copy-start | bytes 98308
  346.7 21.6 %all-to-all-start.2 = ((bf16[32,1,40,256]{3,2,1,0:T(8,128)(2,1)}), bf16[32,1,40,256]{3,2,1,0:T(8,128)(2,1)S(1)}, u32[]{:S(2)}, u32[]{:S(2)}) async-start(bf16[32,1,40,256]{3,2,1,0:T(8,128)(2,1)} %bitcast.164), calls=%async_computation.3 | async-start | bytes 1310720 | tf_op jit(solution)/shard_map/all_to_all | solution.py:159
  368.4 4.3 %copy-start.1 = (bf16[1,1024,2,352]{1,3,2,0:T(8,128)(2,1)S(1)}, bf16[1,1024,2,352]{1,3,2,0:T(8,128)(2,1)}, u32[]{:S(2)}) copy-start(bf16[1,1024,2,352]{1,3,2,0:T(8,128)(2,1)} %param.24) | copy-start | bytes 4325380
Sparse Core Ops, SparseCore 0:
  53.3 101.3 all-gather.2
  210.8 36.5 all-reduce.6
  274.8 31.1 all-gather.4
  313.5 33.1 reduce-scatter.1

commit v3 on v1

--- a/solution.py
+++ b/solution.py
@@ -4,6 +4,8 @@
 import jax.numpy as jnp
 from jax import lax
 from jax.sharding import PartitionSpec as P
+from jax.experimental import pallas as pl
+from jax.experimental.pallas import tpu as pltpu
 
 HEAD_DIM = 64
 EXPERTS = 16
@@ -55,6 +57,95 @@
     context = context * inside[:, None, None].astype(jnp.float32)
     placed = jnp.zeros((row_count,) + context.shape[1:], jnp.float32)
     return lax.dynamic_update_slice_in_dim(placed, context, first, 0)
+
+
+def attention_kernel(
+    group_ref, start_ref, length_ref, query_ref, key_ref, value_ref, prefix_ref, out_ref
+):
+    request = pl.program_id(0)
+
+    @pl.when(request == 0)
+    def _():
+        out_ref[...] = jnp.zeros_like(out_ref)
+
+    start = start_ref[request]
+    stop = start + length_ref[request]
+    rows, width = query_ref.shape
+    row_ids = lax.broadcasted_iota(jnp.int32, (rows, rows), 0)
+    col_ids = lax.broadcasted_iota(jnp.int32, (rows, rows), 1)
+    suffix_ok = (col_ids <= row_ids) & (col_ids >= start)
+    lane_head = lax.broadcasted_iota(jnp.int32, (1, width), 1) // HEAD_DIM
+    query = query_ref[...]
+    keys = key_ref[...]
+    values = value_ref[...]
+    prefix_keys = prefix_ref[0, 0]
+    prefix_values = prefix_ref[0, 1]
+    scale = 1.0 / math.sqrt(HEAD_DIM)
+    contract = (((1,), (1,)), ((), ()))
+    context = jnp.zeros((rows, width), jnp.float32)
+    for head in range(width // HEAD_DIM):
+        in_head = lane_head == head
+        query_h = jnp.where(in_head, query, jnp.zeros_like(query))
+        score_pre = lax.dot_general(
+            query_h, prefix_keys, contract, preferred_element_type=jnp.float32
+        ) * scale
+        score_suf = lax.dot_general(
+            query_h, keys, contract, preferred_element_type=jnp.float32
+        ) * scale
+        score_suf = jnp.where(suffix_ok, score_suf, -1e30)
+        highest = jnp.maximum(
+            jnp.max(score_pre, axis=1, keepdims=True), jnp.max(score_suf, axis=1, keepdims=True)
+        )
+        weight_pre = jnp.exp(score_pre - highest)
+        weight_suf = jnp.exp(score_suf - highest)
+        totals = jnp.sum(weight_pre, axis=1, keepdims=True) + jnp.sum(
+            weight_suf, axis=1, keepdims=True
+        )
+        mixed = jnp.dot(
+            weight_pre.astype(jnp.bfloat16), prefix_values, preferred_element_type=jnp.float32
+        ) + jnp.dot(weight_suf.astype(jnp.bfloat16), values, preferred_element_type=jnp.float32)
+        context = context + jnp.where(in_head, mixed / totals, 0.0)
+    row_in = lax.broadcasted_iota(jnp.int32, (rows, 1), 0)
+    inside = (row_in >= start) & (row_in < stop)
+    out_ref[...] = jnp.where(inside, context.astype(out_ref.dtype), out_ref[...])
+
+
+def attention(query, keys, values, prefix, block_groups, starts, block_lengths, interpret=False):
+    rows, width = query.shape
+    slots = prefix.shape[0]
+    full = lambda i, g, s, n: (0, 0)
+    grid_spec = pltpu.PrefetchScalarGridSpec(
+        num_scalar_prefetch=3,
+        grid=(block_groups.shape[0],),
+        in_specs=[
+            pl.BlockSpec((rows, width), full),
+            pl.BlockSpec((rows, width), full),
+            pl.BlockSpec((rows, width), full),
+            pl.BlockSpec((1, 2, PREFIX, width), lambda i, g, s, n: (g[i], 0, 0, 0)),
+        ],
+        out_specs=pl.BlockSpec((rows, width), full),
+    )
+    flops = 4 * 2 * 2 * rows * (PREFIX + rows) * width * block_groups.shape[0]
+    return pl.pallas_call(
+        attention_kernel,
+        grid_spec=grid_spec,
+        out_shape=jax.ShapeDtypeStruct((rows, width), jnp.bfloat16),
+        compiler_params=pltpu.CompilerParams(dimension_semantics=("arbitrary",)),
+        interpret=interpret,
+        cost_estimate=pl.CostEstimate(
+            flops=flops,
+            transcendentals=4 * rows * (PREFIX + rows) * block_groups.shape[0],
+            bytes_accessed=slots * 2 * PREFIX * width * 2 + 4 * rows * width * 2,
+        ),
+    )(
+        jnp.clip(block_groups, 0, slots - 1),
+        starts,
+        block_lengths,
+        query,
+        keys,
+        values,
+        prefix,
+    )
 
 
 def slot_ranks(identity, experts):
@@ -108,31 +199,19 @@
     )
     qkv = qkv.astype(jnp.bfloat16).reshape(row_count, 3, quarter)
     suffix_kv = jnp.stack([qkv[:, 1], qkv[:, 2]], axis=1)
-    query_all = qkv[:, 0].reshape(row_count, local_heads, HEAD_DIM)
-    key_all = qkv[:, 1].reshape(row_count, local_heads, HEAD_DIM)
-    value_all = qkv[:, 2].reshape(row_count, local_heads, HEAD_DIM)
     own_slot = prefix_cache[0]
     block_lengths = lengths[0]
     block_groups = groups[0]
     starts = jnp.cumsum(block_lengths) - block_lengths
-    context = jnp.zeros((row_count, local_heads, HEAD_DIM), jnp.float32)
     req_total = lax.axis_size("req")
     pieces = own_slot.reshape(req_total, PREFIX // req_total, 2, quarter)
     pieces = lax.all_to_all(pieces, "req", split_axis=0, concat_axis=0, tiled=True)
     owned = jnp.take(pieces, owners, axis=0)
     cached = lax.all_gather(owned, "req", axis=1, tiled=True)
-    for request in range(REQ_DEV):
-        prefix_kv = cached[block_groups[request]].reshape(PREFIX, 2, local_heads, HEAD_DIM)
-        context = context + request_context(
-            query_all,
-            key_all,
-            value_all,
-            prefix_kv,
-            starts[request],
-            block_lengths[request],
-            SUF_MOST,
-        )
-    context = context.reshape(row_count, quarter).astype(jnp.bfloat16)
+    cached = jnp.transpose(cached, (0, 2, 1, 3))
+    context = attention(
+        qkv[:, 0], qkv[:, 1], qkv[:, 2], cached, block_groups, starts, block_lengths
+    )
     partial_attn = jnp.dot(context, w_out, preferred_element_type=jnp.float32)
     resid = tokens.astype(jnp.float32) + lax.psum_scatter(
         partial_attn.astype(jnp.bfloat16), "exp", scatter_dimension=1, tiled=True

time: 376 us -> 344 us (0.915)
  local copies, waits for them, and re-layouts: 74.8 us -> 32.1 us
  waiting for transfers between devices: 145 us -> 168 us
  Pallas kernels: 0 us -> 19.2 us
  between operations: 29.5 us -> 14.1 us
  matrix products: 20.6 us -> 9.25 us
  other arithmetic: 23.5 us -> 18.8 us
    dynamic_slice x6 -> x0, local copies, waits for them, and re-layouts: 21.8 us -> none  [the longest x5 20.7 us: shards(): cached[block_groups[request]].reshape(PREFIX, 2, local_heads, HEAD_DIM)]
    all_gather x1, waiting for transfers between devices: 61.2 us -> 81.5 us  [shards(): cached = lax.all_gather(owned, 'req', axis=1, tiled=True)]
    pallas_call x0 -> x1, Pallas kernels: none -> 19.2 us  [attention(): pl.pallas_call(attention_kernel, grid_spec=grid_spec, out_shape=jax.Shape...]
    dot_general x8 -> x0, matrix products: 12.3 us -> none  [the longest x4 6.21 us: request_context(): jnp.einsum('qhd,khd->hqk', query_win, keys, preferred_element_type=jnp.fl...]
    squeeze x4 -> x0, local copies, waits for them, and re-layouts: 9.79 us -> none  [request_context(): values = jnp.concatenate([prefix_kv[:, 1], value_win], axis=0)]
    add x3 -> x0, local copies, waits for them, and re-layouts: 5.05 us -> none  [shards(): context + request_context(query_all, key_all, value_all, prefix_kv, start...]
    convert_element_type x5 -> x0, other arithmetic: 4.69 us -> none  [the longest x4 4.67 us: request_context(): context = context * inside[:, None, None].astype(jnp.float32)]
  transfers between devices with their start and end apart: 5 -> 5, of which waited for: 5 -> 5; matrix products, arithmetic and copies ran while one was open for 8% -> 6% of each run, Pallas kernels for 0% -> 0%
where the time goes in v3:
time: 344 us; the launch traced here: 343 us
  waiting for transfers between devices  168 us (49%)
  blocking collectives  64.8 us (19%)
  local copies, waits for them, and re-layouts  32.1 us (9%)
  Pallas kernels  19.2 us (6%)
  other arithmetic  18.8 us (5%)
  starting transfers between devices  17 us (5%)
  between operations  14.1 us (4%)
  matrix products  9.25 us (3%)
    all_gather x1, waiting for transfers between devices, shards(): cached = lax.all_gather(owned, 'req', axis=1, tiled=True)  81.5 us
    all_to_all x1, blocking collectives, shards(): lax.all_to_all(outgoing_rows, 'req', split_axis=0, concat_axis=0, tiled=T...  43 us
    all_to_all x1, waiting for transfers between devices, shards(): lax.all_to_all(pieces, 'req', split_axis=0, concat_axis=0, tiled=True)  27.8 us
    all_to_all x1, waiting for transfers between devices, shards(): lax.all_to_all(partial_out.astype(jnp.bfloat16), 'req', split_axis=0, con...  27.2 us
    pallas_call x1, Pallas kernels, attention(): pl.pallas_call(attention_kernel, grid_spec=grid_spec, out_shape=jax.Shape...  19.2 us
    reduce_scatter x1, waiting for transfers between devices, shards(): lax.psum_scatter(mixture.astype(jnp.bfloat16), 'exp', scatter_dimension=1...  18.3 us
    reduce_scatter x1, waiting for transfers between devices, shards(): lax.psum_scatter(partial_attn.astype(jnp.bfloat16), 'exp', scatter_dimens...  12.7 us
    all_to_all x1, starting transfers between devices, shards(): lax.all_to_all(pieces, 'req', split_axis=0, concat_axis=0, tiled=True)  11.5 us
  transfers between devices with their start and end apart: 5, of which 5 were waited for; matrix products, arithmetic and copies ran while one was open for 6% of the time, Pallas kernels for 0%

profile of v3, /device:TPU:1, one launch (start us, length us, event | category | flops | bytes accessed | tf_op | source)
XLA Modules:
  0.0 342.9 jit_solution(11634315503817939714)
XLA Ops:
  7.2 3.5 %copy.73 = bf16[32,64,2,256]{3,1,2,0:T(8,128)(2,1)} copy(bf16[32,64,2,256]{3,2,1,0:T(2,128)(2,1)} %bitcast.91) | data formatting | bytes 4194304 | tf_op jit(solution)/shard_map/reshape;squeeze | solution.py:207
  10.7 11.5 %all-to-all-start = ((bf16[32,64,2,256]{3,1,2,0:T(8,128)(2,1)}), bf16[32,64,2,256]{3,1,2,0:T(8,128)(2,1)S(1)}, u32[]{:S(2)}, u32[]{:S(2)}) async-start(bf16[32,64,2,256]{3,1,2,0:T(8,128)(2,1)} %copy.73), calls=%async_computation | async-start | bytes 4194304 | tf_op jit(solution)/shard_map/all_to_all | solution.py:208
  22.1 0.0 all-gather.2.cloned.1.call-start
  22.2 27.8 %all-to-all-done = bf16[32,64,2,256]{3,1,2,0:T(8,128)(2,1)S(1)} async-done(((bf16[32,64,2,256]{3,1,2,0:T(8,128)(2,1)}), bf16[32,64,2,256]{3,1,2,0:T(8,128)(2,1)S(1)}, u32[]{:S(2)}, u32[]{:S(2)}) %all-to-all-start) | async-done | bytes 2097184 | tf_op jit(solution)/shard_map/all_to_all | solution.py:208
  50.1 1.3 gather_fusion
  51.3 1.7 broadcast_select_fusion
  53.1 0.0 all-gather.2.cloned.1.call-update
  53.1 0.0 reduce-scatter.3.cloned.1.call-start
  53.2 0.1 copy.74
  53.3 0.1 eq.29
  53.5 0.1 eq.25
  53.6 1.4 reduce-window.19
  55.0 0.1 copy.77
  55.2 0.1 mul.127
  55.3 1.7 copy.67
  57.1 8.5 %all_gather.9 = bf16[256,1024]{1,0:T(8,128)(2,1)S(1)} all-gather(bf16[256,256]{1,0:T(8,128)(2,1)S(1)} %copy-done.5), channel_id=1, replica_groups=mesh['req'=32,'exp'=4] {'exp'}, dimensions={1}, use_global_device_ids=true | all-gather | bytes 655360 | tf_op jit(solution)/shard_map/all_gather | solution.py:191
  65.6 0.2 fusion.15
  65.8 1.4 convolution_convert_fusion.1
  67.2 1.2 copy.68
  68.4 0.8 copy.89
  69.2 0.7 copy.88
  70.0 0.8 copy.87
  70.8 0.5 clamp_bitcast_fusion.group_ref
  71.3 0.6 bitcast_subtract_fusion.start_ref
  71.9 81.5 %all-gather.2.cloned.1.call-done = bf16[4,2048,2,256]{3,1,2,0:T(8,128)(2,1)} async-done(((bf16[4,64,2,256]{3,1,2,0:T(8,128)(2,1)}), bf16[4,2048,2,256]{3,1,2,0:T(8,128)(2,1)}) %all-gather.2.cloned.1.call-update) | async-done | bytes 8388624 | tf_op jit(solution)/shard_map/all_gather | solution.py:210
  153.4 19.2 %shard_map.140 = bf16[256,256]{1,0:T(8,128)(2,1)} custom-call(s32[4]{0:T(128)} %clamp_bitcast_fusion.group_ref, s32[4]{0:T(128)} %bitcast_subtract_fusion.start_ref, s32[4]{0:T(128)} %bitcast.101, bf16[256,256]{1,0:T(8,128)(2,1)} %bitcast.95, bf16[256,256]{1,0:T(8,128)(2,1)} %bitcast.94, bf16[256,256]{1,0:T(8,128)(2,1)} %bitcast.93, ...), custom_call_target="tpu_custom_call" | custom-call | flops 9663676416 | bytes 8912896 | tf_op jit(solution)/shard_map/pallas_call | solution.py:129
  172.6 2.0 convolution_convert_fusion
  174.6 0.0 reduce-scatter.3.cloned.1.call-update
  174.7 1.2 reduce-window.20
  175.8 0.2 slice_reduce_fusion
  176.1 0.8 dynamic_slice.3
  176.8 0.1 fusion.29
  176.9 2.4 scatter_custom_fusion
  179.4 12.7 %reduce-scatter.3.cloned.1.call-done = bf16[256,256]{1,0:T(8,128)(2,1)} async-done(((bf16[256,1024]{1,0:T(8,128)(2,1)}), bf16[256,256]{1,0:T(8,128)(2,1)}) %reduce-scatter.3.cloned.1.call-update) | async-done | bytes 131088 | tf_op jit(solution)/shard_map/reduce_scatter | solution.py:216
  192.1 1.0 multiply_reduce_fusion.1
  193.2 5.1 %psum.7 = f32[256]{0:T(256)S(1)} all-reduce(f32[256]{0:T(256)S(1)} %multiply_reduce_fusion.1), channel_id=1, replica_groups=mesh['req'=32,'exp'=4] {'exp'}, use_global_device_ids=true, to_apply=%region_4.5 | all-reduce | flops 256 | bytes 2048 | tf_op jit(solution)/shard_map/psum | solution.py:219
  198.3 1.0 multiply_convert_fusion
  199.3 8.2 %all_gather.11 = bf16[256,1024]{1,0:T(8,128)(2,1)S(1)} all-gather(bf16[256,256]{1,0:T(8,128)(2,1)S(1)} %multiply_convert_fusion), channel_id=1, replica_groups=mesh['req'=32,'exp'=4] {'exp'}, dimensions={1}, use_global_device_ids=true | all-gather | bytes 655360 | tf_op jit(solution)/shard_map/all_gather | solution.py:225
  207.5 0.8 copy-done.1
  208.4 2.8 gather_fusion.1
  211.2 0.4 broadcast_in_dim.52
  211.6 43.0 %all_to_all.15 = bf16[32,1,40,1024]{3,2,1,0:T(8,128)(2,1)S(1)} all-to-all(bf16[32,1,40,1024]{3,2,1,0:T(8,128)(2,1)S(1)} %bitcast.87), channel_id=1, replica_groups=mesh['req'=32,'exp'=4] {'req'}, dimensions={0} | all-to-all | bytes 5242880 | tf_op jit(solution)/shard_map/all_to_all | solution.py:238
  254.6 2.3 fusion.2
  256.9 3.3 convert_bitcast_fusion
  260.2 5.4 %all-to-all-start.2 = ((bf16[32,1,40,1024]{3,2,1,0:T(8,128)(2,1)}), bf16[32,1,40,1024]{3,2,1,0:T(8,128)(2,1)}, u32[]{:S(2)}, u32[]{:S(2)}) async-start(bf16[32,1,40,1024]{3,2,1,0:T(8,128)(2,1)} %convert_bitcast_fusion), calls=%async_computation.3 | async-start | bytes 5242880 | tf_op jit(solution)/shard_map/all_to_all | solution.py:240
  265.6 0.0 reduce-scatter.5.cloned.1.call-start
  265.7 0.1 copy.79
  265.8 0.1 reshape.249
  266.0 0.2 lt.66
  266.2 0.1 copy.81
  266.3 0.2 fusion.42
  266.5 4.6 %gather_fusion.3 = f32[512]{0:T(512)S(1)} fusion(f32[256,16]{0,1:T(8,128)S(1)} %fusion.42, s32[512]{0:T(512)S(1)} %reshape.249), kind=kCustom, calls=%fused_computation.3 | custom fusion | bytes 8192 | tf_op jit(solution)/shard_map/jit(take_along_axis)/gather | solution.py:227
  271.1 0.1 reshape.252
  271.2 0.1 copy.80
  271.3 0.8 copy.82
  272.2 27.2 %all-to-all-done.2 = bf16[32,1,40,1024]{3,2,1,0:T(8,128)(2,1)} async-done(((bf16[32,1,40,1024]{3,2,1,0:T(8,128)(2,1)}), bf16[32,1,40,1024]{3,2,1,0:T(8,128)(2,1)}, u32[]{:S(2)}, u32[]{:S(2)}) %all-to-all-start.2) | async-done | bytes 2621472 | tf_op jit(solution)/shard_map/all_to_all | solution.py:240
  299.4 4.1 %convert_reduce_fusion = f32[16,40,1024]{2,1,0:T(8,128)} fusion(bf16[16,2,40,1024]{3,2,1,0:T(8,128)(2,1)} %bitcast.84), kind=kLoop, calls=%fused_computation.5 | loop fusion | flops 1966080 | bytes 5242880 | tf_op jit(solution)/shard_map/reduce_sum | solution.py:244
  303.5 4.6 %gather_fusion.2 = f32[512,1024]{1,0:T(8,128)S(1)} fusion(f32[640,1024]{1,0:T(8,128)} %bitcast.86, s32[1024]{0:T(1024)S(1)} %pad_clamp_fusion), kind=kCustom, calls=%fused_computation.2 | custom fusion | bytes 4196352 | tf_op jit(solution)/shard_map/gather | solution.py:248
  308.1 2.3 reshape.221
  310.4 5.2 %multiply_reduce_fusion = bf16[256,1024]{1,0:T(8,128)(2,1)} fusion(f32[256,2,1024]{2,1,0:T(2,128)} %reshape.221, f32[256,2]{1,0:T(8,128)} %copy.82), kind=kLoop, calls=%fused_computation.10 | loop fusion | flops 786432 | bytes 2623488 | tf_op jit(solution)/shard_map/reduce_sum | solution.py:250
  315.6 0.0 reduce-scatter.5.cloned.1.call-update
  315.7 0.9 copy.83
  316.5 18.3 %reduce-scatter.5.cloned.1.call-done = bf16[256,256]{1,0:T(8,128)(2,1)} async-done(((bf16[256,1024]{1,0:T(8,128)(2,1)}), bf16[256,256]{1,0:T(8,128)(2,1)}) %reduce-scatter.5.cloned.1.call-update) | async-done | bytes 131088 | tf_op jit(solution)/shard_map/reduce_scatter | solution.py:251
  334.8 1.6 add_convert_fusion
  (53 shorter events, 0.3 us)
Async XLA Ops:
  7.2 247.4 %copy-start = (bf16[1,1024,2,352]{1,3,2,0:T(8,128)(2,1)S(1)}, bf16[1,1024,2,352]{1,3,2,0:T(8,128)(2,1)}, u32[]{:S(2)}) copy-start(bf16[1,1024,2,352]{1,3,2,0:T(8,128)(2,1)} %param.24) | copy-start | bytes 4325380
  10.7 11.5 %copy-start.13 = (s32[4]{0:T(128)S(1)}, s32[4]{0:T(128)}, u32[]{:S(2)}) copy-start(s32[4]{0:T(128)} %param.16) | copy-start | bytes 52
  10.7 42.5 %copy-start.9 = (s32[256,2]{0,1:T(2,128)S(1)}, s32[256,2]{0,1:T(2,128)}, u32[]{:S(2)}) copy-start(s32[256,2]{0,1:T(2,128)} %param.23) | copy-start | bytes 6148
  10.7 39.4 %all-to-all-start = ((bf16[32,64,2,256]{3,1,2,0:T(8,128)(2,1)}), bf16[32,64,2,256]{3,1,2,0:T(8,128)(2,1)S(1)}, u32[]{:S(2)}, u32[]{:S(2)}) async-start(bf16[32,64,2,256]{3,1,2,0:T(8,128)(2,1)} %copy.73), calls=%async_computation | async-start | bytes 4194304 | tf_op jit(solution)/shard_map/all_to_all | solution.py:208
  22.1 131.2 %all-gather.2.cloned.1.call-start = ((), (), s32[]{:S(2)}) async-start(), calls=%async_computation.5 | async-start | bytes 8650752 | tf_op jit(solution)/shard_map/all_gather | solution.py:210
  53.1 4.0 %copy-start.5 = (bf16[256,256]{1,0:T(8,128)(2,1)S(1)}, bf16[256,256]{1,0:T(8,128)(2,1)}, u32[]{:S(2)}) copy-start(bf16[256,256]{1,0:T(8,128)(2,1)} %param.13) | copy-start | bytes 393220
  53.1 139.0 %reduce-scatter.3.cloned.1.call-start = ((), (), s32[]{:S(2)}) async-start(), calls=%async_computation.6 | async-start | bytes 655360 | tf_op jit(solution)/shard_map/reduce_scatter | solution.py:216
  55.3 10.4 %copy-start.12 = (f32[1024]{0:T(1024)S(1)}, f32[1024]{0:T(1024)}, u32[]{:S(2)}) copy-start(f32[1024]{0:T(1024)} %param.18) | copy-start | bytes 12292
  67.2 3.6 %copy-start.14 = (s32[1,4]{1,0:T(1,128)S(1)}, s32[1,4]{1,0:T(1,128)}, u32[]{:S(2)}) copy-start(s32[1,4]{1,0:T(1,128)} %param.15) | copy-start | bytes 52
  67.2 4.1 %copy-start.15 = (s32[1,4]{1,0:T(1,128)S(1)}, s32[1,4]{1,0:T(1,128)}, u32[]{:S(2)}) copy-start(s32[1,4]{1,0:T(1,128)} %param.14) | copy-start | bytes 52
  67.2 4.1 %copy-start.16 = (s32[4,1]{0,1:T(1,128)S(1)}, s32[4,1]{0,1:T(1,128)}, u32[]{:S(2)}) copy-start(s32[4,1]{0,1:T(1,128)} %reduce-window.19) | copy-start | bytes 52
  68.4 104.2 %copy-start.3 = (bf16[256,768]{0,1:T(8,128)(2,1)}, bf16[256,768]{0,1:T(8,128)(2,1)S(1)}, u32[]{:S(2)}) copy-start(bf16[256,768]{0,1:T(8,128)(2,1)S(1)} %copy.68) | copy-start | bytes 1179652
  153.4 19.2 %copy-start.8 = (bf16[256,1024]{1,0:T(8,128)(2,1)S(1)}, bf16[256,1024]{1,0:T(8,128)(2,1)}, u32[]{:S(2)}) copy-start(bf16[256,1024]{1,0:T(8,128)(2,1)} %param.20) | copy-start | bytes 1572868
  207.5 0.8 copy-start.1
  254.6 2.3 copy-start.11
  260.2 6.1 %copy-start.2 = (bf16[256,1024]{1,0:T(8,128)(2,1)S(1)}, bf16[256,1024]{1,0:T(8,128)(2,1)}, u32[]{:S(2)}) copy-start(bf16[256,1024]{1,0:T(8,128)(2,1)} %copy-done.1) | copy-start | bytes 1572868
  260.2 6.1 %copy-start.10 = (bf16[1024,16]{0,1:T(8,128)(2,1)S(1)}, bf16[1024,16]{0,1:T(8,128)(2,1)}, u32[]{:S(2)}) copy-start(bf16[1024,16]{0,1:T(8,128)(2,1)} %param.22) | copy-start | bytes 98308
  260.2 39.2 %all-to-all-start.2 = ((bf16[32,1,40,1024]{3,2,1,0:T(8,128)(2,1)}), bf16[32,1,40,1024]{3,2,1,0:T(8,128)(2,1)}, u32[]{:S(2)}, u32[]{:S(2)}) async-start(bf16[32,1,40,1024]{3,2,1,0:T(8,128)(2,1)} %convert_bitcast_fusion), calls=%async_computation.3 | async-start | bytes 5242880 | tf_op jit(solution)/shard_map/all_to_all | solution.py:240
  265.6 69.2 %reduce-scatter.5.cloned.1.call-start = ((), (), s32[]{:S(2)}) async-start(), calls=%async_computation.7 | async-start | bytes 655360 | tf_op jit(solution)/shard_map/reduce_scatter | solution.py:251
  310.4 5.2 %copy-start.4 = (bf16[256,768]{0,1:T(8,128)(2,1)S(1)}, bf16[256,768]{0,1:T(8,128)(2,1)}, u32[]{:S(2)}) copy-start(bf16[256,768]{0,1:T(8,128)(2,1)} %copy-done.3) | copy-start | bytes 1179652
  310.4 24.4 %copy-start.6 = (bf16[256,256]{1,0:T(8,128)(2,1)S(1)}, bf16[256,256]{1,0:T(8,128)(2,1)}, u32[]{:S(2)}) copy-start(bf16[256,256]{1,0:T(8,128)(2,1)} %param.13) | copy-start | bytes 393220
  310.4 24.4 %copy-start.7 = (bf16[256,256]{1,0:T(8,128)(2,1)S(1)}, bf16[256,256]{1,0:T(8,128)(2,1)}, u32[]{:S(2)}) copy-start(bf16[256,256]{1,0:T(8,128)(2,1)} %reduce-scatter.3.cloned.1.call-done) | copy-start | bytes 393220
Sparse Core Ops, SparseCore 0:
  53.2 100.1 all-gather.1
  174.8 17.3 reduce-scatter.2
  315.7 19.0 reduce-scatter.4

commit v4 on v3

--- a/solution.py
+++ b/solution.py
@@ -240,14 +240,19 @@
     returned = lax.all_to_all(
         partial_out.astype(jnp.bfloat16), "req", split_axis=0, concat_axis=0, tiled=True
     ).astype(partial_out.dtype)
-    out_columns = returned.shape[3]
-    summed = jnp.sum(returned.reshape(EXPERTS, SPLIT, CAP, out_columns), axis=1).reshape(
-        EXPERTS * CAP, out_columns
-    )
-    source = flat_ids * CAP + jnp.minimum(ranks, CAP - 1)
-    chosen = summed[source].reshape(row_count, TOP, out_columns)
-    scale = jnp.where(kept, gates, 0.0).reshape(row_count, TOP)
-    mixture = jnp.sum(chosen * scale[:, :, None], axis=1)
+    block_count, _, _, out_columns = returned.shape
+    pair_column = flat_ids * (SPLIT * CAP) + jnp.minimum(ranks, CAP - 1)
+    pair_scale = jnp.where(kept, gates, 0.0)
+    columns_all = lax.broadcasted_iota(jnp.int32, (row_count * TOP, block_count * CAP), 1)
+    offset = columns_all - pair_column[:, None]
+    hit = (offset == 0) | (offset == CAP)
+    selection = jnp.where(hit, pair_scale[:, None], 0.0).reshape(row_count, TOP, -1).sum(axis=1)
+    mixture = jnp.dot(
+        selection,
+        returned.reshape(block_count * CAP, out_columns).astype(jnp.float32),
+        precision=lax.Precision.HIGHEST,
+        preferred_element_type=jnp.float32,
+    )
     moe_part = lax.psum_scatter(
         mixture.astype(jnp.bfloat16), "exp", scatter_dimension=1, tiled=True
     ).astype(jnp.float32)

time: 344 us -> 332 us (0.965)
  other arithmetic: 18.8 us -> 9.57 us
  local copies, waits for them, and re-layouts: 32.1 us -> 24.6 us
  matrix products: 9.25 us -> 14.1 us
    reduce_sum x2 -> x1, other arithmetic: 9.34 us -> 0.7 us  [shards(): jnp.where(hit, pair_scale[:, None], 0.0).reshape(row_count, TOP, -1)]
    dot_general x0 -> x1, matrix products: none -> 4.84 us  [shards(): jnp.dot(selection, returned.reshape(block_count * CAP, out_columns).astyp...]
    gather x1 -> x0, local copies, waits for them, and re-layouts: 4.56 us -> none  [shards(): chosen = summed[source].reshape(row_count, TOP, out_columns)]
  transfers between devices with their start and end apart: 5 -> 5, of which waited for: 5 -> 5; matrix products, arithmetic and copies ran while one was open for 6% -> 7% of each run, Pallas kernels for 0% -> 0%
where the time goes in v4:
time: 332 us
  waiting for transfers between devices  168 us (51%)
  blocking collectives  64.8 us (20%)
  local copies, waits for them, and re-layouts  24.6 us (7%)
  Pallas kernels  19.2 us (6%)
  starting transfers between devices  17 us (5%)
  matrix products  14.1 us (4%)
  between operations  14.1 us (4%)
  other arithmetic  9.57 us (3%)
    all_gather x1, waiting for transfers between devices, shards(): cached = lax.all_gather(owned, 'req', axis=1, tiled=True)  80.9 us
    all_to_all x1, blocking collectives, shards(): lax.all_to_all(outgoing_rows, 'req', split_axis=0, concat_axis=0, tiled=T...  43 us
    all_to_all x1, waiting for transfers between devices, shards(): lax.all_to_all(pieces, 'req', split_axis=0, concat_axis=0, tiled=True)  27.8 us
    all_to_all x1, waiting for transfers between devices, shards(): lax.all_to_all(partial_out.astype(jnp.bfloat16), 'req', split_axis=0, con...  27.3 us
    pallas_call x1, Pallas kernels, attention(): pl.pallas_call(attention_kernel, grid_spec=grid_spec, out_shape=jax.Shape...  19.2 us
    reduce_scatter x1, waiting for transfers between devices, shards(): lax.psum_scatter(mixture.astype(jnp.bfloat16), 'exp', scatter_dimension=1...  18.3 us
    reduce_scatter x1, waiting for transfers between devices, shards(): lax.psum_scatter(partial_attn.astype(jnp.bfloat16), 'exp', scatter_dimens...  13.7 us
    all_to_all x1, starting transfers between devices, shards(): lax.all_to_all(pieces, 'req', split_axis=0, concat_axis=0, tiled=True)  11.5 us
  transfers between devices with their start and end apart: 5, of which 5 were waited for; matrix products, arithmetic and copies ran while one was open for 7% of the time, Pallas kernels for 0%

profile of v4, /device:TPU:1, one launch (start us, length us, event | category | flops | bytes accessed | tf_op | source)
XLA Modules:
  0.0 331.5 jit_solution(6820034060304876031)
XLA Ops:
  7.2 0.0 copy-start
  7.2 3.5 %copy.102 = bf16[32,64,2,256]{3,1,2,0:T(8,128)(2,1)} copy(bf16[32,64,2,256]{3,2,1,0:T(2,128)(2,1)} %bitcast.87) | data formatting | bytes 4194304 | tf_op jit(solution)/shard_map/reshape;squeeze | solution.py:207
  10.7 11.5 %all-to-all-start = ((bf16[32,64,2,256]{3,1,2,0:T(8,128)(2,1)}), bf16[32,64,2,256]{3,1,2,0:T(8,128)(2,1)S(1)}, u32[]{:S(2)}, u32[]{:S(2)}) async-start(bf16[32,64,2,256]{3,1,2,0:T(8,128)(2,1)} %copy.102), calls=%async_computation | async-start | bytes 4194304 | tf_op jit(solution)/shard_map/all_to_all | solution.py:208
  22.1 0.0 all-gather.2.cloned.1.call-start
  22.2 27.8 %all-to-all-done = bf16[32,64,2,256]{3,1,2,0:T(8,128)(2,1)S(1)} async-done(((bf16[32,64,2,256]{3,1,2,0:T(8,128)(2,1)}), bf16[32,64,2,256]{3,1,2,0:T(8,128)(2,1)S(1)}, u32[]{:S(2)}, u32[]{:S(2)}) %all-to-all-start) | async-done | bytes 2097184 | tf_op jit(solution)/shard_map/all_to_all | solution.py:208
  50.1 1.3 gather_fusion
  51.3 1.7 broadcast_select_fusion
  53.1 0.0 all-gather.2.cloned.1.call-update
  53.1 0.0 reduce-scatter.3.cloned.1.call-start
  53.2 0.1 copy.103
  53.3 0.1 eq.43
  53.5 0.1 eq.39
  53.6 0.8 reduce-window.19
  54.4 1.1 reduce-window.20
  55.6 0.2 slice_reduce_fusion
  55.9 1.7 copy.96
  57.6 8.5 %all_gather.9 = bf16[256,1024]{1,0:T(8,128)(2,1)S(1)} all-gather(bf16[256,256]{1,0:T(8,128)(2,1)S(1)} %copy-done.5), channel_id=1, replica_groups=mesh['req'=32,'exp'=4] {'exp'}, dimensions={1}, use_global_device_ids=true | all-gather | bytes 655360 | tf_op jit(solution)/shard_map/all_gather | solution.py:191
  66.1 0.2 fusion.18
  66.4 1.4 convolution_convert_fusion.2
  67.8 1.2 copy.97
  69.0 0.8 copy.118
  69.8 0.7 copy.117
  70.5 0.8 copy.116
  71.3 0.1 fusion.32
  71.4 0.6 clamp_bitcast_fusion.group_ref
  72.0 0.5 bitcast_subtract_fusion.start_ref
  72.5 80.9 %all-gather.2.cloned.1.call-done = bf16[4,2048,2,256]{3,1,2,0:T(8,128)(2,1)} async-done(((bf16[4,64,2,256]{3,1,2,0:T(8,128)(2,1)}), bf16[4,2048,2,256]{3,1,2,0:T(8,128)(2,1)}) %all-gather.2.cloned.1.call-update) | async-done | bytes 8388624 | tf_op jit(solution)/shard_map/all_gather | solution.py:210
  153.4 19.2 %shard_map.140 = bf16[256,256]{1,0:T(8,128)(2,1)} custom-call(s32[4]{0:T(128)} %clamp_bitcast_fusion.group_ref, s32[4]{0:T(128)} %bitcast_subtract_fusion.start_ref, s32[4]{0:T(128)} %bitcast.96, bf16[256,256]{1,0:T(8,128)(2,1)} %bitcast.91, bf16[256,256]{1,0:T(8,128)(2,1)} %bitcast.90, bf16[256,256]{1,0:T(8,128)(2,1)} %bitcast.89, ...), custom_call_target="tpu_custom_call" | custom-call | flops 9663676416 | bytes 8912896 | tf_op jit(solution)/shard_map/pallas_call | solution.py:129
  172.6 2.0 convolution_convert_fusion
  174.6 0.0 reduce-scatter.3.cloned.1.call-update
  174.7 0.1 min.28
  174.8 0.1 copy.106
  174.9 0.1 copy.110
  175.0 0.1 mul.126
  175.2 0.8 dynamic_slice.3
  176.0 2.4 scatter_custom_fusion
  178.4 13.7 %reduce-scatter.3.cloned.1.call-done = bf16[256,256]{1,0:T(8,128)(2,1)} async-done(((bf16[256,1024]{1,0:T(8,128)(2,1)}), bf16[256,256]{1,0:T(8,128)(2,1)}) %reduce-scatter.3.cloned.1.call-update) | async-done | bytes 131088 | tf_op jit(solution)/shard_map/reduce_scatter | solution.py:216
  192.1 1.0 multiply_reduce_fusion
  193.1 5.1 %psum.7 = f32[256]{0:T(256)S(1)} all-reduce(f32[256]{0:T(256)S(1)} %multiply_reduce_fusion), channel_id=1, replica_groups=mesh['req'=32,'exp'=4] {'exp'}, use_global_device_ids=true, to_apply=%region_7.8 | all-reduce | flops 256 | bytes 2048 | tf_op jit(solution)/shard_map/psum | solution.py:219
  198.3 1.0 multiply_convert_fusion
  199.3 8.2 %all_gather.11 = bf16[256,1024]{1,0:T(8,128)(2,1)S(1)} all-gather(bf16[256,256]{1,0:T(8,128)(2,1)S(1)} %multiply_convert_fusion), channel_id=1, replica_groups=mesh['req'=32,'exp'=4] {'exp'}, dimensions={1}, use_global_device_ids=true | all-gather | bytes 655360 | tf_op jit(solution)/shard_map/all_gather | solution.py:225
  207.5 0.8 copy-done.1
  208.3 2.8 gather_fusion.1
  211.2 0.4 broadcast_in_dim.69
  211.5 43.0 %all_to_all.15 = bf16[32,1,40,1024]{3,2,1,0:T(8,128)(2,1)S(1)} all-to-all(bf16[32,1,40,1024]{3,2,1,0:T(8,128)(2,1)S(1)} %bitcast.83), channel_id=1, replica_groups=mesh['req'=32,'exp'=4] {'req'}, dimensions={0} | all-to-all | bytes 5242880 | tf_op jit(solution)/shard_map/all_to_all | solution.py:238
  254.5 2.3 fusion.5
  256.9 3.3 convert_bitcast_fusion
  260.1 5.4 %all-to-all-start.2 = ((bf16[32,1,40,1024]{3,2,1,0:T(8,128)(2,1)}), bf16[32,1,40,1024]{3,2,1,0:T(8,128)(2,1)}, u32[]{:S(2)}, u32[]{:S(2)}) async-start(bf16[32,1,40,1024]{3,2,1,0:T(8,128)(2,1)} %convert_bitcast_fusion), calls=%async_computation.3 | async-start | bytes 5242880 | tf_op jit(solution)/shard_map/all_to_all | solution.py:240
  265.6 0.0 reduce-scatter.5.cloned.1.call-start
  265.7 0.1 copy.107
  265.8 0.1 reshape.232
  266.0 0.2 lt.56
  266.1 0.1 copy.109
  266.2 0.2 fusion.45
  266.5 4.6 %gather_fusion.2 = f32[512]{0:T(512)S(1)} fusion(f32[256,16]{0,1:T(8,128)S(1)} %fusion.45, s32[512]{0:T(512)S(1)} %reshape.232), kind=kCustom, calls=%fused_computation.2 | custom fusion | bytes 8192 | tf_op jit(solution)/shard_map/jit(take_along_axis)/gather | solution.py:227
  271.0 0.1 reshape.235
  271.2 0.1 copy.108
  271.3 0.7 select_reduce_fusion
  272.0 27.3 %all-to-all-done.2 = bf16[32,1,40,1024]{3,2,1,0:T(8,128)(2,1)} async-done(((bf16[32,1,40,1024]{3,2,1,0:T(8,128)(2,1)}), bf16[32,1,40,1024]{3,2,1,0:T(8,128)(2,1)}, u32[]{:S(2)}, u32[]{:S(2)}) %all-to-all-start.2) | async-done | bytes 2621472 | tf_op jit(solution)/shard_map/all_to_all | solution.py:240
  299.3 4.8 %convolution_convert_fusion.1 = bf16[256,1024]{1,0:T(8,128)(2,1)} fusion(f32[256,1280]{1,0:T(8,128)S(1)} %select_reduce_fusion, bf16[1280,1024]{1,0:T(8,128)(2,1)} %bitcast.34), kind=kOutput, calls=%fused_computation.27 | convolution fusion | flops 4026793984 | bytes 4456448 | tf_op jit(solution)/shard_map/dot_general | solution.py:250
  304.2 0.0 reduce-scatter.5.cloned.1.call-update
  304.2 0.9 copy.112
  305.1 18.3 %reduce-scatter.5.cloned.1.call-done = bf16[256,256]{1,0:T(8,128)(2,1)} async-done(((bf16[256,1024]{1,0:T(8,128)(2,1)}), bf16[256,256]{1,0:T(8,128)(2,1)}) %reduce-scatter.5.cloned.1.call-update) | async-done | bytes 131088 | tf_op jit(solution)/shard_map/reduce_scatter | solution.py:256
  323.4 1.6 add_convert_fusion
  (51 shorter events, 0.3 us)
Async XLA Ops:
  7.2 247.4 %copy-start = (bf16[1,1024,2,352]{1,3,2,0:T(8,128)(2,1)S(1)}, bf16[1,1024,2,352]{1,3,2,0:T(8,128)(2,1)}, u32[]{:S(2)}) copy-start(bf16[1,1024,2,352]{1,3,2,0:T(8,128)(2,1)} %param.24) | copy-start | bytes 4325380
  10.7 11.5 %copy-start.13 = (s32[4]{0:T(128)S(1)}, s32[4]{0:T(128)}, u32[]{:S(2)}) copy-start(s32[4]{0:T(128)} %param.16) | copy-start | bytes 52
  10.7 42.5 %copy-start.8 = (s32[256,2]{0,1:T(2,128)S(1)}, s32[256,2]{0,1:T(2,128)}, u32[]{:S(2)}) copy-start(s32[256,2]{0,1:T(2,128)} %param.23) | copy-start | bytes 6148
  10.7 39.4 %all-to-all-start = ((bf16[32,64,2,256]{3,1,2,0:T(8,128)(2,1)}), bf16[32,64,2,256]{3,1,2,0:T(8,128)(2,1)S(1)}, u32[]{:S(2)}, u32[]{:S(2)}) async-start(bf16[32,64,2,256]{3,1,2,0:T(8,128)(2,1)} %copy.102), calls=%async_computation | async-start | bytes 4194304 | tf_op jit(solution)/shard_map/all_to_all | solution.py:208
  22.1 131.2 %all-gather.2.cloned.1.call-start = ((), (), s32[]{:S(2)}) async-start(), calls=%async_computation.5 | async-start | bytes 8650752 | tf_op jit(solution)/shard_map/all_gather | solution.py:210
  53.1 4.5 %copy-start.5 = (bf16[256,256]{1,0:T(8,128)(2,1)S(1)}, bf16[256,256]{1,0:T(8,128)(2,1)}, u32[]{:S(2)}) copy-start(bf16[256,256]{1,0:T(8,128)(2,1)} %param.13) | copy-start | bytes 393220
  53.1 139.0 %reduce-scatter.3.cloned.1.call-start = ((), (), s32[]{:S(2)}) async-start(), calls=%async_computation.6 | async-start | bytes 655360 | tf_op jit(solution)/shard_map/reduce_scatter | solution.py:216
  55.8 10.5 %copy-start.10 = (s32[16,5]{0,1:T(8,128)}, s32[16,5]{0,1:T(8,128)S(1)}, u32[]{:S(2)}) copy-start(s32[16,5]{0,1:T(8,128)S(1)} %reduce-window.21) | copy-start | bytes 964
  55.8 10.5 %copy-start.12 = (f32[1024]{0:T(1024)S(1)}, f32[1024]{0:T(1024)}, u32[]{:S(2)}) copy-start(f32[1024]{0:T(1024)} %param.18) | copy-start | bytes 12292
  66.3 5.0 %slice-start = ((s32[16,5]{0,1:T(8,128)}), s32[16,4]{0,1:T(4,128)S(1)}, s32[]{:S(2)}) async-start(s32[16,5]{0,1:T(8,128)} %copy-done.10), calls=%async_computation.8 | async-start | bytes 4096 | tf_op jit(solution)/shard_map/slice.1
  66.3 5.1 %copy-start.14 = (s32[1,4]{1,0:T(1,128)S(1)}, s32[1,4]{1,0:T(1,128)}, u32[]{:S(2)}) copy-start(s32[1,4]{1,0:T(1,128)} %param.15) | copy-start | bytes 52
  66.3 5.7 %copy-start.15 = (s32[1,4]{1,0:T(1,128)S(1)}, s32[1,4]{1,0:T(1,128)}, u32[]{:S(2)}) copy-start(s32[1,4]{1,0:T(1,128)} %param.14) | copy-start | bytes 52
  69.0 103.7 %copy-start.3 = (bf16[256,768]{0,1:T(8,128)(2,1)}, bf16[256,768]{0,1:T(8,128)(2,1)S(1)}, u32[]{:S(2)}) copy-start(bf16[256,768]{0,1:T(8,128)(2,1)S(1)} %copy.97) | copy-start | bytes 1179652
  153.4 19.2 %copy-start.7 = (bf16[256,1024]{1,0:T(8,128)(2,1)S(1)}, bf16[256,1024]{1,0:T(8,128)(2,1)}, u32[]{:S(2)}) copy-start(bf16[256,1024]{1,0:T(8,128)(2,1)} %param.20) | copy-start | bytes 1572868
  207.5 0.8 copy-start.1
  254.5 2.3 copy-start.11
  260.1 6.1 %copy-start.2 = (bf16[256,1024]{1,0:T(8,128)(2,1)S(1)}, bf16[256,1024]{1,0:T(8,128)(2,1)}, u32[]{:S(2)}) copy-start(bf16[256,1024]{1,0:T(8,128)(2,1)} %copy-done.1) | copy-start | bytes 1572868
  260.1 6.1 %copy-start.9 = (bf16[1024,16]{0,1:T(8,128)(2,1)S(1)}, bf16[1024,16]{0,1:T(8,128)(2,1)}, u32[]{:S(2)}) copy-start(bf16[1024,16]{0,1:T(8,128)(2,1)} %param.22) | copy-start | bytes 98308
  260.1 39.2 %all-to-all-start.2 = ((bf16[32,1,40,1024]{3,2,1,0:T(8,128)(2,1)}), bf16[32,1,40,1024]{3,2,1,0:T(8,128)(2,1)}, u32[]{:S(2)}, u32[]{:S(2)}) async-start(bf16[32,1,40,1024]{3,2,1,0:T(8,128)(2,1)} %convert_bitcast_fusion), calls=%async_computation.3 | async-start | bytes 5242880 | tf_op jit(solution)/shard_map/all_to_all | solution.py:240
  265.6 57.8 %reduce-scatter.5.cloned.1.call-start = ((), (), s32[]{:S(2)}) async-start(), calls=%async_computation.7 | async-start | bytes 655360 | tf_op jit(solution)/shard_map/reduce_scatter | solution.py:256
  299.3 4.9 %copy-start.4 = (bf16[256,768]{0,1:T(8,128)(2,1)S(1)}, bf16[256,768]{0,1:T(8,128)(2,1)}, u32[]{:S(2)}) copy-start(bf16[256,768]{0,1:T(8,128)(2,1)} %copy-done.3) | copy-start | bytes 1179652
  299.3 24.0 %copy-start.6 = (bf16[256,256]{1,0:T(8,128)(2,1)S(1)}, bf16[256,256]{1,0:T(8,128)(2,1)}, u32[]{:S(2)}) copy-start(bf16[256,256]{1,0:T(8,128)(2,1)} %reduce-scatter.3.cloned.1.call-done) | copy-start | bytes 393220
Sparse Core Ops, SparseCore 0:
  53.2 100.1 all-gather.1
  174.8 17.3 reduce-scatter.2
  304.3 19.0 reduce-scatter.4

commit v5 on v4

--- a/solution.py
+++ b/solution.py
@@ -212,17 +212,13 @@
     context = attention(
         qkv[:, 0], qkv[:, 1], qkv[:, 2], cached, block_groups, starts, block_lengths
     )
-    partial_attn = jnp.dot(context, w_out, preferred_element_type=jnp.float32)
-    resid = tokens.astype(jnp.float32) + lax.psum_scatter(
-        partial_attn.astype(jnp.bfloat16), "exp", scatter_dimension=1, tiled=True
-    ).astype(jnp.float32)
-    squares = lax.psum(jnp.sum(resid * resid, axis=1), "exp")
+    context_full = lax.all_gather(context, "exp", axis=1, tiled=True)
+    w_out_full = lax.all_gather(w_out, "exp", axis=0, tiled=True)
+    attn_full = jnp.dot(context_full, w_out_full, preferred_element_type=jnp.float32)
+    resid_full = rows_whole.astype(jnp.float32) + attn_full
+    x_source = norm_rows(resid_full, moe_gain).astype(jnp.bfloat16)
     column_start = lax.axis_index("exp") * quarter
-    gain_part = lax.dynamic_slice_in_dim(moe_gain, column_start, quarter, 0)
-    x_part = (resid * lax.rsqrt(squares / full_width + epsilon)[:, None] * gain_part).astype(
-        jnp.bfloat16
-    )
-    x_source = lax.all_gather(x_part, "exp", axis=1, tiled=True)
+    resid = lax.dynamic_slice_in_dim(resid_full, column_start, quarter, 1)
     logits = jnp.dot(x_source, w_router, preferred_element_type=jnp.float32)
     gates = jax.nn.sigmoid(jnp.take_along_axis(logits, expert_ids, axis=1)).reshape(-1)
     flat_ids, ranks = slot_ranks(expert_ids, EXPERTS)

time: 332 us -> 315 us (0.949)
  waiting for transfers between devices: 168 us -> 151 us
    reduce_scatter x1 -> x0, waiting for transfers between devices: 13.7 us -> none  [shards(): lax.psum_scatter(partial_attn.astype(jnp.bfloat16), 'exp', scatter_dimens...]
    psum x1 -> x0, blocking collectives: 5.12 us -> none  [shards(): squares = lax.psum(jnp.sum(resid * resid, axis=1), 'exp')]
    all_gather x1, waiting for transfers between devices: 80.9 us -> 76 us  [shards(): cached = lax.all_gather(owned, 'req', axis=1, tiled=True)]
    all_gather x1, blocking collectives: 8.19 us -> 11.6 us  [shards(): context_full = lax.all_gather(context, 'exp', axis=1, tiled=True)]
  transfers between devices with their start and end apart: 5 -> 5, of which waited for: 5 -> 5; matrix products, arithmetic and copies ran while one was open for 7% -> 7% of each run, Pallas kernels for 0% -> 6%
where the time goes in v5:
time: 315 us; the launch traced here: 314 us
  waiting for transfers between devices  151 us (48%)
  blocking collectives  63.7 us (20%)
  local copies, waits for them, and re-layouts  25 us (8%)
  Pallas kernels  19.1 us (6%)
  starting transfers between devices  16.7 us (5%)
  matrix products  15.5 us (5%)
  between operations  14.1 us (4%)
  other arithmetic  9.33 us (3%)
    all_gather x1, waiting for transfers between devices, shards(): cached = lax.all_gather(owned, 'req', axis=1, tiled=True)  76 us
    all_to_all x1, blocking collectives, shards(): lax.all_to_all(outgoing_rows, 'req', split_axis=0, concat_axis=0, tiled=T...  43.3 us
    all_to_all x1, waiting for transfers between devices, shards(): lax.all_to_all(pieces, 'req', split_axis=0, concat_axis=0, tiled=True)  27.8 us
    all_to_all x1, waiting for transfers between devices, shards(): lax.all_to_all(partial_out.astype(jnp.bfloat16), 'req', split_axis=0, con...  26.2 us
    pallas_call x1, Pallas kernels, attention(): pl.pallas_call(attention_kernel, grid_spec=grid_spec, out_shape=jax.Shape...  19.1 us
    reduce_scatter x1, waiting for transfers between devices, shards(): lax.psum_scatter(mixture.astype(jnp.bfloat16), 'exp', scatter_dimension=1...  18.5 us
    all_gather x1, blocking collectives, shards(): context_full = lax.all_gather(context, 'exp', axis=1, tiled=True)  11.6 us
    all_to_all x1, starting transfers between devices, shards(): lax.all_to_all(pieces, 'req', split_axis=0, concat_axis=0, tiled=True)  11.5 us
  transfers between devices with their start and end apart: 5, of which 5 were waited for; matrix products, arithmetic and copies ran while one was open for 7% of the time, Pallas kernels for 6%

profile of v5, /device:TPU:1, one launch (start us, length us, event | category | flops | bytes accessed | tf_op | source)
XLA Modules:
  0.0 314.2 jit_solution(4604352134457583217)
XLA Ops:
  7.2 0.0 copy-start
  7.2 3.5 %copy.102 = bf16[32,64,2,256]{3,1,2,0:T(8,128)(2,1)} copy(bf16[32,64,2,256]{3,2,1,0:T(2,128)(2,1)} %bitcast.86) | data formatting | bytes 4194304 | tf_op jit(solution)/shard_map/reshape;squeeze | solution.py:207
  10.7 11.5 %all-to-all-start = ((bf16[32,64,2,256]{3,1,2,0:T(8,128)(2,1)}), bf16[32,64,2,256]{3,1,2,0:T(8,128)(2,1)S(1)}, u32[]{:S(2)}, u32[]{:S(2)}) async-start(bf16[32,64,2,256]{3,1,2,0:T(8,128)(2,1)} %copy.102), calls=%async_computation | async-start | bytes 4194304 | tf_op jit(solution)/shard_map/all_to_all | solution.py:208
  22.1 0.0 all-gather.3.cloned.1.call-start
  22.2 27.8 %all-to-all-done = bf16[32,64,2,256]{3,1,2,0:T(8,128)(2,1)S(1)} async-done(((bf16[32,64,2,256]{3,1,2,0:T(8,128)(2,1)}), bf16[32,64,2,256]{3,1,2,0:T(8,128)(2,1)S(1)}, u32[]{:S(2)}, u32[]{:S(2)}) %all-to-all-start) | async-done | bytes 2097184 | tf_op jit(solution)/shard_map/all_to_all | solution.py:208
  50.1 1.3 gather_fusion
  51.3 1.7 broadcast_select_fusion
  53.1 0.0 all-gather.3.cloned.1.call-update
  53.1 0.0 all-gather.5.cloned.1.call-start
  53.1 0.7 all-gather.5.cloned.1.call-update
  53.8 8.7 %all_gather.12 = bf16[256,1024]{1,0:T(8,128)(2,1)S(1)} all-gather(bf16[256,256]{1,0:T(8,128)(2,1)} %param.13), channel_id=1, replica_groups=mesh['req'=32,'exp'=4] {'exp'}, dimensions={1}, use_global_device_ids=true | all-gather | bytes 655360 | tf_op jit(solution)/shard_map/all_gather | solution.py:191
  62.6 0.2 fusion.18
  62.8 2.6 copy.96
  65.4 2.0 convolution_convert_fusion.1
  67.4 0.0 copy-start.14
  67.4 0.0 copy-start.13
  67.4 0.2 copy.97
  67.7 0.1 copy.103
  67.8 0.1 eq.43
  68.0 0.1 eq.39
  68.1 0.8 copy.116
  68.9 0.8 copy.117
  69.6 0.8 copy.118
  70.4 0.2 reduce-window.19
  70.6 1.1 reduce-window.20
  71.7 0.2 slice_reduce_fusion
  72.0 0.1 fusion.32
  72.1 0.1 min.28
  72.3 0.1 copy.106
  72.3 0.6 broadcast_multiply_fusion
  72.9 0.1 copy.110
  73.0 0.1 mul.126
  73.2 2.4 scatter_custom_fusion
  75.7 0.6 pad_clamp_fusion
  76.3 0.5 clamp_bitcast_fusion.group_ref
  76.8 0.6 bitcast_subtract_fusion.start_ref
  77.4 76.0 %all-gather.3.cloned.1.call-done = bf16[4,2048,2,256]{3,1,2,0:T(8,128)(2,1)} async-done(((bf16[4,64,2,256]{3,1,2,0:T(8,128)(2,1)}), bf16[4,2048,2,256]{3,1,2,0:T(8,128)(2,1)}) %all-gather.3.cloned.1.call-update) | async-done | bytes 8388624 | tf_op jit(solution)/shard_map/all_gather | solution.py:210
  153.4 19.1 %shard_map.140 = bf16[256,256]{1,0:T(8,128)(2,1)} custom-call(s32[4]{0:T(128)} %clamp_bitcast_fusion.group_ref, s32[4]{0:T(128)} %bitcast_subtract_fusion.start_ref, s32[4]{0:T(128)} %bitcast.94, bf16[256,256]{1,0:T(8,128)(2,1)} %bitcast.88, bf16[256,256]{1,0:T(8,128)(2,1)} %bitcast.89, bf16[256,256]{1,0:T(8,128)(2,1)} %bitcast.90, ...), custom_call_target="tpu_custom_call" | custom-call | flops 9663676416 | bytes 8912896 | tf_op jit(solution)/shard_map/pallas_call | solution.py:129
  172.5 11.6 %all_gather.14 = bf16[256,1024]{1,0:T(8,128)(2,1)S(1)} all-gather(bf16[256,256]{1,0:T(8,128)(2,1)} %shard_map.140), channel_id=1, replica_groups=mesh['req'=32,'exp'=4] {'exp'}, dimensions={1}, use_global_device_ids=true | all-gather | bytes 655360 | tf_op jit(solution)/shard_map/all_gather | solution.py:215
  184.1 1.7 all-gather.5.cloned.1.call-done
  185.8 2.4 multiply_reduce_fusion
  188.2 0.2 multiply_convert_fusion
  188.4 3.6 %gather_fusion.1 = bf16[640,1024]{1,0:T(8,128)(2,1)} fusion(bf16[257,1024]{1,0:T(8,128)(2,1)S(1)} %concatenate.3, s32[1024]{0:T(1024)} %pad_clamp_fusion), kind=kCustom, calls=%fused_computation.1 | custom fusion | bytes 2624000 | tf_op jit(solution)/shard_map/gather | solution.py:228
  192.0 1.7 broadcast_in_dim.69
  193.7 43.3 %all_to_all.15 = bf16[32,1,40,1024]{3,2,1,0:T(8,128)(2,1)S(1)} all-to-all(bf16[32,1,40,1024]{3,2,1,0:T(8,128)(2,1)S(1)} %bitcast.82), channel_id=1, replica_groups=mesh['req'=32,'exp'=4] {'req'}, dimensions={0} | all-to-all | bytes 5242880 | tf_op jit(solution)/shard_map/all_to_all | solution.py:234
  237.0 2.3 fusion.5
  239.3 3.3 %convert_bitcast_fusion = bf16[32,1,40,1024]{3,2,1,0:T(8,128)(2,1)} fusion(f32[32,1,40,2,352]{4,2,3,0,1:T(8,128)S(1)} %fusion.5, bf16[1,352,1024]{2,1,0:T(8,128)(2,1)S(1)} %copy-done.10), kind=kOutput, calls=%fused_computation.7 | convolution fusion | flops 928563200 | bytes 6946816 | tf_op jit(solution)/shard_map/slch,lhd->slcd/dot_general | solution.py:173
  242.6 5.1 %all-to-all-start.2 = ((bf16[32,1,40,1024]{3,2,1,0:T(8,128)(2,1)}), bf16[32,1,40,1024]{3,2,1,0:T(8,128)(2,1)}, u32[]{:S(2)}, u32[]{:S(2)}) async-start(bf16[32,1,40,1024]{3,2,1,0:T(8,128)(2,1)} %convert_bitcast_fusion), calls=%async_computation.2 | async-start | bytes 5242880 | tf_op jit(solution)/shard_map/all_to_all | solution.py:236
  247.7 0.0 reduce-scatter.2.cloned.1.call-start
  247.8 0.1 copy.107
  247.9 0.1 reshape.236
  248.1 0.2 lt.57
  248.3 0.1 copy.109
  248.4 0.2 fusion.45
  248.6 4.6 %gather_fusion.2 = f32[512]{0:T(512)S(1)} fusion(f32[256,16]{0,1:T(8,128)S(1)} %fusion.45, s32[512]{0:T(512)S(1)} %reshape.236), kind=kCustom, calls=%fused_computation.2 | custom fusion | bytes 8192 | tf_op jit(solution)/shard_map/jit(take_along_axis)/gather | solution.py:223
  253.2 0.1 reshape.239
  253.4 0.1 copy.108
  253.5 1.8 select_reduce_fusion
  255.3 26.2 %all-to-all-done.2 = bf16[32,1,40,1024]{3,2,1,0:T(8,128)(2,1)} async-done(((bf16[32,1,40,1024]{3,2,1,0:T(8,128)(2,1)}), bf16[32,1,40,1024]{3,2,1,0:T(8,128)(2,1)}, u32[]{:S(2)}, u32[]{:S(2)}) %all-to-all-start.2) | async-done | bytes 2621472 | tf_op jit(solution)/shard_map/all_to_all | solution.py:236
  281.4 5.2 %convolution_convert_fusion = bf16[256,1024]{1,0:T(8,128)(2,1)} fusion(f32[256,1280]{1,0:T(8,128)} %select_reduce_fusion, bf16[1280,1024]{1,0:T(8,128)(2,1)} %bitcast.34), kind=kOutput, calls=%fused_computation.27 | convolution fusion | flops 4026793984 | bytes 4456448 | tf_op jit(solution)/shard_map/dot_general | solution.py:246
  286.7 0.0 reduce-scatter.2.cloned.1.call-update
  286.7 0.9 copy.112
  287.6 18.5 %reduce-scatter.2.cloned.1.call-done = bf16[256,256]{1,0:T(8,128)(2,1)} async-done(((bf16[256,1024]{1,0:T(8,128)(2,1)}), bf16[256,256]{1,0:T(8,128)(2,1)}) %reduce-scatter.2.cloned.1.call-update) | async-done | bytes 131088 | tf_op jit(solution)/shard_map/reduce_scatter | solution.py:252
  306.1 1.6 add_convert_fusion
  (45 shorter events, 0.3 us)
Async XLA Ops:
  7.2 229.9 %copy-start = (bf16[1,1024,2,352]{1,3,2,0:T(8,128)(2,1)S(1)}, bf16[1,1024,2,352]{1,3,2,0:T(8,128)(2,1)}, u32[]{:S(2)}) copy-start(bf16[1,1024,2,352]{1,3,2,0:T(8,128)(2,1)} %param.24) | copy-start | bytes 4325380
  10.7 11.5 %copy-start.12 = (s32[4]{0:T(128)S(1)}, s32[4]{0:T(128)}, u32[]{:S(2)}) copy-start(s32[4]{0:T(128)} %param.16) | copy-start | bytes 52
  10.7 39.4 %all-to-all-start = ((bf16[32,64,2,256]{3,1,2,0:T(8,128)(2,1)}), bf16[32,64,2,256]{3,1,2,0:T(8,128)(2,1)S(1)}, u32[]{:S(2)}, u32[]{:S(2)}) async-start(bf16[32,64,2,256]{3,1,2,0:T(8,128)(2,1)} %copy.102), calls=%async_computation | async-start | bytes 4194304 | tf_op jit(solution)/shard_map/all_to_all | solution.py:208
  22.1 131.2 %all-gather.3.cloned.1.call-start = ((), (), s32[]{:S(2)}) async-start(), calls=%async_computation.4 | async-start | bytes 8650752 | tf_op jit(solution)/shard_map/all_gather | solution.py:210
  53.1 132.7 %all-gather.5.cloned.1.call-start = ((), (), s32[]{:S(2)}) async-start(), calls=%async_computation.5 | async-start | bytes 2621440 | tf_op jit(solution)/shard_map/all_gather | solution.py:216
  62.6 2.8 copy-start.11
  65.4 2.3 copy-start.3
  67.4 3.0 copy-start.14
  67.4 8.8 %copy-start.13 = (s32[1,4]{1,0:T(1,128)S(1)}, s32[1,4]{1,0:T(1,128)}, u32[]{:S(2)}) copy-start(s32[1,4]{1,0:T(1,128)} %param.15) | copy-start | bytes 52
  67.6 104.8 %copy-start.1 = (bf16[256,768]{0,1:T(8,128)(2,1)}, bf16[256,768]{0,1:T(8,128)(2,1)S(1)}, u32[]{:S(2)}) copy-start(bf16[256,768]{0,1:T(8,128)(2,1)S(1)} %copy.97) | copy-start | bytes 1179652
  72.1 100.4 %copy-start.6 = (s32[512]{0:T(512)}, s32[512]{0:T(512)S(1)}, u32[]{:S(2)}) copy-start(s32[512]{0:T(512)S(1)} %fusion.32) | copy-start | bytes 6148
  184.1 4.1 %copy-start.9 = (f32[1024]{0:T(1024)S(1)}, f32[1024]{0:T(1024)}, u32[]{:S(2)}) copy-start(f32[1024]{0:T(1024)} %param.21) | copy-start | bytes 12292
  237.0 2.3 copy-start.10
  242.6 5.2 %copy-start.4 = (s32[256,2]{0,1:T(2,128)S(1)}, s32[256,2]{0,1:T(2,128)}, u32[]{:S(2)}) copy-start(s32[256,2]{0,1:T(2,128)} %param.23) | copy-start | bytes 6148
  242.6 5.5 %copy-start.7 = (s32[512]{0:T(512)S(1)}, s32[512]{0:T(512)}, u32[]{:S(2)}) copy-start(s32[512]{0:T(512)} %copy-done.6) | copy-start | bytes 6148
  242.6 5.8 %copy-start.5 = (bf16[1024,16]{0,1:T(8,128)(2,1)S(1)}, bf16[1024,16]{0,1:T(8,128)(2,1)}, u32[]{:S(2)}) copy-start(bf16[1024,16]{0,1:T(8,128)(2,1)} %param.22) | copy-start | bytes 98308
  242.6 38.8 %all-to-all-start.2 = ((bf16[32,1,40,1024]{3,2,1,0:T(8,128)(2,1)}), bf16[32,1,40,1024]{3,2,1,0:T(8,128)(2,1)}, u32[]{:S(2)}, u32[]{:S(2)}) async-start(bf16[32,1,40,1024]{3,2,1,0:T(8,128)(2,1)} %convert_bitcast_fusion), calls=%async_computation.2 | async-start | bytes 5242880 | tf_op jit(solution)/shard_map/all_to_all | solution.py:236
  247.7 58.4 %reduce-scatter.2.cloned.1.call-start = ((), (), s32[]{:S(2)}) async-start(), calls=%async_computation.6 | async-start | bytes 655360 | tf_op jit(solution)/shard_map/reduce_scatter | solution.py:252
  248.6 4.8 %copy-start.8 = (s32[256,2]{0,1:T(2,128)S(1)}, s32[256,2]{0,1:T(2,128)}, u32[]{:S(2)}) copy-start(s32[256,2]{0,1:T(2,128)} %get-tuple-element.18) | copy-start | bytes 6148
  281.4 5.2 %copy-start.2 = (bf16[256,768]{0,1:T(8,128)(2,1)S(1)}, bf16[256,768]{0,1:T(8,128)(2,1)}, u32[]{:S(2)}) copy-start(bf16[256,768]{0,1:T(8,128)(2,1)} %copy-done.1) | copy-start | bytes 1179652
Sparse Core Ops, SparseCore 0:
  53.2 100.1 all-gather.2
  155.0 30.7 all-gather.4
  286.8 19.2 reduce-scatter.1

commit v6 on v5

--- a/solution.py
+++ b/solution.py
@@ -213,7 +213,14 @@
         qkv[:, 0], qkv[:, 1], qkv[:, 2], cached, block_groups, starts, block_lengths
     )
     context_full = lax.all_gather(context, "exp", axis=1, tiled=True)
-    w_out_full = lax.all_gather(w_out, "exp", axis=0, tiled=True)
+    exp_total = lax.axis_size("exp")
+    w_out_full = lax.all_to_all(
+        jnp.broadcast_to(w_out[None], (exp_total,) + w_out.shape),
+        "exp",
+        split_axis=0,
+        concat_axis=0,
+        tiled=True,
+    ).reshape(exp_total * w_out.shape[0], w_out.shape[1])
     attn_full = jnp.dot(context_full, w_out_full, preferred_element_type=jnp.float32)
     resid_full = rows_whole.astype(jnp.float32) + attn_full
     x_source = norm_rows(resid_full, moe_gain).astype(jnp.bfloat16)
@@ -249,9 +256,15 @@
         precision=lax.Precision.HIGHEST,
         preferred_element_type=jnp.float32,
     )
-    moe_part = lax.psum_scatter(
-        mixture.astype(jnp.bfloat16), "exp", scatter_dimension=1, tiled=True
-    ).astype(jnp.float32)
+    blocks = jnp.transpose(
+        mixture.astype(jnp.bfloat16).reshape(row_count, exp_total, quarter), (1, 0, 2)
+    )
+    moe_part = jnp.sum(
+        lax.all_to_all(blocks, "exp", split_axis=0, concat_axis=0, tiled=True).astype(
+            jnp.float32
+        ),
+        axis=0,
+    )
     hidden_out = (resid + moe_part).astype(jnp.bfloat16)
     return (hidden_out, suffix_kv)
 

time: 315 us -> 305 us (0.968)
  waiting for transfers between devices: 151 us -> 102 us
  local copies, waits for them, and re-layouts: 25 us -> 42.2 us
  starting transfers between devices: 16.7 us -> 28.5 us
  other arithmetic: 9.33 us -> 14.8 us
  blocking collectives: 63.7 us -> 68.7 us
    all_gather x1, waiting for transfers between devices: 76 us -> 39.6 us  [shards(): cached = lax.all_gather(owned, 'req', axis=1, tiled=True)]
    reduce_scatter x1 -> x0, waiting for transfers between devices: 18.5 us -> none  [shards(): lax.psum_scatter(mixture.astype(jnp.bfloat16), 'exp', scatter_dimension=1...]
    all_to_all x0 -> x2, starting transfers between devices: none -> 11.5 us  [the longest x1 5.87 us: shards(): lax.all_to_all(jnp.broadcast_to(w_out[None], (exp_total,) + w_out.shape),...]
    all_gather x1, blocking collectives: 8.72 us -> 19.6 us  [shards(): rows_whole = lax.all_gather(tokens, 'exp', axis=1, tiled=True)]
    all_to_all x0 -> x2, waiting for transfers between devices: none -> 6.96 us  [the longest x1 6.95 us: shards(): lax.all_to_all(blocks, 'exp', split_axis=0, concat_axis=0, tiled=True)]
    unnamed x36 -> x28, local copies, waits for them, and re-layouts: 5.98 us -> 11.7 us
    another operation x3, other arithmetic: 1.36 us -> 4.57 us
  transfers between devices with their start and end apart: 5 -> 5, of which waited for: 5 -> 4; matrix products, arithmetic and copies ran while one was open for 7% -> 15% of each run, Pallas kernels for 6% -> 6%
where the time goes in v6:
time: 305 us; the launch traced here: 304 us
  waiting for transfers between devices  102 us (33%)
  blocking collectives  68.7 us (23%)
  local copies, waits for them, and re-layouts  42.2 us (14%)
  starting transfers between devices  28.5 us (9%)
  Pallas kernels  19.1 us (6%)
  other arithmetic  14.8 us (5%)
  matrix products  14.7 us (5%)
  between operations  14.3 us (5%)
    all_to_all x1, blocking collectives, shards(): lax.all_to_all(outgoing_rows, 'req', split_axis=0, concat_axis=0, tiled=T...  40.6 us
    all_gather x1, waiting for transfers between devices, shards(): cached = lax.all_gather(owned, 'req', axis=1, tiled=True)  39.6 us
    all_to_all x1, waiting for transfers between devices, shards(): lax.all_to_all(pieces, 'req', split_axis=0, concat_axis=0, tiled=True)  27.8 us
    all_to_all x1, waiting for transfers between devices, shards(): lax.all_to_all(partial_out.astype(jnp.bfloat16), 'req', split_axis=0, con...  27.4 us
    all_gather x1, blocking collectives, shards(): rows_whole = lax.all_gather(tokens, 'exp', axis=1, tiled=True)  19.6 us
    pallas_call x1, Pallas kernels, attention(): pl.pallas_call(attention_kernel, grid_spec=grid_spec, out_shape=jax.Shape...  19.1 us
    unnamed x28, local copies, waits for them, and re-layouts  11.7 us
    all_to_all x1, starting transfers between devices, shards(): lax.all_to_all(pieces, 'req', split_axis=0, concat_axis=0, tiled=True)  11.5 us
  transfers between devices with their start and end apart: 5, of which 4 were waited for; matrix products, arithmetic and copies ran while one was open for 15% of the time, Pallas kernels for 6%

profile of v6, /device:TPU:1, one launch (start us, length us, event | category | flops | bytes accessed | tf_op | source)
XLA Modules:
  0.0 304.1 jit_solution(15597701201627034432)
XLA Ops:
  7.2 3.5 %copy.104 = bf16[32,64,2,256]{3,1,2,0:T(8,128)(2,1)} copy(bf16[32,64,2,256]{3,2,1,0:T(2,128)(2,1)} %bitcast.96) | data formatting | bytes 4194304 | tf_op jit(solution)/shard_map/reshape;squeeze | solution.py:207
  10.7 11.5 %all-to-all-start = ((bf16[32,64,2,256]{3,1,2,0:T(8,128)(2,1)}), bf16[32,64,2,256]{3,1,2,0:T(8,128)(2,1)S(1)}, u32[]{:S(2)}, u32[]{:S(2)}) async-start(bf16[32,64,2,256]{3,1,2,0:T(8,128)(2,1)} %copy.104), calls=%async_computation | async-start | bytes 4194304 | tf_op jit(solution)/shard_map/all_to_all | solution.py:208
  22.2 27.8 %all-to-all-done = bf16[32,64,2,256]{3,1,2,0:T(8,128)(2,1)S(1)} async-done(((bf16[32,64,2,256]{3,1,2,0:T(8,128)(2,1)}), bf16[32,64,2,256]{3,1,2,0:T(8,128)(2,1)S(1)}, u32[]{:S(2)}, u32[]{:S(2)}) %all-to-all-start) | async-done | bytes 2097184 | tf_op jit(solution)/shard_map/all_to_all | solution.py:208
  50.1 1.3 gather_fusion
  51.3 1.7 broadcast_select_fusion
  53.1 2.7 broadcast_in_dim.67
  55.8 5.9 %all-to-all-start.1 = ((bf16[4,256,1024]{2,1,0:T(8,128)(2,1)}), bf16[4,256,1024]{2,1,0:T(8,128)(2,1)S(1)}, u32[]{:S(2)}, u32[]{:S(2)}) async-start(bf16[4,256,1024]{2,1,0:T(8,128)(2,1)} %broadcast_in_dim.67), calls=%async_computation.1 | async-start | bytes 4194304 | tf_op jit(solution)/shard_map/all_to_all | solution.py:217
  61.7 0.8 copy.105
  62.5 1.1 eq.43
  63.5 1.0 eq.39
  64.6 0.6 fusion.33
  65.2 3.1 %reduce-window.20 = s32[16,4,128]{2,0,1:T(8,128)} reduce-window(s32[16,4,128]{2,0,1:T(8,128)} %fusion.33, s32[]{:T(128)} %constant.31.clone.1), window={size=1x1x128 pad=0_0x0_0x127_0}, to_apply=%region_2.3 | reduce-window | flops 1040384 | bytes 65540 | tf_op jit(solution)/shard_map/reduce-window.1
  68.3 1.0 slice_reduce_fusion
  69.4 0.9 fusion.32
  70.2 0.8 min.28
  71.0 1.0 copy.108
  72.0 0.6 broadcast_multiply_fusion
  72.6 1.5 copy.112
  74.0 1.0 mul.126
  75.1 2.6 copy.98
  77.7 19.6 %all_gather.9 = bf16[256,1024]{1,0:T(8,128)(2,1)S(1)} all-gather(bf16[256,256]{1,0:T(8,128)(2,1)} %param.13), channel_id=1, replica_groups=mesh['req'=32,'exp'=4] {'exp'}, dimensions={1}, use_global_device_ids=true | all-gather | bytes 655360 | tf_op jit(solution)/shard_map/all_gather | solution.py:191
  97.3 0.2 fusion.18
  97.4 0.6 copy-done.2
  98.1 2.9 convolution_convert_fusion.1
  100.9 1.9 copy.99
  102.9 0.6 add_select_fusion
  103.4 0.6 compare_select_fusion
  104.0 2.6 scatter_custom_fusion
  106.6 1.8 fusion.44
  108.4 1.4 reduce-window.19
  109.8 1.7 copy.121
  111.5 1.7 copy.120
  113.1 1.7 copy.119
  114.8 1.2 clamp_bitcast_fusion.group_ref
  116.0 1.3 bitcast_subtract_fusion.start_ref
  117.3 39.6 %all-gather.2.cloned.1.call-done = bf16[4,2048,2,256]{3,1,2,0:T(8,128)(2,1)} async-done(((bf16[4,64,2,256]{3,1,2,0:T(8,128)(2,1)}), bf16[4,2048,2,256]{3,1,2,0:T(8,128)(2,1)}) %all-gather.2.cloned.1.call-update) | async-done | bytes 8388624 | tf_op jit(solution)/shard_map/all_gather | solution.py:210
  156.9 19.1 %shard_map.140 = bf16[256,256]{1,0:T(8,128)(2,1)} custom-call(s32[4]{0:T(128)} %clamp_bitcast_fusion.group_ref, s32[4]{0:T(128)} %bitcast_subtract_fusion.start_ref, s32[4]{0:T(128)} %bitcast.106, bf16[256,256]{1,0:T(8,128)(2,1)} %bitcast.101, bf16[256,256]{1,0:T(8,128)(2,1)} %bitcast.100, bf16[256,256]{1,0:T(8,128)(2,1)} %bitcast.99, ...), custom_call_target="tpu_custom_call" | custom-call | flops 9663676416 | bytes 8912896 | tf_op jit(solution)/shard_map/pallas_call | solution.py:129
  176.0 8.5 %all_gather.11 = bf16[256,1024]{1,0:T(8,128)(2,1)} all-gather(bf16[256,256]{1,0:T(8,128)(2,1)} %shard_map.140), channel_id=1, replica_groups=mesh['req'=32,'exp'=4] {'exp'}, dimensions={1}, use_global_device_ids=true | all-gather | bytes 655360 | tf_op jit(solution)/shard_map/all_gather | solution.py:215
  184.5 2.0 multiply_reduce_fusion
  186.5 1.0 copy-done.1
  187.6 0.2 multiply_convert_fusion
  187.7 0.8 copy-done.3
  188.6 2.8 gather_fusion.1
  191.4 0.4 broadcast_in_dim.76
  191.8 40.6 %all_to_all.25 = bf16[32,1,40,1024]{3,2,1,0:T(8,128)(2,1)S(1)} all-to-all(bf16[32,1,40,1024]{3,2,1,0:T(8,128)(2,1)S(1)} %bitcast.91), channel_id=1, replica_groups=mesh['req'=32,'exp'=4] {'req'}, dimensions={0} | all-to-all | bytes 5242880 | tf_op jit(solution)/shard_map/all_to_all | solution.py:241
  232.4 2.3 fusion.5
  234.7 3.3 %convert_bitcast_fusion = bf16[32,1,40,1024]{3,2,1,0:T(8,128)(2,1)} fusion(f32[32,1,40,2,352]{4,2,3,0,1:T(8,128)S(1)} %fusion.5, bf16[1,352,1024]{2,1,0:T(8,128)(2,1)S(1)} %copy-done.9), kind=kOutput, calls=%fused_computation.7 | convolution fusion | flops 928563200 | bytes 6946816 | tf_op jit(solution)/shard_map/slch,lhd->slcd/dot_general | solution.py:173
  238.0 5.4 %all-to-all-start.3 = ((bf16[32,1,40,1024]{3,2,1,0:T(8,128)(2,1)}), bf16[32,1,40,1024]{3,2,1,0:T(8,128)(2,1)}, u32[]{:S(2)}, u32[]{:S(2)}) async-start(bf16[32,1,40,1024]{3,2,1,0:T(8,128)(2,1)} %convert_bitcast_fusion), calls=%async_computation.3 | async-start | bytes 5242880 | tf_op jit(solution)/shard_map/all_to_all | solution.py:243
  243.4 0.1 copy.109
  243.6 0.1 reshape.245
  243.7 0.2 lt.57
  243.9 0.1 copy.111
  244.0 0.2 fusion.45
  244.3 4.6 %gather_fusion.2 = f32[512]{0:T(512)S(1)} fusion(f32[256,16]{0,1:T(8,128)S(1)} %fusion.45, s32[512]{0:T(512)S(1)} %reshape.245), kind=kCustom, calls=%fused_computation.2 | custom fusion | bytes 8192 | tf_op jit(solution)/shard_map/jit(take_along_axis)/gather | solution.py:230
  248.8 0.1 reshape.248
  249.0 0.1 copy.110
  249.1 0.7 select_reduce_fusion
  249.8 27.4 %all-to-all-done.3 = bf16[32,1,40,1024]{3,2,1,0:T(8,128)(2,1)} async-done(((bf16[32,1,40,1024]{3,2,1,0:T(8,128)(2,1)}), bf16[32,1,40,1024]{3,2,1,0:T(8,128)(2,1)}, u32[]{:S(2)}, u32[]{:S(2)}) %all-to-all-start.3) | async-done | bytes 2621472 | tf_op jit(solution)/shard_map/all_to_all | solution.py:243
  277.2 4.0 %convolution_convert_fusion = bf16[256,1024]{1,0:T(8,128)(2,1)S(1)} fusion(f32[256,1280]{1,0:T(8,128)S(1)} %select_reduce_fusion, bf16[1280,1024]{1,0:T(8,128)(2,1)} %bitcast.35), kind=kOutput, calls=%fused_computation.27 | convolution fusion | flops 4026793984 | bytes 4456448 | tf_op jit(solution)/shard_map/dot_general | solution.py:253
  281.2 0.8 copy.126
  282.0 5.7 %all-to-all-start.4 = ((bf16[4,256,256]{2,1,0:T(8,128)(2,1)}), bf16[4,256,256]{2,1,0:T(8,128)(2,1)S(1)}, u32[]{:S(2)}, u32[]{:S(2)}) async-start(bf16[4,256,256]{2,1,0:T(8,128)(2,1)} %bitcast.89), calls=%async_computation.4 | async-start | bytes 1048576 | tf_op jit(solution)/shard_map/all_to_all | solution.py:263
  287.7 0.9 copy.115
  288.6 7.0 %all-to-all-done.4 = bf16[4,256,256]{2,1,0:T(8,128)(2,1)S(1)} async-done(((bf16[4,256,256]{2,1,0:T(8,128)(2,1)}), bf16[4,256,256]{2,1,0:T(8,128)(2,1)S(1)}, u32[]{:S(2)}, u32[]{:S(2)}) %all-to-all-start.4) | async-done | bytes 524320 | tf_op jit(solution)/shard_map/all_to_all | solution.py:263
  295.6 1.7 add_convert_fusion
  (38 shorter events, 0.3 us)
Async XLA Ops:
  7.2 225.2 %copy-start = (bf16[1,1024,2,352]{1,3,2,0:T(8,128)(2,1)S(1)}, bf16[1,1024,2,352]{1,3,2,0:T(8,128)(2,1)}, u32[]{:S(2)}) copy-start(bf16[1,1024,2,352]{1,3,2,0:T(8,128)(2,1)} %param.24) | copy-start | bytes 4325380
  10.7 11.5 %copy-start.10 = (s32[4]{0:T(128)S(1)}, s32[4]{0:T(128)}, u32[]{:S(2)}) copy-start(s32[4]{0:T(128)} %param.16) | copy-start | bytes 52
  10.7 39.4 %all-to-all-start = ((bf16[32,64,2,256]{3,1,2,0:T(8,128)(2,1)}), bf16[32,64,2,256]{3,1,2,0:T(8,128)(2,1)S(1)}, u32[]{:S(2)}, u32[]{:S(2)}) async-start(bf16[32,64,2,256]{3,1,2,0:T(8,128)(2,1)} %copy.104), calls=%async_computation | async-start | bytes 4194304 | tf_op jit(solution)/shard_map/all_to_all | solution.py:208
  22.1 134.8 %all-gather.2.cloned.1.call-start = ((), (), s32[]{:S(2)}) async-start(), calls=%async_computation.5 | async-start | bytes 8650752 | tf_op jit(solution)/shard_map/all_gather | solution.py:210
  55.8 5.9 %copy-start.6 = (s32[256,2]{0,1:T(2,128)S(1)}, s32[256,2]{0,1:T(2,128)}, u32[]{:S(2)}) copy-start(s32[256,2]{0,1:T(2,128)} %param.23) | copy-start | bytes 6148
  55.8 128.7 %all-to-all-start.1 = ((bf16[4,256,1024]{2,1,0:T(8,128)(2,1)}), bf16[4,256,1024]{2,1,0:T(8,128)(2,1)S(1)}, u32[]{:S(2)}, u32[]{:S(2)}) async-start(bf16[4,256,1024]{2,1,0:T(8,128)(2,1)} %broadcast_in_dim.67), calls=%async_computation.1 | async-start | bytes 4194304 | tf_op jit(solution)/shard_map/all_to_all | solution.py:217
  97.3 0.8 copy-start.2
  184.5 3.0 %copy-start.8 = (f32[1024]{0:T(1024)S(1)}, f32[1024]{0:T(1024)}, u32[]{:S(2)}) copy-start(f32[1024]{0:T(1024)} %param.21) | copy-start | bytes 12292
  186.5 1.0 copy-start.1
  187.7 0.8 copy-start.3
  232.4 2.3 copy-start.9
  238.0 6.0 %copy-start.4 = (bf16[256,1024]{1,0:T(8,128)(2,1)S(1)}, bf16[256,1024]{1,0:T(8,128)(2,1)}, u32[]{:S(2)}) copy-start(bf16[256,1024]{1,0:T(8,128)(2,1)} %copy-done.3) | copy-start | bytes 1572868
  238.0 6.0 %copy-start.7 = (bf16[1024,16]{0,1:T(8,128)(2,1)S(1)}, bf16[1024,16]{0,1:T(8,128)(2,1)}, u32[]{:S(2)}) copy-start(bf16[1024,16]{0,1:T(8,128)(2,1)} %param.22) | copy-start | bytes 98308
  238.0 39.2 %all-to-all-start.3 = ((bf16[32,1,40,1024]{3,2,1,0:T(8,128)(2,1)}), bf16[32,1,40,1024]{3,2,1,0:T(8,128)(2,1)}, u32[]{:S(2)}, u32[]{:S(2)}) async-start(bf16[32,1,40,1024]{3,2,1,0:T(8,128)(2,1)} %convert_bitcast_fusion), calls=%async_computation.3 | async-start | bytes 5242880 | tf_op jit(solution)/shard_map/all_to_all | solution.py:243
  281.2 6.5 %copy-start.5 = (bf16[256,768]{0,1:T(8,128)(2,1)S(1)}, bf16[256,768]{0,1:T(8,128)(2,1)}, u32[]{:S(2)}) copy-start(bf16[256,768]{0,1:T(8,128)(2,1)} %copy.99) | copy-start | bytes 1179652
  282.0 13.5 %all-to-all-start.4 = ((bf16[4,256,256]{2,1,0:T(8,128)(2,1)}), bf16[4,256,256]{2,1,0:T(8,128)(2,1)S(1)}, u32[]{:S(2)}, u32[]{:S(2)}) async-start(bf16[4,256,256]{2,1,0:T(8,128)(2,1)} %bitcast.89), calls=%async_computation.4 | async-start | bytes 1048576 | tf_op jit(solution)/shard_map/all_to_all | solution.py:263
Sparse Core Ops, SparseCore 0:
  53.2 103.6 all-gather.1

commit v7 on v6

--- a/solution.py
+++ b/solution.py
@@ -16,6 +16,7 @@
 REQ_DEV = 4
 SUF_MOST = 128
 CAP = 40
+WINDOW = SUF_MOST + 16
 
 
 epsilon = 1e-06
@@ -70,14 +71,16 @@
 
     start = start_ref[request]
     stop = start + length_ref[request]
-    rows, width = query_ref.shape
-    row_ids = lax.broadcasted_iota(jnp.int32, (rows, rows), 0)
-    col_ids = lax.broadcasted_iota(jnp.int32, (rows, rows), 1)
+    total_rows, width = query_ref.shape
+    rows = WINDOW
+    first = pl.multiple_of(jnp.minimum((start // 16) * 16, total_rows - rows), 16)
+    row_ids = first + lax.broadcasted_iota(jnp.int32, (rows, rows), 0)
+    col_ids = first + lax.broadcasted_iota(jnp.int32, (rows, rows), 1)
     suffix_ok = (col_ids <= row_ids) & (col_ids >= start)
     lane_head = lax.broadcasted_iota(jnp.int32, (1, width), 1) // HEAD_DIM
-    query = query_ref[...]
-    keys = key_ref[...]
-    values = value_ref[...]
+    query = query_ref[pl.ds(first, rows), :]
+    keys = key_ref[pl.ds(first, rows), :]
+    values = value_ref[pl.ds(first, rows), :]
     prefix_keys = prefix_ref[0, 0]
     prefix_values = prefix_ref[0, 1]
     scale = 1.0 / math.sqrt(HEAD_DIM)
@@ -105,9 +108,11 @@
             weight_pre.astype(jnp.bfloat16), prefix_values, preferred_element_type=jnp.float32
         ) + jnp.dot(weight_suf.astype(jnp.bfloat16), values, preferred_element_type=jnp.float32)
         context = context + jnp.where(in_head, mixed / totals, 0.0)
-    row_in = lax.broadcasted_iota(jnp.int32, (rows, 1), 0)
+    row_in = first + lax.broadcasted_iota(jnp.int32, (rows, 1), 0)
     inside = (row_in >= start) & (row_in < stop)
-    out_ref[...] = jnp.where(inside, context.astype(out_ref.dtype), out_ref[...])
+    out_ref[pl.ds(first, rows), :] = jnp.where(
+        inside, context.astype(out_ref.dtype), out_ref[pl.ds(first, rows), :]
+    )
 
 
 def attention(query, keys, values, prefix, block_groups, starts, block_lengths, interpret=False):
@@ -125,7 +130,7 @@
         ],
         out_specs=pl.BlockSpec((rows, width), full),
     )
-    flops = 4 * 2 * 2 * rows * (PREFIX + rows) * width * block_groups.shape[0]
+    flops = 4 * 2 * 2 * WINDOW * (PREFIX + WINDOW) * width * block_groups.shape[0]
     return pl.pallas_call(
         attention_kernel,
         grid_spec=grid_spec,
@@ -134,7 +139,7 @@
         interpret=interpret,
         cost_estimate=pl.CostEstimate(
             flops=flops,
-            transcendentals=4 * rows * (PREFIX + rows) * block_groups.shape[0],
+            transcendentals=4 * WINDOW * (PREFIX + WINDOW) * block_groups.shape[0],
             bytes_accessed=slots * 2 * PREFIX * width * 2 + 4 * rows * width * 2,
         ),
     )(

time: 305 us -> 303 us (level)
    unnamed x28 -> x30, local copies, waits for them, and re-layouts: 11.7 us -> 11.7 us
where the time goes in v7:
time: 303 us; the launch traced here: 302 us
  waiting for transfers between devices  103 us (34%)
  blocking collectives  67.9 us (22%)
  local copies, waits for them, and re-layouts  42.2 us (14%)
  starting transfers between devices  28.5 us (9%)
  Pallas kernels  16.8 us (6%)
  matrix products  14.7 us (5%)
  between operations  14.3 us (5%)
  other arithmetic  14.2 us (5%)
    all_gather x1, waiting for transfers between devices, shards(): cached = lax.all_gather(owned, 'req', axis=1, tiled=True)  41.1 us
    all_to_all x1, blocking collectives, shards(): lax.all_to_all(outgoing_rows, 'req', split_axis=0, concat_axis=0, tiled=T...  40.6 us
    all_to_all x1, waiting for transfers between devices, shards(): lax.all_to_all(pieces, 'req', split_axis=0, concat_axis=0, tiled=True)  27.8 us
    all_to_all x1, waiting for transfers between devices, shards(): lax.all_to_all(partial_out.astype(jnp.bfloat16), 'req', split_axis=0, con...  27.4 us
    all_gather x1, blocking collectives, shards(): rows_whole = lax.all_gather(tokens, 'exp', axis=1, tiled=True)  18.8 us
    pallas_call x1, Pallas kernels, attention(): pl.pallas_call(attention_kernel, grid_spec=grid_spec, out_shape=jax.Shape...  16.8 us
    unnamed x30, local copies, waits for them, and re-layouts  11.7 us
    all_to_all x1, starting transfers between devices, shards(): lax.all_to_all(pieces, 'req', split_axis=0, concat_axis=0, tiled=True)  11.5 us
  transfers between devices with their start and end apart: 5, of which 4 were waited for; matrix products, arithmetic and copies ran while one was open for 15% of the time, Pallas kernels for 6%

profile of v7, /device:TPU:1, one launch (start us, length us, event | category | flops | bytes accessed | tf_op | source)
XLA Modules:
  0.0 301.8 jit_solution(6335340072466990874)
XLA Ops:
  7.2 3.5 %copy.104 = bf16[32,64,2,256]{3,1,2,0:T(8,128)(2,1)} copy(bf16[32,64,2,256]{3,2,1,0:T(2,128)(2,1)} %bitcast.96) | data formatting | bytes 4194304 | tf_op jit(solution)/shard_map/reshape;squeeze | solution.py:212
  10.7 11.5 %all-to-all-start = ((bf16[32,64,2,256]{3,1,2,0:T(8,128)(2,1)}), bf16[32,64,2,256]{3,1,2,0:T(8,128)(2,1)S(1)}, u32[]{:S(2)}, u32[]{:S(2)}) async-start(bf16[32,64,2,256]{3,1,2,0:T(8,128)(2,1)} %copy.104), calls=%async_computation | async-start | bytes 4194304 | tf_op jit(solution)/shard_map/all_to_all | solution.py:213
  22.2 27.8 %all-to-all-done = bf16[32,64,2,256]{3,1,2,0:T(8,128)(2,1)S(1)} async-done(((bf16[32,64,2,256]{3,1,2,0:T(8,128)(2,1)}), bf16[32,64,2,256]{3,1,2,0:T(8,128)(2,1)S(1)}, u32[]{:S(2)}, u32[]{:S(2)}) %all-to-all-start) | async-done | bytes 2097184 | tf_op jit(solution)/shard_map/all_to_all | solution.py:213
  50.1 1.3 gather_fusion
  51.3 1.7 broadcast_select_fusion
  53.1 2.7 broadcast_in_dim.67
  55.8 5.9 %all-to-all-start.1 = ((bf16[4,256,1024]{2,1,0:T(8,128)(2,1)}), bf16[4,256,1024]{2,1,0:T(8,128)(2,1)S(1)}, u32[]{:S(2)}, u32[]{:S(2)}) async-start(bf16[4,256,1024]{2,1,0:T(8,128)(2,1)} %broadcast_in_dim.67), calls=%async_computation.1 | async-start | bytes 4194304 | tf_op jit(solution)/shard_map/all_to_all | solution.py:222
  61.7 0.8 copy.105
  62.5 1.0 eq.43
  63.5 1.0 eq.39
  64.6 0.7 reduce-window.19
  65.3 0.6 fusion.33
  66.0 3.1 %reduce-window.20 = s32[16,4,128]{2,0,1:T(8,128)} reduce-window(s32[16,4,128]{2,0,1:T(8,128)} %fusion.33, s32[]{:T(128)} %constant.31.clone.1), window={size=1x1x128 pad=0_0x0_0x127_0}, to_apply=%region_2.3 | reduce-window | flops 1040384 | bytes 65540 | tf_op jit(solution)/shard_map/reduce-window.1
  69.1 1.0 slice_reduce_fusion
  70.1 0.9 fusion.32
  71.0 0.8 min.28
  71.8 1.0 copy.108
  72.7 0.6 broadcast_multiply_fusion
  73.3 1.5 copy.112
  74.8 1.0 mul.126
  75.8 2.6 copy.98
  78.4 18.8 %all_gather.9 = bf16[256,1024]{1,0:T(8,128)(2,1)S(1)} all-gather(bf16[256,256]{1,0:T(8,128)(2,1)} %param.13), channel_id=1, replica_groups=mesh['req'=32,'exp'=4] {'exp'}, dimensions={1}, use_global_device_ids=true | all-gather | bytes 655360 | tf_op jit(solution)/shard_map/all_gather | solution.py:196
  97.2 0.2 fusion.18
  97.4 0.6 copy-done.2
  98.1 2.9 convolution_convert_fusion.1
  100.9 1.9 copy.99
  102.8 1.8 fusion.44
  104.6 1.7 copy.121
  106.3 1.7 copy.120
  107.9 1.7 copy.119
  109.6 0.6 compare_select_fusion
  110.2 0.6 add_select_fusion
  110.8 2.6 scatter_custom_fusion
  113.4 1.2 clamp_bitcast_fusion.group_ref
  114.6 1.2 bitcast_subtract_fusion.start_ref
  115.9 41.1 %all-gather.2.cloned.1.call-done = bf16[4,2048,2,256]{3,1,2,0:T(8,128)(2,1)} async-done(((bf16[4,64,2,256]{3,1,2,0:T(8,128)(2,1)}), bf16[4,2048,2,256]{3,1,2,0:T(8,128)(2,1)}) %all-gather.2.cloned.1.call-update) | async-done | bytes 8388624 | tf_op jit(solution)/shard_map/all_gather | solution.py:215
  156.9 16.8 %shard_map.140 = bf16[256,256]{1,0:T(8,128)(2,1)} custom-call(s32[4]{0:T(128)} %clamp_bitcast_fusion.group_ref, s32[4]{0:T(128)} %bitcast_subtract_fusion.start_ref, s32[4]{0:T(128)} %bitcast.105, bf16[256,256]{1,0:T(8,128)(2,1)} %bitcast.101, bf16[256,256]{1,0:T(8,128)(2,1)} %bitcast.100, bf16[256,256]{1,0:T(8,128)(2,1)} %bitcast.99, ...), custom_call_target="tpu_custom_call" | custom-call | flops 5171576832 | bytes 8912896 | tf_op jit(solution)/shard_map/pallas_call | solution.py:134
  173.7 8.5 %all_gather.11 = bf16[256,1024]{1,0:T(8,128)(2,1)} all-gather(bf16[256,256]{1,0:T(8,128)(2,1)} %shard_map.140), channel_id=1, replica_groups=mesh['req'=32,'exp'=4] {'exp'}, dimensions={1}, use_global_device_ids=true | all-gather | bytes 655360 | tf_op jit(solution)/shard_map/all_gather | solution.py:220
  182.2 2.0 multiply_reduce_fusion
  184.2 1.0 copy-done.1
  185.2 0.2 multiply_convert_fusion
  185.4 0.8 copy-done.3
  186.2 2.8 gather_fusion.1
  189.1 0.4 broadcast_in_dim.76
  189.5 40.6 %all_to_all.25 = bf16[32,1,40,1024]{3,2,1,0:T(8,128)(2,1)S(1)} all-to-all(bf16[32,1,40,1024]{3,2,1,0:T(8,128)(2,1)S(1)} %bitcast.91), channel_id=1, replica_groups=mesh['req'=32,'exp'=4] {'req'}, dimensions={0} | all-to-all | bytes 5242880 | tf_op jit(solution)/shard_map/all_to_all | solution.py:246
  230.1 2.3 fusion.5
  232.4 3.3 %convert_bitcast_fusion = bf16[32,1,40,1024]{3,2,1,0:T(8,128)(2,1)} fusion(f32[32,1,40,2,352]{4,2,3,0,1:T(8,128)S(1)} %fusion.5, bf16[1,352,1024]{2,1,0:T(8,128)(2,1)S(1)} %copy-done.9), kind=kOutput, calls=%fused_computation.7 | convolution fusion | flops 928563200 | bytes 6946816 | tf_op jit(solution)/shard_map/slch,lhd->slcd/dot_general | solution.py:178
  235.7 5.4 %all-to-all-start.3 = ((bf16[32,1,40,1024]{3,2,1,0:T(8,128)(2,1)}), bf16[32,1,40,1024]{3,2,1,0:T(8,128)(2,1)}, u32[]{:S(2)}, u32[]{:S(2)}) async-start(bf16[32,1,40,1024]{3,2,1,0:T(8,128)(2,1)} %convert_bitcast_fusion), calls=%async_computation.3 | async-start | bytes 5242880 | tf_op jit(solution)/shard_map/all_to_all | solution.py:248
  241.1 0.1 copy.109
  241.3 0.1 reshape.245
  241.4 0.2 lt.57
  241.6 0.1 copy.111
  241.7 0.2 fusion.45
  242.0 4.6 %gather_fusion.2 = f32[512]{0:T(512)S(1)} fusion(f32[256,16]{0,1:T(8,128)S(1)} %fusion.45, s32[512]{0:T(512)S(1)} %reshape.245), kind=kCustom, calls=%fused_computation.2 | custom fusion | bytes 8192 | tf_op jit(solution)/shard_map/jit(take_along_axis)/gather | solution.py:235
  246.5 0.1 reshape.248
  246.7 0.1 copy.110
  246.8 0.7 select_reduce_fusion
  247.5 27.4 %all-to-all-done.3 = bf16[32,1,40,1024]{3,2,1,0:T(8,128)(2,1)} async-done(((bf16[32,1,40,1024]{3,2,1,0:T(8,128)(2,1)}), bf16[32,1,40,1024]{3,2,1,0:T(8,128)(2,1)}, u32[]{:S(2)}, u32[]{:S(2)}) %all-to-all-start.3) | async-done | bytes 2621472 | tf_op jit(solution)/shard_map/all_to_all | solution.py:248
  274.9 4.0 %convolution_convert_fusion = bf16[256,1024]{1,0:T(8,128)(2,1)S(1)} fusion(f32[256,1280]{1,0:T(8,128)S(1)} %select_reduce_fusion, bf16[1280,1024]{1,0:T(8,128)(2,1)} %bitcast.35), kind=kOutput, calls=%fused_computation.27 | convolution fusion | flops 4026793984 | bytes 4456448 | tf_op jit(solution)/shard_map/dot_general | solution.py:258
  278.9 0.8 copy.126
  279.7 5.7 %all-to-all-start.4 = ((bf16[4,256,256]{2,1,0:T(8,128)(2,1)}), bf16[4,256,256]{2,1,0:T(8,128)(2,1)S(1)}, u32[]{:S(2)}, u32[]{:S(2)}) async-start(bf16[4,256,256]{2,1,0:T(8,128)(2,1)} %bitcast.89), calls=%async_computation.4 | async-start | bytes 1048576 | tf_op jit(solution)/shard_map/all_to_all | solution.py:268
  285.4 0.9 copy.115
  286.3 7.0 %all-to-all-done.4 = bf16[4,256,256]{2,1,0:T(8,128)(2,1)S(1)} async-done(((bf16[4,256,256]{2,1,0:T(8,128)(2,1)}), bf16[4,256,256]{2,1,0:T(8,128)(2,1)S(1)}, u32[]{:S(2)}, u32[]{:S(2)}) %all-to-all-start.4) | async-done | bytes 524320 | tf_op jit(solution)/shard_map/all_to_all | solution.py:268
  293.3 1.7 add_convert_fusion
  (40 shorter events, 0.3 us)
Async XLA Ops:
  7.2 222.9 %copy-start = (bf16[1,1024,2,352]{1,3,2,0:T(8,128)(2,1)S(1)}, bf16[1,1024,2,352]{1,3,2,0:T(8,128)(2,1)}, u32[]{:S(2)}) copy-start(bf16[1,1024,2,352]{1,3,2,0:T(8,128)(2,1)} %param.24) | copy-start | bytes 4325380
  10.7 11.5 %copy-start.10 = (s32[4]{0:T(128)S(1)}, s32[4]{0:T(128)}, u32[]{:S(2)}) copy-start(s32[4]{0:T(128)} %param.16) | copy-start | bytes 52
  10.7 39.4 %all-to-all-start = ((bf16[32,64,2,256]{3,1,2,0:T(8,128)(2,1)}), bf16[32,64,2,256]{3,1,2,0:T(8,128)(2,1)S(1)}, u32[]{:S(2)}, u32[]{:S(2)}) async-start(bf16[32,64,2,256]{3,1,2,0:T(8,128)(2,1)} %copy.104), calls=%async_computation | async-start | bytes 4194304 | tf_op jit(solution)/shard_map/all_to_all | solution.py:213
  22.1 134.8 %all-gather.2.cloned.1.call-start = ((), (), s32[]{:S(2)}) async-start(), calls=%async_computation.5 | async-start | bytes 8650752 | tf_op jit(solution)/shard_map/all_gather | solution.py:215
  55.8 5.9 %copy-start.6 = (s32[256,2]{0,1:T(2,128)S(1)}, s32[256,2]{0,1:T(2,128)}, u32[]{:S(2)}) copy-start(s32[256,2]{0,1:T(2,128)} %param.23) | copy-start | bytes 6148
  55.8 8.8 %copy-start.11 = (s32[1,4]{1,0:T(1,128)S(1)}, s32[1,4]{1,0:T(1,128)}, u32[]{:S(2)}) copy-start(s32[1,4]{1,0:T(1,128)} %param.14) | copy-start | bytes 52
  55.8 126.4 %all-to-all-start.1 = ((bf16[4,256,1024]{2,1,0:T(8,128)(2,1)}), bf16[4,256,1024]{2,1,0:T(8,128)(2,1)S(1)}, u32[]{:S(2)}, u32[]{:S(2)}) async-start(bf16[4,256,1024]{2,1,0:T(8,128)(2,1)} %broadcast_in_dim.67), calls=%async_computation.1 | async-start | bytes 4194304 | tf_op jit(solution)/shard_map/all_to_all | solution.py:222
  97.2 0.8 copy-start.2
  182.2 3.0 %copy-start.8 = (f32[1024]{0:T(1024)S(1)}, f32[1024]{0:T(1024)}, u32[]{:S(2)}) copy-start(f32[1024]{0:T(1024)} %param.21) | copy-start | bytes 12292
  184.2 1.0 copy-start.1
  185.4 0.8 copy-start.3
  230.1 2.3 copy-start.9
  235.7 6.0 %copy-start.4 = (bf16[256,1024]{1,0:T(8,128)(2,1)S(1)}, bf16[256,1024]{1,0:T(8,128)(2,1)}, u32[]{:S(2)}) copy-start(bf16[256,1024]{1,0:T(8,128)(2,1)} %copy-done.3) | copy-start | bytes 1572868
  235.7 6.0 %copy-start.7 = (bf16[1024,16]{0,1:T(8,128)(2,1)S(1)}, bf16[1024,16]{0,1:T(8,128)(2,1)}, u32[]{:S(2)}) copy-start(bf16[1024,16]{0,1:T(8,128)(2,1)} %param.22) | copy-start | bytes 98308
  235.7 39.2 %all-to-all-start.3 = ((bf16[32,1,40,1024]{3,2,1,0:T(8,128)(2,1)}), bf16[32,1,40,1024]{3,2,1,0:T(8,128)(2,1)}, u32[]{:S(2)}, u32[]{:S(2)}) async-start(bf16[32,1,40,1024]{3,2,1,0:T(8,128)(2,1)} %convert_bitcast_fusion), calls=%async_computation.3 | async-start | bytes 5242880 | tf_op jit(solution)/shard_map/all_to_all | solution.py:248
  278.8 6.5 %copy-start.5 = (bf16[256,768]{0,1:T(8,128)(2,1)S(1)}, bf16[256,768]{0,1:T(8,128)(2,1)}, u32[]{:S(2)}) copy-start(bf16[256,768]{0,1:T(8,128)(2,1)} %copy.99) | copy-start | bytes 1179652
  279.7 13.6 %all-to-all-start.4 = ((bf16[4,256,256]{2,1,0:T(8,128)(2,1)}), bf16[4,256,256]{2,1,0:T(8,128)(2,1)S(1)}, u32[]{:S(2)}, u32[]{:S(2)}) async-start(bf16[4,256,256]{2,1,0:T(8,128)(2,1)} %bitcast.89), calls=%async_computation.4 | async-start | bytes 1048576 | tf_op jit(solution)/shard_map/all_to_all | solution.py:268
Sparse Core Ops, SparseCore 0:
  53.2 103.6 all-gather.1

commit v8 on v7

--- a/solution.py
+++ b/solution.py
@@ -61,7 +61,7 @@
 
 
 def attention_kernel(
-    group_ref, start_ref, length_ref, query_ref, key_ref, value_ref, prefix_ref, out_ref
+    group_ref, start_ref, length_ref, query_ref, key_ref, value_ref, prefix_ref, last_ref, out_ref
 ):
     request = pl.program_id(0)
 
@@ -81,8 +81,9 @@
     query = query_ref[pl.ds(first, rows), :]
     keys = key_ref[pl.ds(first, rows), :]
     values = value_ref[pl.ds(first, rows), :]
-    prefix_keys = prefix_ref[0, 0]
-    prefix_values = prefix_ref[0, 1]
+    is_last = group_ref[request] == GROUPS - 1
+    prefix_keys = jnp.where(is_last, last_ref[0, 0], prefix_ref[0, 0])
+    prefix_values = jnp.where(is_last, last_ref[0, 1], prefix_ref[0, 1])
     scale = 1.0 / math.sqrt(HEAD_DIM)
     contract = (((1,), (1,)), ((), ()))
     context = jnp.zeros((rows, width), jnp.float32)
@@ -117,6 +118,7 @@
 
 def attention(query, keys, values, prefix, block_groups, starts, block_lengths, interpret=False):
     rows, width = query.shape
+    prefix, last = prefix
     slots = prefix.shape[0]
     full = lambda i, g, s, n: (0, 0)
     grid_spec = pltpu.PrefetchScalarGridSpec(
@@ -126,7 +128,10 @@
             pl.BlockSpec((rows, width), full),
             pl.BlockSpec((rows, width), full),
             pl.BlockSpec((rows, width), full),
-            pl.BlockSpec((1, 2, PREFIX, width), lambda i, g, s, n: (g[i], 0, 0, 0)),
+            pl.BlockSpec(
+                (1, 2, PREFIX, width), lambda i, g, s, n: (jnp.minimum(g[i], GROUPS - 2), 0, 0, 0)
+            ),
+            pl.BlockSpec((1, 2, PREFIX, width), lambda i, g, s, n: (0, 0, 0, 0)),
         ],
         out_specs=pl.BlockSpec((rows, width), full),
     )
@@ -143,13 +148,14 @@
             bytes_accessed=slots * 2 * PREFIX * width * 2 + 4 * rows * width * 2,
         ),
     )(
-        jnp.clip(block_groups, 0, slots - 1),
+        jnp.clip(block_groups, 0, GROUPS - 1),
         starts,
         block_lengths,
         query,
         keys,
         values,
         prefix,
+        last,
     )
 
 
@@ -212,10 +218,19 @@
     pieces = own_slot.reshape(req_total, PREFIX // req_total, 2, quarter)
     pieces = lax.all_to_all(pieces, "req", split_axis=0, concat_axis=0, tiled=True)
     owned = jnp.take(pieces, owners, axis=0)
-    cached = lax.all_gather(owned, "req", axis=1, tiled=True)
+    cached = lax.all_gather(owned[: GROUPS - 1], "req", axis=1, tiled=True)
     cached = jnp.transpose(cached, (0, 2, 1, 3))
+    last_piece = jnp.transpose(owned[GROUPS - 1], (1, 0, 2))
+    last = lax.all_to_all(
+        jnp.broadcast_to(last_piece[None], (req_total,) + last_piece.shape),
+        "req",
+        split_axis=0,
+        concat_axis=0,
+        tiled=True,
+    )
+    last = jnp.transpose(last, (1, 0, 2, 3)).reshape(1, 2, PREFIX, quarter)
     context = attention(
-        qkv[:, 0], qkv[:, 1], qkv[:, 2], cached, block_groups, starts, block_lengths
+        qkv[:, 0], qkv[:, 1], qkv[:, 2], (cached, last), block_groups, starts, block_lengths
     )
     context_full = lax.all_gather(context, "exp", axis=1, tiled=True)
     exp_total = lax.axis_size("exp")

time: 303 us -> 327 us (1.079)
  blocking collectives: 67.9 us -> 79.7 us
  local copies, waits for them, and re-layouts: 42.2 us -> 47.5 us
  starting transfers between devices: 28.5 us -> 33.4 us
    all_gather x1, blocking collectives: 18.8 us -> 29.1 us  [shards(): rows_whole = lax.all_gather(tokens, 'exp', axis=1, tiled=True)]
    all_to_all x0 -> x1, starting transfers between devices: none -> 7.06 us  [shards(): lax.all_to_all(jnp.broadcast_to(last_piece[None], (req_total,) + last_pie...]
    unnamed x30 -> x32, local copies, waits for them, and re-layouts: 11.7 us -> 11.1 us
  transfers between devices with their start and end apart: 5 -> 6, of which waited for: 4 -> 4; matrix products, arithmetic and copies ran while one was open for 15% -> 16% of each run, Pallas kernels for 6% -> 5%
where the time goes in v8:
time: 327 us; the launch traced here: 326 us
  waiting for transfers between devices  104 us (32%)
  blocking collectives  79.7 us (24%)
  local copies, waits for them, and re-layouts  47.5 us (15%)
  starting transfers between devices  33.4 us (10%)
  Pallas kernels  17.5 us (5%)
  matrix products  14.8 us (5%)
  other arithmetic  14.4 us (4%)
  between operations  14.3 us (4%)
    all_gather x1, waiting for transfers between devices, shards(): cached = lax.all_gather(owned[:GROUPS - 1], 'req', axis=1, tiled=True)  41.7 us
    all_to_all x1, blocking collectives, shards(): lax.all_to_all(outgoing_rows, 'req', split_axis=0, concat_axis=0, tiled=T...  41.4 us
    all_gather x1, blocking collectives, shards(): rows_whole = lax.all_gather(tokens, 'exp', axis=1, tiled=True)  29.1 us
    all_to_all x1, waiting for transfers between devices, shards(): lax.all_to_all(pieces, 'req', split_axis=0, concat_axis=0, tiled=True)  27.8 us
    all_to_all x1, waiting for transfers between devices, shards(): lax.all_to_all(partial_out.astype(jnp.bfloat16), 'req', split_axis=0, con...  27.4 us
    pallas_call x1, Pallas kernels, attention(): pl.pallas_call(attention_kernel, grid_spec=grid_spec, out_shape=jax.Shape...  17.5 us
    all_to_all x1, starting transfers between devices, shards(): lax.all_to_all(pieces, 'req', split_axis=0, concat_axis=0, tiled=True)  11.5 us
    unnamed x32, local copies, waits for them, and re-layouts  11.1 us
  transfers between devices with their start and end apart: 6, of which 4 were waited for; matrix products, arithmetic and copies ran while one was open for 16% of the time, Pallas kernels for 5%

profile of v8, /device:TPU:1, one launch (start us, length us, event | category | flops | bytes accessed | tf_op | source)
XLA Modules:
  0.0 325.5 jit_solution(4600184382709326878)
XLA Ops:
  7.2 3.5 %copy.106 = bf16[32,64,2,256]{3,1,2,0:T(8,128)(2,1)} copy(bf16[32,64,2,256]{3,2,1,0:T(2,128)(2,1)} %bitcast.102) | data formatting | bytes 4194304 | tf_op jit(solution)/shard_map/reshape;squeeze | solution.py:218
  10.7 11.5 %all-to-all-start = ((bf16[32,64,2,256]{3,1,2,0:T(8,128)(2,1)}), bf16[32,64,2,256]{3,1,2,0:T(8,128)(2,1)S(1)}, u32[]{:S(2)}, u32[]{:S(2)}) async-start(bf16[32,64,2,256]{3,1,2,0:T(8,128)(2,1)} %copy.106), calls=%async_computation | async-start | bytes 4194304 | tf_op jit(solution)/shard_map/all_to_all | solution.py:219
  22.2 27.8 %all-to-all-done = bf16[32,64,2,256]{3,1,2,0:T(8,128)(2,1)S(1)} async-done(((bf16[32,64,2,256]{3,1,2,0:T(8,128)(2,1)}), bf16[32,64,2,256]{3,1,2,0:T(8,128)(2,1)S(1)}, u32[]{:S(2)}, u32[]{:S(2)}) %all-to-all-start) | async-done | bytes 2097184 | tf_op jit(solution)/shard_map/all_to_all | solution.py:219
  50.1 1.3 gather_fusion
  51.3 1.0 broadcast_select_fusion
  52.4 0.7 slice.48
  53.1 1.6 broadcast_in_dim.73
  54.7 7.1 %all-to-all-start.1 = ((bf16[32,2,64,256]{3,2,1,0:T(8,128)(2,1)}), bf16[32,2,64,256]{3,2,1,0:T(8,128)(2,1)S(1)}, u32[]{:S(2)}, u32[]{:S(2)}) async-start(bf16[32,2,64,256]{3,2,1,0:T(8,128)(2,1)} %broadcast_in_dim.73), calls=%async_computation.1 | async-start | bytes 4194304 | tf_op jit(solution)/shard_map/all_to_all | solution.py:224
  61.8 29.1 %all_gather.9 = bf16[256,1024]{1,0:T(8,128)(2,1)} all-gather(bf16[256,256]{1,0:T(8,128)(2,1)} %param.13), channel_id=1, replica_groups=mesh['req'=32,'exp'=4] {'exp'}, dimensions={1}, use_global_device_ids=true | all-gather | bytes 655360 | tf_op jit(solution)/shard_map/all_gather | solution.py:202
  90.9 0.8 copy.108
  91.7 1.0 eq.43
  92.7 1.0 eq.39
  93.8 2.6 copy.100
  96.4 1.2 fusion.18
  97.7 3.0 convolution_convert_fusion.1
  100.6 2.0 copy.101
  102.6 1.9 fusion.44
  104.5 1.7 copy.122
  106.1 1.7 copy.123
  107.8 1.7 copy.124
  109.5 0.7 reduce-window.19
  110.2 0.6 fusion.33
  110.8 3.1 reduce-window.20
  114.0 1.0 slice_reduce_fusion
  115.0 0.9 fusion.32
  115.8 0.8 min.28
  116.6 1.0 copy.111
  117.6 0.6 broadcast_multiply_fusion
  118.2 1.5 copy.115
  119.7 1.0 mul.126
  120.7 0.6 compare_select_fusion
  121.3 3.0 broadcast_in_dim.74
  124.3 3.8 %all-to-all-start.2 = ((bf16[4,256,1024]{2,1,0:T(8,128)(2,1)}), bf16[4,256,1024]{2,1,0:T(8,128)(2,1)S(1)}, u32[]{:S(2)}, u32[]{:S(2)}) async-start(bf16[4,256,1024]{2,1,0:T(8,128)(2,1)} %broadcast_in_dim.74), calls=%async_computation.2 | async-start | bytes 4194304 | tf_op jit(solution)/shard_map/all_to_all | solution.py:237
  128.1 0.5 add_select_fusion
  128.6 2.6 scatter_custom_fusion
  131.2 1.1 clamp_bitcast_fusion.group_ref
  132.4 1.2 bitcast_subtract_fusion.start_ref
  133.6 3.1 copy.107
  136.8 41.7 %all-gather.2.cloned.1.call-done = bf16[3,2048,2,256]{3,1,2,0:T(8,128)(2,1)} async-done(((bf16[3,64,2,256]{3,1,2,0:T(8,128)(2,1)}), bf16[3,2048,2,256]{3,1,2,0:T(8,128)(2,1)}) %all-gather.2.cloned.1.call-update) | async-done | bytes 6291472 | tf_op jit(solution)/shard_map/all_gather | solution.py:221
  178.4 17.5 %shard_map.140 = bf16[256,256]{1,0:T(8,128)(2,1)} custom-call(s32[4]{0:T(128)} %clamp_bitcast_fusion.group_ref, s32[4]{0:T(128)} %bitcast_subtract_fusion.start_ref, s32[4]{0:T(128)} %bitcast.112, bf16[256,256]{1,0:T(8,128)(2,1)} %bitcast.106, bf16[256,256]{1,0:T(8,128)(2,1)} %bitcast.107, bf16[256,256]{1,0:T(8,128)(2,1)} %bitcast.108, ...), custom_call_target="tpu_custom_call" | custom-call | flops 5171576832 | bytes 6815744 | tf_op jit(solution)/shard_map/pallas_call | solution.py:139
  195.9 9.1 %all_gather.11 = bf16[256,1024]{1,0:T(8,128)(2,1)} all-gather(bf16[256,256]{1,0:T(8,128)(2,1)} %shard_map.140), channel_id=1, replica_groups=mesh['req'=32,'exp'=4] {'exp'}, dimensions={1}, use_global_device_ids=true | all-gather | bytes 655360 | tf_op jit(solution)/shard_map/all_gather | solution.py:235
  205.1 2.0 multiply_reduce_fusion
  207.1 1.0 copy-done.2
  208.1 0.2 multiply_convert_fusion
  208.3 0.8 copy-done.3
  209.1 2.8 gather_fusion.1
  212.0 0.4 broadcast_in_dim.83
  212.4 41.4 %all_to_all.30 = bf16[32,1,40,1024]{3,2,1,0:T(8,128)(2,1)S(1)} all-to-all(bf16[32,1,40,1024]{3,2,1,0:T(8,128)(2,1)S(1)} %bitcast.96), channel_id=1, replica_groups=mesh['req'=32,'exp'=4] {'req'}, dimensions={0} | all-to-all | bytes 5242880 | tf_op jit(solution)/shard_map/all_to_all | solution.py:261
  253.8 2.3 fusion.5
  256.1 3.3 %convert_bitcast_fusion = bf16[32,1,40,1024]{3,2,1,0:T(8,128)(2,1)} fusion(f32[32,1,40,2,352]{4,2,3,0,1:T(8,128)S(1)} %fusion.5, bf16[1,352,1024]{2,1,0:T(8,128)(2,1)S(1)} %copy-done.9), kind=kOutput, calls=%fused_computation.7 | convolution fusion | flops 928563200 | bytes 6946816 | tf_op jit(solution)/shard_map/slch,lhd->slcd/dot_general | solution.py:184
  259.4 5.4 %all-to-all-start.4 = ((bf16[32,1,40,1024]{3,2,1,0:T(8,128)(2,1)}), bf16[32,1,40,1024]{3,2,1,0:T(8,128)(2,1)}, u32[]{:S(2)}, u32[]{:S(2)}) async-start(bf16[32,1,40,1024]{3,2,1,0:T(8,128)(2,1)} %convert_bitcast_fusion), calls=%async_computation.4 | async-start | bytes 5242880 | tf_op jit(solution)/shard_map/all_to_all | solution.py:263
  265.0 0.1 reshape.250
  265.2 0.2 lt.57
  265.5 0.2 fusion.45
  265.7 4.6 %gather_fusion.2 = f32[512]{0:T(512)S(1)} fusion(f32[256,16]{0,1:T(8,128)S(1)} %fusion.45, s32[512]{0:T(512)S(1)} %reshape.250), kind=kCustom, calls=%fused_computation.2 | custom fusion | bytes 8192 | tf_op jit(solution)/shard_map/jit(take_along_axis)/gather | solution.py:250
  270.3 0.1 reshape.253
  270.5 0.7 select_reduce_fusion
  271.2 27.4 %all-to-all-done.4 = bf16[32,1,40,1024]{3,2,1,0:T(8,128)(2,1)} async-done(((bf16[32,1,40,1024]{3,2,1,0:T(8,128)(2,1)}), bf16[32,1,40,1024]{3,2,1,0:T(8,128)(2,1)}, u32[]{:S(2)}, u32[]{:S(2)}) %all-to-all-start.4) | async-done | bytes 2621472 | tf_op jit(solution)/shard_map/all_to_all | solution.py:263
  298.6 4.0 %convolution_convert_fusion = bf16[256,1024]{1,0:T(8,128)(2,1)S(1)} fusion(f32[256,1280]{1,0:T(8,128)S(1)} %select_reduce_fusion, bf16[1280,1024]{1,0:T(8,128)(2,1)} %bitcast.39), kind=kOutput, calls=%fused_computation.27 | convolution fusion | flops 4026793984 | bytes 4456448 | tf_op jit(solution)/shard_map/dot_general | solution.py:273
  302.6 0.8 copy.129
  303.4 5.7 %all-to-all-start.5 = ((bf16[4,256,256]{2,1,0:T(8,128)(2,1)}), bf16[4,256,256]{2,1,0:T(8,128)(2,1)S(1)}, u32[]{:S(2)}, u32[]{:S(2)}) async-start(bf16[4,256,256]{2,1,0:T(8,128)(2,1)} %bitcast.95), calls=%async_computation.5 | async-start | bytes 1048576 | tf_op jit(solution)/shard_map/all_to_all | solution.py:283
  309.2 0.9 copy.118
  310.0 7.0 %all-to-all-done.5 = bf16[4,256,256]{2,1,0:T(8,128)(2,1)S(1)} async-done(((bf16[4,256,256]{2,1,0:T(8,128)(2,1)}), bf16[4,256,256]{2,1,0:T(8,128)(2,1)S(1)}, u32[]{:S(2)}, u32[]{:S(2)}) %all-to-all-start.5) | async-done | bytes 524320 | tf_op jit(solution)/shard_map/all_to_all | solution.py:283
  317.0 1.7 add_convert_fusion
  (48 shorter events, 0.7 us)
Async XLA Ops:
  7.2 246.6 %copy-start = (bf16[1,1024,2,352]{1,3,2,0:T(8,128)(2,1)S(1)}, bf16[1,1024,2,352]{1,3,2,0:T(8,128)(2,1)}, u32[]{:S(2)}) copy-start(bf16[1,1024,2,352]{1,3,2,0:T(8,128)(2,1)} %param.24) | copy-start | bytes 4325380
  10.7 11.5 %copy-start.11 = (s32[4]{0:T(128)S(1)}, s32[4]{0:T(128)}, u32[]{:S(2)}) copy-start(s32[4]{0:T(128)} %param.16) | copy-start | bytes 52
  10.7 39.4 %all-to-all-start = ((bf16[32,64,2,256]{3,1,2,0:T(8,128)(2,1)}), bf16[32,64,2,256]{3,1,2,0:T(8,128)(2,1)S(1)}, u32[]{:S(2)}, u32[]{:S(2)}) async-start(bf16[32,64,2,256]{3,1,2,0:T(8,128)(2,1)} %copy.106), calls=%async_computation | async-start | bytes 4194304 | tf_op jit(solution)/shard_map/all_to_all | solution.py:219
  22.1 156.3 %all-gather.2.cloned.1.call-start = ((), (), s32[]{:S(2)}) async-start(), calls=%async_computation.6 | async-start | bytes 6488064 | tf_op jit(solution)/shard_map/all_gather | solution.py:221
  54.7 36.2 %copy-start.6 = (s32[256,2]{0,1:T(2,128)S(1)}, s32[256,2]{0,1:T(2,128)}, u32[]{:S(2)}) copy-start(s32[256,2]{0,1:T(2,128)} %param.23) | copy-start | bytes 6148
  54.7 66.6 %all-to-all-start.1 = ((bf16[32,2,64,256]{3,2,1,0:T(8,128)(2,1)}), bf16[32,2,64,256]{3,2,1,0:T(8,128)(2,1)S(1)}, u32[]{:S(2)}, u32[]{:S(2)}) async-start(bf16[32,2,64,256]{3,2,1,0:T(8,128)(2,1)} %broadcast_in_dim.73), calls=%async_computation.1 | async-start | bytes 4194304 | tf_op jit(solution)/shard_map/all_to_all | solution.py:224
  90.9 6.8 %copy-start.10 = (f32[1024]{0:T(1024)S(1)}, f32[1024]{0:T(1024)}, u32[]{:S(2)}) copy-start(f32[1024]{0:T(1024)} %param.18) | copy-start | bytes 12292
  100.6 8.8 %copy-start.12 = (s32[1,4]{1,0:T(1,128)S(1)}, s32[1,4]{1,0:T(1,128)}, u32[]{:S(2)}) copy-start(s32[1,4]{1,0:T(1,128)} %param.14) | copy-start | bytes 52
  121.3 3.0 copy-start.1
  124.3 80.8 %all-to-all-start.2 = ((bf16[4,256,1024]{2,1,0:T(8,128)(2,1)}), bf16[4,256,1024]{2,1,0:T(8,128)(2,1)S(1)}, u32[]{:S(2)}, u32[]{:S(2)}) async-start(bf16[4,256,1024]{2,1,0:T(8,128)(2,1)} %broadcast_in_dim.74), calls=%async_computation.2 | async-start | bytes 4194304 | tf_op jit(solution)/shard_map/all_to_all | solution.py:237
  205.1 3.0 copy-start.8
  207.1 1.0 copy-start.2
  208.3 0.8 copy-start.3
  253.8 2.3 copy-start.9
  259.4 6.0 %copy-start.4 = (bf16[256,1024]{1,0:T(8,128)(2,1)S(1)}, bf16[256,1024]{1,0:T(8,128)(2,1)}, u32[]{:S(2)}) copy-start(bf16[256,1024]{1,0:T(8,128)(2,1)} %copy-done.3) | copy-start | bytes 1572868
  259.4 6.0 %copy-start.7 = (bf16[1024,16]{0,1:T(8,128)(2,1)S(1)}, bf16[1024,16]{0,1:T(8,128)(2,1)}, u32[]{:S(2)}) copy-start(bf16[1024,16]{0,1:T(8,128)(2,1)} %param.22) | copy-start | bytes 98308
  259.4 39.2 %all-to-all-start.4 = ((bf16[32,1,40,1024]{3,2,1,0:T(8,128)(2,1)}), bf16[32,1,40,1024]{3,2,1,0:T(8,128)(2,1)}, u32[]{:S(2)}, u32[]{:S(2)}) async-start(bf16[32,1,40,1024]{3,2,1,0:T(8,128)(2,1)} %convert_bitcast_fusion), calls=%async_computation.4 | async-start | bytes 5242880 | tf_op jit(solution)/shard_map/all_to_all | solution.py:263
  302.6 6.5 %copy-start.5 = (bf16[256,768]{0,1:T(8,128)(2,1)S(1)}, bf16[256,768]{0,1:T(8,128)(2,1)}, u32[]{:S(2)}) copy-start(bf16[256,768]{0,1:T(8,128)(2,1)} %copy.101) | copy-start | bytes 1179652
  303.4 13.5 %all-to-all-start.5 = ((bf16[4,256,256]{2,1,0:T(8,128)(2,1)}), bf16[4,256,256]{2,1,0:T(8,128)(2,1)S(1)}, u32[]{:S(2)}, u32[]{:S(2)}) async-start(bf16[4,256,256]{2,1,0:T(8,128)(2,1)} %bitcast.95), calls=%async_computation.5 | async-start | bytes 1048576 | tf_op jit(solution)/shard_map/all_to_all | solution.py:283
Sparse Core Ops, SparseCore 0:
  53.2 125.1 all-gather.1

commit v9 on v7

--- a/solution.py
+++ b/solution.py
@@ -247,7 +247,7 @@
     )
     returned = lax.all_to_all(
         partial_out.astype(jnp.bfloat16), "req", split_axis=0, concat_axis=0, tiled=True
-    ).astype(partial_out.dtype)
+    )
     block_count, _, _, out_columns = returned.shape
     pair_column = flat_ids * (SPLIT * CAP) + jnp.minimum(ranks, CAP - 1)
     pair_scale = jnp.where(kept, gates, 0.0)
@@ -255,11 +255,11 @@
     offset = columns_all - pair_column[:, None]
     hit = (offset == 0) | (offset == CAP)
     selection = jnp.where(hit, pair_scale[:, None], 0.0).reshape(row_count, TOP, -1).sum(axis=1)
-    mixture = jnp.dot(
-        selection,
-        returned.reshape(block_count * CAP, out_columns).astype(jnp.float32),
-        precision=lax.Precision.HIGHEST,
-        preferred_element_type=jnp.float32,
+    selection_hi = selection.astype(jnp.bfloat16)
+    selection_lo = (selection - selection_hi.astype(jnp.float32)).astype(jnp.bfloat16)
+    returned_rows = returned.reshape(block_count * CAP, out_columns)
+    mixture = jnp.dot(selection_hi, returned_rows, preferred_element_type=jnp.float32) + jnp.dot(
+        selection_lo, returned_rows, preferred_element_type=jnp.float32
     )
     blocks = jnp.transpose(
         mixture.astype(jnp.bfloat16).reshape(row_count, exp_total, quarter), (1, 0, 2)

time: 303 us -> 304 us (level)
  no operation moved by 1% of the time
where the time goes in v9:
time: 304 us; the launch traced here: 303 us
  waiting for transfers between devices  103 us (34%)
  blocking collectives  67.9 us (22%)
  local copies, waits for them, and re-layouts  42.2 us (14%)
  starting transfers between devices  28.5 us (9%)
  Pallas kernels  16.8 us (6%)
  matrix products  15.9 us (5%)
  between operations  14.3 us (5%)
  other arithmetic  14.2 us (5%)
    all_gather x1, waiting for transfers between devices, shards(): cached = lax.all_gather(owned, 'req', axis=1, tiled=True)  41.1 us
    all_to_all x1, blocking collectives, shards(): lax.all_to_all(outgoing_rows, 'req', split_axis=0, concat_axis=0, tiled=T...  40.6 us
    all_to_all x1, waiting for transfers between devices, shards(): lax.all_to_all(pieces, 'req', split_axis=0, concat_axis=0, tiled=True)  27.8 us
    all_to_all x1, waiting for transfers between devices, shards(): lax.all_to_all(partial_out.astype(jnp.bfloat16), 'req', split_axis=0, con...  27.4 us
    all_gather x1, blocking collectives, shards(): rows_whole = lax.all_gather(tokens, 'exp', axis=1, tiled=True)  18.8 us
    pallas_call x1, Pallas kernels, attention(): pl.pallas_call(attention_kernel, grid_spec=grid_spec, out_shape=jax.Shape...  16.8 us
    unnamed x30, local copies, waits for them, and re-layouts  11.7 us
    all_to_all x1, starting transfers between devices, shards(): lax.all_to_all(pieces, 'req', split_axis=0, concat_axis=0, tiled=True)  11.5 us
  transfers between devices with their start and end apart: 5, of which 4 were waited for; matrix products, arithmetic and copies ran while one was open for 15% of the time, Pallas kernels for 6%

profile of v9, /device:TPU:1, one launch (start us, length us, event | category | flops | bytes accessed | tf_op | source)
XLA Modules:
  0.0 303.0 jit_solution(11520880612849334687)
XLA Ops:
  7.2 3.5 %copy.104 = bf16[32,64,2,256]{3,1,2,0:T(8,128)(2,1)} copy(bf16[32,64,2,256]{3,2,1,0:T(2,128)(2,1)} %bitcast.96) | data formatting | bytes 4194304 | tf_op jit(solution)/shard_map/reshape;squeeze | solution.py:212
  10.7 11.5 %all-to-all-start = ((bf16[32,64,2,256]{3,1,2,0:T(8,128)(2,1)}), bf16[32,64,2,256]{3,1,2,0:T(8,128)(2,1)S(1)}, u32[]{:S(2)}, u32[]{:S(2)}) async-start(bf16[32,64,2,256]{3,1,2,0:T(8,128)(2,1)} %copy.104), calls=%async_computation | async-start | bytes 4194304 | tf_op jit(solution)/shard_map/all_to_all | solution.py:213
  22.2 27.8 %all-to-all-done = bf16[32,64,2,256]{3,1,2,0:T(8,128)(2,1)S(1)} async-done(((bf16[32,64,2,256]{3,1,2,0:T(8,128)(2,1)}), bf16[32,64,2,256]{3,1,2,0:T(8,128)(2,1)S(1)}, u32[]{:S(2)}, u32[]{:S(2)}) %all-to-all-start) | async-done | bytes 2097184 | tf_op jit(solution)/shard_map/all_to_all | solution.py:213
  50.1 1.3 gather_fusion
  51.3 1.7 broadcast_select_fusion
  53.1 2.7 broadcast_in_dim.67
  55.8 5.9 %all-to-all-start.1 = ((bf16[4,256,1024]{2,1,0:T(8,128)(2,1)}), bf16[4,256,1024]{2,1,0:T(8,128)(2,1)S(1)}, u32[]{:S(2)}, u32[]{:S(2)}) async-start(bf16[4,256,1024]{2,1,0:T(8,128)(2,1)} %broadcast_in_dim.67), calls=%async_computation.1 | async-start | bytes 4194304 | tf_op jit(solution)/shard_map/all_to_all | solution.py:222
  61.7 0.8 copy.105
  62.5 1.0 eq.43
  63.5 1.0 eq.39
  64.6 0.7 reduce-window.19
  65.3 0.6 fusion.37
  66.0 3.1 %reduce-window.20 = s32[16,4,128]{2,0,1:T(8,128)} reduce-window(s32[16,4,128]{2,0,1:T(8,128)} %fusion.37, s32[]{:T(128)} %constant.31.clone.1), window={size=1x1x128 pad=0_0x0_0x127_0}, to_apply=%region_2.3 | reduce-window | flops 1040384 | bytes 65540 | tf_op jit(solution)/shard_map/reduce-window.1
  69.1 1.0 slice_reduce_fusion
  70.1 0.9 fusion.36
  71.0 0.8 min.28
  71.8 1.0 copy.108
  72.7 0.6 multiply_add_fusion
  73.3 1.5 copy.112
  74.8 1.0 mul.126
  75.8 2.6 copy.98
  78.4 18.8 %all_gather.9 = bf16[256,1024]{1,0:T(8,128)(2,1)S(1)} all-gather(bf16[256,256]{1,0:T(8,128)(2,1)} %param.13), channel_id=1, replica_groups=mesh['req'=32,'exp'=4] {'exp'}, dimensions={1}, use_global_device_ids=true | all-gather | bytes 655360 | tf_op jit(solution)/shard_map/all_gather | solution.py:196
  97.2 0.2 fusion.19
  97.4 0.6 copy-done.2
  98.1 2.9 convolution_convert_fusion
  100.9 1.9 copy.99
  102.8 1.8 fusion.48
  104.6 1.7 copy.121
  106.3 1.7 copy.120
  107.9 1.7 copy.119
  109.6 0.6 compare_select_fusion
  110.2 0.6 add_select_fusion
  110.8 2.6 scatter_custom_fusion
  113.4 1.2 clamp_bitcast_fusion.group_ref
  114.6 1.2 bitcast_subtract_fusion.start_ref
  115.9 41.1 %all-gather.2.cloned.1.call-done = bf16[4,2048,2,256]{3,1,2,0:T(8,128)(2,1)} async-done(((bf16[4,64,2,256]{3,1,2,0:T(8,128)(2,1)}), bf16[4,2048,2,256]{3,1,2,0:T(8,128)(2,1)}) %all-gather.2.cloned.1.call-update) | async-done | bytes 8388624 | tf_op jit(solution)/shard_map/all_gather | solution.py:215
  156.9 16.8 %shard_map.140 = bf16[256,256]{1,0:T(8,128)(2,1)} custom-call(s32[4]{0:T(128)} %clamp_bitcast_fusion.group_ref, s32[4]{0:T(128)} %bitcast_subtract_fusion.start_ref, s32[4]{0:T(128)} %bitcast.105, bf16[256,256]{1,0:T(8,128)(2,1)} %bitcast.101, bf16[256,256]{1,0:T(8,128)(2,1)} %bitcast.100, bf16[256,256]{1,0:T(8,128)(2,1)} %bitcast.99, ...), custom_call_target="tpu_custom_call" | custom-call | flops 5171576832 | bytes 8912896 | tf_op jit(solution)/shard_map/pallas_call | solution.py:134
  173.7 8.5 %all_gather.11 = bf16[256,1024]{1,0:T(8,128)(2,1)} all-gather(bf16[256,256]{1,0:T(8,128)(2,1)} %shard_map.140), channel_id=1, replica_groups=mesh['req'=32,'exp'=4] {'exp'}, dimensions={1}, use_global_device_ids=true | all-gather | bytes 655360 | tf_op jit(solution)/shard_map/all_gather | solution.py:220
  182.2 2.0 multiply_reduce_fusion
  184.2 1.0 copy-done.1
  185.2 0.2 multiply_convert_fusion
  185.4 0.8 copy-done.3
  186.2 2.8 gather_fusion.1
  189.1 0.4 broadcast_in_dim.76
  189.4 40.6 %all_to_all.25 = bf16[32,1,40,1024]{3,2,1,0:T(8,128)(2,1)S(1)} all-to-all(bf16[32,1,40,1024]{3,2,1,0:T(8,128)(2,1)S(1)} %bitcast.91), channel_id=1, replica_groups=mesh['req'=32,'exp'=4] {'req'}, dimensions={0} | all-to-all | bytes 5242880 | tf_op jit(solution)/shard_map/all_to_all | solution.py:246
  230.1 2.3 fusion.5
  232.4 3.3 %convert_bitcast_fusion = bf16[32,1,40,1024]{3,2,1,0:T(8,128)(2,1)} fusion(f32[32,1,40,2,352]{4,2,3,0,1:T(8,128)S(1)} %fusion.5, bf16[1,352,1024]{2,1,0:T(8,128)(2,1)S(1)} %copy-done.9), kind=kOutput, calls=%fused_computation.7 | convolution fusion | flops 928563200 | bytes 6946816 | tf_op jit(solution)/shard_map/slch,lhd->slcd/dot_general | solution.py:178
  235.7 5.4 %all-to-all-start.3 = ((bf16[32,1,40,1024]{3,2,1,0:T(8,128)(2,1)}), bf16[32,1,40,1024]{3,2,1,0:T(8,128)(2,1)}, u32[]{:S(2)}, u32[]{:S(2)}) async-start(bf16[32,1,40,1024]{3,2,1,0:T(8,128)(2,1)} %convert_bitcast_fusion), calls=%async_computation.3 | async-start | bytes 5242880 | tf_op jit(solution)/shard_map/all_to_all | solution.py:248
  241.1 0.1 copy.109
  241.3 0.1 reshape.245
  241.4 0.2 lt.57
  241.6 0.1 copy.111
  241.7 0.2 fusion.49
  242.0 4.6 %gather_fusion.2 = f32[512]{0:T(512)S(1)} fusion(f32[256,16]{0,1:T(8,128)S(1)} %fusion.49, s32[512]{0:T(512)S(1)} %reshape.245), kind=kCustom, calls=%fused_computation.2 | custom fusion | bytes 8192 | tf_op jit(solution)/shard_map/jit(take_along_axis)/gather | solution.py:235
  246.5 0.1 reshape.248
  246.8 0.7 select_reduce_fusion
  247.5 27.4 %all-to-all-done.3 = bf16[32,1,40,1024]{3,2,1,0:T(8,128)(2,1)} async-done(((bf16[32,1,40,1024]{3,2,1,0:T(8,128)(2,1)}), bf16[32,1,40,1024]{3,2,1,0:T(8,128)(2,1)}, u32[]{:S(2)}, u32[]{:S(2)}) %all-to-all-start.3) | async-done | bytes 2621472 | tf_op jit(solution)/shard_map/all_to_all | solution.py:248
  274.9 2.6 fusion.32
  277.5 2.6 fusion.18
  280.1 0.8 copy.126
  280.9 5.7 %all-to-all-start.4 = ((bf16[4,256,256]{2,1,0:T(8,128)(2,1)}), bf16[4,256,256]{2,1,0:T(8,128)(2,1)S(1)}, u32[]{:S(2)}, u32[]{:S(2)}) async-start(bf16[4,256,256]{2,1,0:T(8,128)(2,1)} %bitcast.89), calls=%async_computation.4 | async-start | bytes 1048576 | tf_op jit(solution)/shard_map/all_to_all | solution.py:268
  286.6 0.9 copy.115
  287.5 7.0 %all-to-all-done.4 = bf16[4,256,256]{2,1,0:T(8,128)(2,1)S(1)} async-done(((bf16[4,256,256]{2,1,0:T(8,128)(2,1)}), bf16[4,256,256]{2,1,0:T(8,128)(2,1)S(1)}, u32[]{:S(2)}, u32[]{:S(2)}) %all-to-all-start.4) | async-done | bytes 524320 | tf_op jit(solution)/shard_map/all_to_all | solution.py:268
  294.5 1.7 add_convert_fusion
  (41 shorter events, 0.4 us)
Async XLA Ops:
  7.2 222.9 %copy-start = (bf16[1,1024,2,352]{1,3,2,0:T(8,128)(2,1)S(1)}, bf16[1,1024,2,352]{1,3,2,0:T(8,128)(2,1)}, u32[]{:S(2)}) copy-start(bf16[1,1024,2,352]{1,3,2,0:T(8,128)(2,1)} %param.24) | copy-start | bytes 4325380
  10.7 11.5 %copy-start.10 = (s32[4]{0:T(128)S(1)}, s32[4]{0:T(128)}, u32[]{:S(2)}) copy-start(s32[4]{0:T(128)} %param.16) | copy-start | bytes 52
  10.7 39.4 %all-to-all-start = ((bf16[32,64,2,256]{3,1,2,0:T(8,128)(2,1)}), bf16[32,64,2,256]{3,1,2,0:T(8,128)(2,1)S(1)}, u32[]{:S(2)}, u32[]{:S(2)}) async-start(bf16[32,64,2,256]{3,1,2,0:T(8,128)(2,1)} %copy.104), calls=%async_computation | async-start | bytes 4194304 | tf_op jit(solution)/shard_map/all_to_all | solution.py:213
  22.1 134.8 %all-gather.2.cloned.1.call-start = ((), (), s32[]{:S(2)}) async-start(), calls=%async_computation.5 | async-start | bytes 8650752 | tf_op jit(solution)/shard_map/all_gather | solution.py:215
  55.8 5.9 %copy-start.6 = (s32[256,2]{0,1:T(2,128)S(1)}, s32[256,2]{0,1:T(2,128)}, u32[]{:S(2)}) copy-start(s32[256,2]{0,1:T(2,128)} %param.23) | copy-start | bytes 6148
  55.8 8.8 %copy-start.11 = (s32[1,4]{1,0:T(1,128)S(1)}, s32[1,4]{1,0:T(1,128)}, u32[]{:S(2)}) copy-start(s32[1,4]{1,0:T(1,128)} %param.14) | copy-start | bytes 52
  55.8 126.3 %all-to-all-start.1 = ((bf16[4,256,1024]{2,1,0:T(8,128)(2,1)}), bf16[4,256,1024]{2,1,0:T(8,128)(2,1)S(1)}, u32[]{:S(2)}, u32[]{:S(2)}) async-start(bf16[4,256,1024]{2,1,0:T(8,128)(2,1)} %broadcast_in_dim.67), calls=%async_computation.1 | async-start | bytes 4194304 | tf_op jit(solution)/shard_map/all_to_all | solution.py:222
  97.2 0.8 copy-start.2
  182.2 3.0 %copy-start.8 = (f32[1024]{0:T(1024)S(1)}, f32[1024]{0:T(1024)}, u32[]{:S(2)}) copy-start(f32[1024]{0:T(1024)} %param.21) | copy-start | bytes 12292
  184.2 1.0 copy-start.1
  185.4 0.8 copy-start.3
  230.1 2.3 copy-start.9
  235.7 6.0 %copy-start.4 = (bf16[256,1024]{1,0:T(8,128)(2,1)S(1)}, bf16[256,1024]{1,0:T(8,128)(2,1)}, u32[]{:S(2)}) copy-start(bf16[256,1024]{1,0:T(8,128)(2,1)} %copy-done.3) | copy-start | bytes 1572868
  235.7 6.0 %copy-start.7 = (bf16[1024,16]{0,1:T(8,128)(2,1)S(1)}, bf16[1024,16]{0,1:T(8,128)(2,1)}, u32[]{:S(2)}) copy-start(bf16[1024,16]{0,1:T(8,128)(2,1)} %param.22) | copy-start | bytes 98308
  235.7 39.2 %all-to-all-start.3 = ((bf16[32,1,40,1024]{3,2,1,0:T(8,128)(2,1)}), bf16[32,1,40,1024]{3,2,1,0:T(8,128)(2,1)}, u32[]{:S(2)}, u32[]{:S(2)}) async-start(bf16[32,1,40,1024]{3,2,1,0:T(8,128)(2,1)} %convert_bitcast_fusion), calls=%async_computation.3 | async-start | bytes 5242880 | tf_op jit(solution)/shard_map/all_to_all | solution.py:248
  280.1 6.5 %copy-start.5 = (bf16[256,768]{0,1:T(8,128)(2,1)S(1)}, bf16[256,768]{0,1:T(8,128)(2,1)}, u32[]{:S(2)}) copy-start(bf16[256,768]{0,1:T(8,128)(2,1)} %copy.99) | copy-start | bytes 1179652
  280.9 13.6 %all-to-all-start.4 = ((bf16[4,256,256]{2,1,0:T(8,128)(2,1)}), bf16[4,256,256]{2,1,0:T(8,128)(2,1)S(1)}, u32[]{:S(2)}, u32[]{:S(2)}) async-start(bf16[4,256,256]{2,1,0:T(8,128)(2,1)} %bitcast.89), calls=%async_computation.4 | async-start | bytes 1048576 | tf_op jit(solution)/shard_map/all_to_all | solution.py:268
Sparse Core Ops, SparseCore 0:
  53.2 103.6 all-gather.1

commit v10 on v7

--- a/solution.py
+++ b/solution.py
@@ -242,12 +242,23 @@
     outgoing_rows = jnp.broadcast_to(picked, (EXPERTS, SPLIT, CAP, columns)).reshape(
         req_total, local_rows, CAP, columns
     )
-    partial_out = expert_apply(
-        lax.all_to_all(outgoing_rows, "req", split_axis=0, concat_axis=0, tiled=True), w_in, w_down
-    )
-    returned = lax.all_to_all(
-        partial_out.astype(jnp.bfloat16), "req", split_axis=0, concat_axis=0, tiled=True
-    ).astype(partial_out.dtype)
+    lanes = 128
+    flat_shape = (req_total, local_rows, CAP * columns // lanes, lanes)
+    arrived = lax.all_to_all(
+        outgoing_rows.reshape(flat_shape), "req", split_axis=0, concat_axis=0, tiled=True
+    ).reshape(outgoing_rows.shape)
+    partial_out = expert_apply(arrived, w_in, w_down)
+    returned = (
+        lax.all_to_all(
+            partial_out.astype(jnp.bfloat16).reshape(flat_shape),
+            "req",
+            split_axis=0,
+            concat_axis=0,
+            tiled=True,
+        )
+        .reshape(partial_out.shape)
+        .astype(partial_out.dtype)
+    )
     block_count, _, _, out_columns = returned.shape
     pair_column = flat_ids * (SPLIT * CAP) + jnp.minimum(ranks, CAP - 1)
     pair_scale = jnp.where(kept, gates, 0.0)

time: 303 us -> 328 us (1.083)
  local copies, waits for them, and re-layouts: 42.2 us -> 64.5 us
    reshape x0 -> x2, local copies, waits for them, and re-layouts: none -> 10.4 us  [the longest x1 5.2 us: shards(): returned.reshape(block_count * CAP, out_columns).astype(jnp.float32)]
    another operation x1 -> x3, local copies, waits for them, and re-layouts: 0.01 us -> 10.4 us
  transfers between devices with their start and end apart: 5 -> 5, of which waited for: 4 -> 4; matrix products, arithmetic and copies ran while one was open for 15% -> 14% of each run, Pallas kernels for 6% -> 5%
where the time goes in v10:
time: 328 us; the launch traced here: 326 us
  waiting for transfers between devices  103 us (31%)
  blocking collectives  68.3 us (21%)
  local copies, waits for them, and re-layouts  64.5 us (20%)
  starting transfers between devices  28.5 us (9%)
  Pallas kernels  16.8 us (5%)
  matrix products  16.4 us (5%)
  between operations  14.3 us (4%)
  other arithmetic  14.2 us (4%)
    all_gather x1, waiting for transfers between devices, shards(): cached = lax.all_gather(owned, 'req', axis=1, tiled=True)  41.1 us
    all_to_all x1, blocking collectives, shards(): lax.all_to_all(outgoing_rows.reshape(flat_shape), 'req', split_axis=0, co...  40.9 us
    all_to_all x1, waiting for transfers between devices, shards(): lax.all_to_all(pieces, 'req', split_axis=0, concat_axis=0, tiled=True)  27.8 us
    all_to_all x1, waiting for transfers between devices, shards(): lax.all_to_all(partial_out.astype(jnp.bfloat16).reshape(flat_shape), 'req...  27.5 us
    all_gather x1, blocking collectives, shards(): rows_whole = lax.all_gather(tokens, 'exp', axis=1, tiled=True)  18.8 us
    pallas_call x1, Pallas kernels, attention(): pl.pallas_call(attention_kernel, grid_spec=grid_spec, out_shape=jax.Shape...  16.8 us
    unnamed x30, local copies, waits for them, and re-layouts  11.7 us
    all_to_all x1, starting transfers between devices, shards(): lax.all_to_all(pieces, 'req', split_axis=0, concat_axis=0, tiled=True)  11.5 us
  transfers between devices with their start and end apart: 5, of which 4 were waited for; matrix products, arithmetic and copies ran while one was open for 14% of the time, Pallas kernels for 5%

profile of v10, /device:TPU:1, one launch (start us, length us, event | category | flops | bytes accessed | tf_op | source)
XLA Modules:
  0.0 326.2 jit_solution(743715996333370872)
XLA Ops:
  7.2 3.5 %copy.104 = bf16[32,64,2,256]{3,1,2,0:T(8,128)(2,1)} copy(bf16[32,64,2,256]{3,2,1,0:T(2,128)(2,1)} %bitcast.100) | data formatting | bytes 4194304 | tf_op jit(solution)/shard_map/reshape;squeeze | solution.py:212
  10.7 11.5 %all-to-all-start = ((bf16[32,64,2,256]{3,1,2,0:T(8,128)(2,1)}), bf16[32,64,2,256]{3,1,2,0:T(8,128)(2,1)S(1)}, u32[]{:S(2)}, u32[]{:S(2)}) async-start(bf16[32,64,2,256]{3,1,2,0:T(8,128)(2,1)} %copy.104), calls=%async_computation | async-start | bytes 4194304 | tf_op jit(solution)/shard_map/all_to_all | solution.py:213
  22.2 27.8 %all-to-all-done = bf16[32,64,2,256]{3,1,2,0:T(8,128)(2,1)S(1)} async-done(((bf16[32,64,2,256]{3,1,2,0:T(8,128)(2,1)}), bf16[32,64,2,256]{3,1,2,0:T(8,128)(2,1)S(1)}, u32[]{:S(2)}, u32[]{:S(2)}) %all-to-all-start) | async-done | bytes 2097184 | tf_op jit(solution)/shard_map/all_to_all | solution.py:213
  50.1 1.3 gather_fusion
  51.3 1.7 broadcast_select_fusion
  53.1 2.7 broadcast_in_dim.67
  55.8 5.9 %all-to-all-start.1 = ((bf16[4,256,1024]{2,1,0:T(8,128)(2,1)}), bf16[4,256,1024]{2,1,0:T(8,128)(2,1)S(1)}, u32[]{:S(2)}, u32[]{:S(2)}) async-start(bf16[4,256,1024]{2,1,0:T(8,128)(2,1)} %broadcast_in_dim.67), calls=%async_computation.1 | async-start | bytes 4194304 | tf_op jit(solution)/shard_map/all_to_all | solution.py:222
  61.7 0.8 copy.105
  62.5 1.0 eq.43
  63.5 1.0 eq.39
  64.6 0.7 reduce-window.19
  65.3 0.6 fusion.33
  66.0 3.1 reduce-window.20
  69.1 1.0 slice_reduce_fusion
  70.1 0.9 fusion.32
  71.0 0.8 min.28
  71.8 1.0 copy.108
  72.7 0.6 broadcast_multiply_fusion
  73.3 1.5 copy.112
  74.8 1.0 mul.126
  75.8 2.6 copy.98
  78.4 18.8 %all_gather.9 = bf16[256,1024]{1,0:T(8,128)(2,1)S(1)} all-gather(bf16[256,256]{1,0:T(8,128)(2,1)} %param.13), channel_id=1, replica_groups=mesh['req'=32,'exp'=4] {'exp'}, dimensions={1}, use_global_device_ids=true | all-gather | bytes 655360 | tf_op jit(solution)/shard_map/all_gather | solution.py:196
  97.2 0.2 fusion.18
  97.4 0.6 copy-done.2
  98.1 2.9 convolution_convert_fusion.1
  100.9 1.9 copy.99
  102.8 1.8 fusion.44
  104.6 1.7 copy.121
  106.3 1.7 copy.120
  107.9 1.7 copy.119
  109.6 0.6 compare_select_fusion
  110.2 0.6 add_select_fusion
  110.8 2.6 scatter_custom_fusion
  113.4 1.2 clamp_bitcast_fusion.group_ref
  114.6 1.2 bitcast_subtract_fusion.start_ref
  115.9 41.1 %all-gather.2.cloned.1.call-done = bf16[4,2048,2,256]{3,1,2,0:T(8,128)(2,1)} async-done(((bf16[4,64,2,256]{3,1,2,0:T(8,128)(2,1)}), bf16[4,2048,2,256]{3,1,2,0:T(8,128)(2,1)}) %all-gather.2.cloned.1.call-update) | async-done | bytes 8388624 | tf_op jit(solution)/shard_map/all_gather | solution.py:215
  156.9 16.8 %shard_map.140 = bf16[256,256]{1,0:T(8,128)(2,1)} custom-call(s32[4]{0:T(128)} %clamp_bitcast_fusion.group_ref, s32[4]{0:T(128)} %bitcast_subtract_fusion.start_ref, s32[4]{0:T(128)} %bitcast.109, bf16[256,256]{1,0:T(8,128)(2,1)} %bitcast.105, bf16[256,256]{1,0:T(8,128)(2,1)} %bitcast.104, bf16[256,256]{1,0:T(8,128)(2,1)} %bitcast.103, ...), custom_call_target="tpu_custom_call" | custom-call | flops 5171576832 | bytes 8912896 | tf_op jit(solution)/shard_map/pallas_call | solution.py:134
  173.7 8.5 %all_gather.11 = bf16[256,1024]{1,0:T(8,128)(2,1)} all-gather(bf16[256,256]{1,0:T(8,128)(2,1)} %shard_map.140), channel_id=1, replica_groups=mesh['req'=32,'exp'=4] {'exp'}, dimensions={1}, use_global_device_ids=true | all-gather | bytes 655360 | tf_op jit(solution)/shard_map/all_gather | solution.py:220
  182.2 2.0 multiply_reduce_fusion
  184.2 1.0 copy-done.1
  185.2 0.2 multiply_convert_fusion
  185.4 0.8 copy-done.3
  186.2 2.8 gather_fusion.1
  189.1 1.9 broadcast_in_dim.76
  191.0 5.2 %reshape_reshape.3 = bf16[32,1,320,128]{3,2,1,0:T(8,128)(2,1)} reshape(bf16[16,2,40,1024]{3,2,1,0:T(8,128)(2,1)} %broadcast_in_dim.76) | data formatting | bytes 5242880 | tf_op jit(solution)/shard_map/reshape;reshape | solution.py:248
  196.1 40.9 %all_to_all.25 = bf16[32,1,320,128]{3,2,1,0:T(8,128)(2,1)} all-to-all(bf16[32,1,320,128]{3,2,1,0:T(8,128)(2,1)} %reshape_reshape.3), channel_id=1, replica_groups=mesh['req'=32,'exp'=4] {'req'}, dimensions={0} | all-to-all | bytes 5242880 | tf_op jit(solution)/shard_map/all_to_all | solution.py:247
  237.1 5.2 %reshape.270 = bf16[32,40,1024,1]{2,1,0,3:T(8,128)(2,1)} reshape(bf16[32,1,320,128]{3,2,1,0:T(8,128)(2,1)} %all_to_all.25) | data formatting | bytes 5242880 | tf_op jit(solution)/shard_map/reshape.11
  242.3 4.1 %fusion.5 = f32[32,1,40,2,352]{4,2,3,0,1:T(8,128)S(1)} fusion(bf16[32,40,1024,1]{2,1,0,3:T(8,128)(2,1)} %reshape.270, bf16[1,1024,2,352]{1,3,2,0:T(8,128)(2,1)S(1)} %copy-done), kind=kOutput, calls=%fused_computation.13 | convolution fusion | flops 1845493760 | bytes 7667712 | tf_op jit(solution)/shard_map/slcd,ldgh->slcgh/dot_general | solution.py:174
  246.4 3.2 convert_bitcast_fusion
  249.6 5.2 %reshape.230 = bf16[32,1,320,128]{3,2,0,1:T(8,128)(2,1)} reshape(bf16[32,1,40,1024]{3,2,0,1:T(8,128)(2,1)} %convert_bitcast_fusion) | data formatting | bytes 5242880 | tf_op jit(solution)/shard_map/reshape | solution.py:253
  254.8 5.4 %all-to-all-start.3 = ((bf16[32,1,320,128]{3,2,1,0:T(8,128)(2,1)}), bf16[32,1,320,128]{3,2,1,0:T(8,128)(2,1)}, u32[]{:S(2)}, u32[]{:S(2)}) async-start(bf16[32,1,320,128]{3,2,1,0:T(8,128)(2,1)} %bitcast.95), calls=%async_computation.3 | async-start | bytes 5242880 | tf_op jit(solution)/shard_map/all_to_all | solution.py:252
  260.4 0.1 reshape.249
  260.6 0.2 lt.57
  260.9 0.2 fusion.45
  261.1 4.6 %gather_fusion.2 = f32[512]{0:T(512)S(1)} fusion(f32[256,16]{0,1:T(8,128)S(1)} %fusion.45, s32[512]{0:T(512)S(1)} %reshape.249), kind=kCustom, calls=%fused_computation.2 | custom fusion | bytes 8192 | tf_op jit(solution)/shard_map/jit(take_along_axis)/gather | solution.py:235
  265.9 0.7 select_reduce_fusion
  266.6 27.5 %all-to-all-done.3 = bf16[32,1,320,128]{3,2,1,0:T(8,128)(2,1)} async-done(((bf16[32,1,320,128]{3,2,1,0:T(8,128)(2,1)}), bf16[32,1,320,128]{3,2,1,0:T(8,128)(2,1)}, u32[]{:S(2)}, u32[]{:S(2)}) %all-to-all-start.3) | async-done | bytes 2621472 | tf_op jit(solution)/shard_map/all_to_all | solution.py:252
  294.1 5.2 %reshape.231 = bf16[1280,1024]{1,0:T(8,128)(2,1)} reshape(bf16[32,1,320,128]{3,2,1,0:T(8,128)(2,1)} %all-to-all-done.3) | data formatting | bytes 5242880 | tf_op jit(solution)/shard_map/reshape | solution.py:271
  299.3 4.0 %convolution_convert_fusion = bf16[256,1024]{1,0:T(8,128)(2,1)S(1)} fusion(f32[256,1280]{1,0:T(8,128)S(1)} %select_reduce_fusion, bf16[1280,1024]{1,0:T(8,128)(2,1)} %reshape.231), kind=kOutput, calls=%fused_computation.27 | convolution fusion | flops 4026793984 | bytes 4456448 | tf_op jit(solution)/shard_map/dot_general | solution.py:269
  303.3 0.8 copy.126
  304.1 5.7 %all-to-all-start.4 = ((bf16[4,256,256]{2,1,0:T(8,128)(2,1)}), bf16[4,256,256]{2,1,0:T(8,128)(2,1)S(1)}, u32[]{:S(2)}, u32[]{:S(2)}) async-start(bf16[4,256,256]{2,1,0:T(8,128)(2,1)} %bitcast.93), calls=%async_computation.4 | async-start | bytes 1048576 | tf_op jit(solution)/shard_map/all_to_all | solution.py:279
  309.8 0.9 copy.115
  310.7 7.0 %all-to-all-done.4 = bf16[4,256,256]{2,1,0:T(8,128)(2,1)S(1)} async-done(((bf16[4,256,256]{2,1,0:T(8,128)(2,1)}), bf16[4,256,256]{2,1,0:T(8,128)(2,1)S(1)}, u32[]{:S(2)}, u32[]{:S(2)}) %all-to-all-start.4) | async-done | bytes 524320 | tf_op jit(solution)/shard_map/all_to_all | solution.py:279
  317.7 1.7 add_convert_fusion
  (44 shorter events, 0.8 us)
Async XLA Ops:
  7.2 235.1 %copy-start = (bf16[1,1024,2,352]{1,3,2,0:T(8,128)(2,1)S(1)}, bf16[1,1024,2,352]{1,3,2,0:T(8,128)(2,1)}, u32[]{:S(2)}) copy-start(bf16[1,1024,2,352]{1,3,2,0:T(8,128)(2,1)} %param.24) | copy-start | bytes 4325380
  10.7 11.5 %copy-start.10 = (s32[4]{0:T(128)S(1)}, s32[4]{0:T(128)}, u32[]{:S(2)}) copy-start(s32[4]{0:T(128)} %param.16) | copy-start | bytes 52
  10.7 39.4 %all-to-all-start = ((bf16[32,64,2,256]{3,1,2,0:T(8,128)(2,1)}), bf16[32,64,2,256]{3,1,2,0:T(8,128)(2,1)S(1)}, u32[]{:S(2)}, u32[]{:S(2)}) async-start(bf16[32,64,2,256]{3,1,2,0:T(8,128)(2,1)} %copy.104), calls=%async_computation | async-start | bytes 4194304 | tf_op jit(solution)/shard_map/all_to_all | solution.py:213
  22.1 134.8 %all-gather.2.cloned.1.call-start = ((), (), s32[]{:S(2)}) async-start(), calls=%async_computation.5 | async-start | bytes 8650752 | tf_op jit(solution)/shard_map/all_gather | solution.py:215
  55.8 5.9 %copy-start.6 = (s32[256,2]{0,1:T(2,128)S(1)}, s32[256,2]{0,1:T(2,128)}, u32[]{:S(2)}) copy-start(s32[256,2]{0,1:T(2,128)} %param.23) | copy-start | bytes 6148
  55.8 8.8 %copy-start.11 = (s32[1,4]{1,0:T(1,128)S(1)}, s32[1,4]{1,0:T(1,128)}, u32[]{:S(2)}) copy-start(s32[1,4]{1,0:T(1,128)} %param.14) | copy-start | bytes 52
  55.8 126.3 %all-to-all-start.1 = ((bf16[4,256,1024]{2,1,0:T(8,128)(2,1)}), bf16[4,256,1024]{2,1,0:T(8,128)(2,1)S(1)}, u32[]{:S(2)}, u32[]{:S(2)}) async-start(bf16[4,256,1024]{2,1,0:T(8,128)(2,1)} %broadcast_in_dim.67), calls=%async_computation.1 | async-start | bytes 4194304 | tf_op jit(solution)/shard_map/all_to_all | solution.py:222
  97.2 0.8 copy-start.2
  182.2 3.0 copy-start.8
  184.2 1.0 copy-start.1
  185.4 0.8 copy-start.3
  242.3 4.1 %copy-start.9 = (bf16[1,352,1024]{2,1,0:T(8,128)(2,1)S(1)}, bf16[1,352,1024]{2,1,0:T(8,128)(2,1)}, u32[]{:S(2)}) copy-start(bf16[1,352,1024]{2,1,0:T(8,128)(2,1)} %param.25) | copy-start | bytes 2162692
  254.8 6.0 %copy-start.4 = (bf16[256,1024]{1,0:T(8,128)(2,1)S(1)}, bf16[256,1024]{1,0:T(8,128)(2,1)}, u32[]{:S(2)}) copy-start(bf16[256,1024]{1,0:T(8,128)(2,1)} %copy-done.3) | copy-start | bytes 1572868
  254.8 6.0 %copy-start.7 = (bf16[1024,16]{0,1:T(8,128)(2,1)S(1)}, bf16[1024,16]{0,1:T(8,128)(2,1)}, u32[]{:S(2)}) copy-start(bf16[1024,16]{0,1:T(8,128)(2,1)} %param.22) | copy-start | bytes 98308
  254.8 39.3 %all-to-all-start.3 = ((bf16[32,1,320,128]{3,2,1,0:T(8,128)(2,1)}), bf16[32,1,320,128]{3,2,1,0:T(8,128)(2,1)}, u32[]{:S(2)}, u32[]{:S(2)}) async-start(bf16[32,1,320,128]{3,2,1,0:T(8,128)(2,1)} %bitcast.95), calls=%async_computation.3 | async-start | bytes 5242880 | tf_op jit(solution)/shard_map/all_to_all | solution.py:252
  303.3 6.5 %copy-start.5 = (bf16[256,768]{0,1:T(8,128)(2,1)S(1)}, bf16[256,768]{0,1:T(8,128)(2,1)}, u32[]{:S(2)}) copy-start(bf16[256,768]{0,1:T(8,128)(2,1)} %copy.99) | copy-start | bytes 1179652
  304.1 13.5 %all-to-all-start.4 = ((bf16[4,256,256]{2,1,0:T(8,128)(2,1)}), bf16[4,256,256]{2,1,0:T(8,128)(2,1)S(1)}, u32[]{:S(2)}, u32[]{:S(2)}) async-start(bf16[4,256,256]{2,1,0:T(8,128)(2,1)} %bitcast.93), calls=%async_computation.4 | async-start | bytes 1048576 | tf_op jit(solution)/shard_map/all_to_all | solution.py:279
Sparse Core Ops, SparseCore 0:
  53.2 103.6 all-gather.1

commit v11 on v7

--- a/solution.py
+++ b/solution.py
@@ -242,9 +242,18 @@
     outgoing_rows = jnp.broadcast_to(picked, (EXPERTS, SPLIT, CAP, columns)).reshape(
         req_total, local_rows, CAP, columns
     )
-    partial_out = expert_apply(
-        lax.all_to_all(outgoing_rows, "req", split_axis=0, concat_axis=0, tiled=True), w_in, w_down
-    )
+    own_index = lax.axis_index("req")
+    shifts = jnp.arange(req_total, dtype=jnp.int32)
+    rolled = jnp.take(outgoing_rows, (own_index + shifts) % req_total, axis=0)
+    arrived = [rolled[0]]
+    for shift in range(1, req_total):
+        arrived.append(
+            lax.ppermute(
+                rolled[shift], "req", [(i, (i + shift) % req_total) for i in range(req_total)]
+            )
+        )
+    partial_out = expert_apply(jnp.stack(arrived, axis=0), w_in, w_down)
+    partial_out = jnp.take(partial_out, (own_index - shifts) % req_total, axis=0)
     returned = lax.all_to_all(
         partial_out.astype(jnp.bfloat16), "req", split_axis=0, concat_axis=0, tiled=True
     ).astype(partial_out.dtype)

time: 303 us -> 479 us (1.58)
  starting transfers between devices: 28.5 us -> 139 us
  waiting for transfers between devices: 103 us -> 192 us
  blocking collectives: 67.9 us -> 27.3 us
  local copies, waits for them, and re-layouts: 42.2 us -> 52.3 us
  other arithmetic: 14.2 us -> 22 us
    ppermute x0 -> x31, waiting for transfers between devices: none -> 102 us  [shards(): lax.ppermute(rolled[shift], 'req', [(i, (i + shift) % req_total) for i in...]
    ppermute x0 -> x31, starting transfers between devices: none -> 74.7 us  [shards(): lax.ppermute(rolled[shift], 'req', [(i, (i + shift) % req_total) for i in...]
    all_to_all x1 -> x0, blocking collectives: 40.6 us -> none  [shards(): lax.all_to_all(outgoing_rows, 'req', split_axis=0, concat_axis=0, tiled=T...]
    all_to_all x1, starting transfers between devices: 5.71 us -> 36.5 us  [shards(): lax.all_to_all(blocks, 'exp', split_axis=0, concat_axis=0, tiled=True)]
    all_to_all x1, waiting for transfers between devices: 27.4 us -> 14.6 us  [shards(): lax.all_to_all(partial_out.astype(jnp.bfloat16), 'req', split_axis=0, con...]
    gather x0 -> x2, local copies, waits for them, and re-layouts: none -> 8.15 us  [the longest x1 4.08 us: shards(): rolled = jnp.take(outgoing_rows, (own_index + shifts) % req_total, axis=0)]
    all_to_all x1, starting transfers between devices: 5.44 us -> 10.4 us  [shards(): lax.all_to_all(partial_out.astype(jnp.bfloat16), 'req', split_axis=0, con...]
    unnamed x30 -> x63, local copies, waits for them, and re-layouts: 11.7 us -> 11.9 us
  transfers between devices with their start and end apart: 5 -> 36, of which waited for: 4 -> 27; matrix products, arithmetic and copies ran while one was open for 15% -> 10% of each run, Pallas kernels for 6% -> 4%
where the time goes in v11:
time: 479 us; the launch traced here: 478 us
  waiting for transfers between devices  192 us (40%)
  starting transfers between devices  139 us (29%)
  local copies, waits for them, and re-layouts  52.3 us (11%)
  blocking collectives  27.3 us (6%)
  other arithmetic  22 us (5%)
  Pallas kernels  16.8 us (4%)
  matrix products  14.7 us (3%)
  between operations  14.5 us (3%)
    ppermute x31, waiting for transfers between devices, shards(): lax.ppermute(rolled[shift], 'req', [(i, (i + shift) % req_total) for i in...  102 us
    ppermute x31, starting transfers between devices, shards(): lax.ppermute(rolled[shift], 'req', [(i, (i + shift) % req_total) for i in...  74.7 us
    all_gather x1, waiting for transfers between devices, shards(): cached = lax.all_gather(owned, 'req', axis=1, tiled=True)  40 us
    all_to_all x1, starting transfers between devices, shards(): lax.all_to_all(blocks, 'exp', split_axis=0, concat_axis=0, tiled=True)  36.5 us
    all_to_all x1, waiting for transfers between devices, shards(): lax.all_to_all(pieces, 'req', split_axis=0, concat_axis=0, tiled=True)  27.8 us
    all_gather x1, blocking collectives, shards(): rows_whole = lax.all_gather(tokens, 'exp', axis=1, tiled=True)  18.8 us
    pallas_call x1, Pallas kernels, attention(): pl.pallas_call(attention_kernel, grid_spec=grid_spec, out_shape=jax.Shape...  16.8 us
    all_to_all x1, waiting for transfers between devices, shards(): lax.all_to_all(partial_out.astype(jnp.bfloat16), 'req', split_axis=0, con...  14.6 us
  transfers between devices with their start and end apart: 36, of which 27 were waited for; matrix products, arithmetic and copies ran while one was open for 10% of the time, Pallas kernels for 4%

profile of v11, /device:TPU:1, one launch (start us, length us, event | category | flops | bytes accessed | tf_op | source)
XLA Modules:
  0.0 478.0 jit_solution(9395791335512565978)
XLA Ops:
  7.2 3.5 copy.259
  10.7 11.5 %all-to-all-start = ((bf16[32,64,2,256]{3,1,2,0:T(8,128)(2,1)}), bf16[32,64,2,256]{3,1,2,0:T(8,128)(2,1)S(1)}, u32[]{:S(2)}, u32[]{:S(2)}) async-start(bf16[32,64,2,256]{3,1,2,0:T(8,128)(2,1)} %copy.259), calls=%async_computation | async-start | bytes 4194304 | tf_op jit(solution)/shard_map/all_to_all | solution.py:213
  22.2 27.8 %all-to-all-done = bf16[32,64,2,256]{3,1,2,0:T(8,128)(2,1)S(1)} async-done(((bf16[32,64,2,256]{3,1,2,0:T(8,128)(2,1)}), bf16[32,64,2,256]{3,1,2,0:T(8,128)(2,1)S(1)}, u32[]{:S(2)}, u32[]{:S(2)}) %all-to-all-start) | async-done | bytes 2097184 | tf_op jit(solution)/shard_map/all_to_all | solution.py:213
  53.1 2.7 broadcast_in_dim.87
  55.8 5.9 %all-to-all-start.1 = ((bf16[4,256,1024]{2,1,0:T(8,128)(2,1)}), bf16[4,256,1024]{2,1,0:T(8,128)(2,1)S(1)}, u32[]{:S(2)}, u32[]{:S(2)}) async-start(bf16[4,256,1024]{2,1,0:T(8,128)(2,1)} %broadcast_in_dim.87), calls=%async_computation.1 | async-start | bytes 4194304 | tf_op jit(solution)/shard_map/all_to_all | solution.py:222
  65.9 3.1 reduce-window.20
  75.8 2.6 copy.253
  78.4 18.8 %all_gather.9 = bf16[256,1024]{1,0:T(8,128)(2,1)S(1)} all-gather(bf16[256,256]{1,0:T(8,128)(2,1)} %param.13), channel_id=1, replica_groups=mesh['req'=32,'exp'=4] {'exp'}, dimensions={1}, use_global_device_ids=true | all-gather | bytes 655360 | tf_op jit(solution)/shard_map/all_gather | solution.py:196
  98.0 2.9 convolution_convert_fusion.1
  100.9 1.9 copy.254
  102.8 1.8 fusion.54
  110.7 2.6 scatter_custom_fusion
  116.8 40.0 %all-gather.2.cloned.1.call-done = bf16[4,2048,2,256]{3,1,2,0:T(8,128)(2,1)} async-done(((bf16[4,64,2,256]{3,1,2,0:T(8,128)(2,1)}), bf16[4,2048,2,256]{3,1,2,0:T(8,128)(2,1)}) %all-gather.2.cloned.1.call-update) | async-done | bytes 8388624 | tf_op jit(solution)/shard_map/all_gather | solution.py:215
  156.9 16.8 %shard_map.140 = bf16[256,256]{1,0:T(8,128)(2,1)} custom-call(s32[4]{0:T(128)} %clamp_bitcast_fusion.group_ref, s32[4]{0:T(128)} %bitcast_subtract_fusion.start_ref, s32[4]{0:T(128)} %bitcast.299, bf16[256,256]{1,0:T(8,128)(2,1)} %bitcast.295, bf16[256,256]{1,0:T(8,128)(2,1)} %bitcast.294, bf16[256,256]{1,0:T(8,128)(2,1)} %bitcast.293, ...), custom_call_target="tpu_custom_call" | custom-call | flops 5171576832 | bytes 8912896 | tf_op jit(solution)/shard_map/pallas_call | solution.py:134
  173.7 8.5 %all_gather.11 = bf16[256,1024]{1,0:T(8,128)(2,1)} all-gather(bf16[256,256]{1,0:T(8,128)(2,1)} %shard_map.140), channel_id=1, replica_groups=mesh['req'=32,'exp'=4] {'exp'}, dimensions={1}, use_global_device_ids=true | all-gather | bytes 655360 | tf_op jit(solution)/shard_map/all_gather | solution.py:220
  182.2 2.0 multiply_reduce_fusion
  186.9 2.8 gather_fusion.1
  189.7 1.9 broadcast_in_dim.98
  191.6 4.1 gather_fusion.2
  195.7 2.0 bitcast_select_fusion.1
  199.0 1.8 collective-permute-start.11
  200.8 5.0 %collective-permute-start.10 = (bf16[1,40,1024]{2,1,0:T(8,128)(2,1)S(1)}, bf16[1,40,1024]{2,1,0:T(8,128)(2,1)S(1)}, u32[]{:S(2)}, u32[]{:S(2)}) collective-permute-start(bf16[1,40,1024]{2,1,0:T(8,128)(2,1)S(1)} %get-tuple-element.34), channel_id=1, source_target_pairs={{0,44},{4,48},{8,52},{12,56},{16,60},{20,64},{24,68},{28,72},{32,7... | collective-permute-start | bytes 245768 | tf_op jit(solution)/shard_map/ppermute | solution.py:251
  207.6 2.4 collective-permute-start.1
  210.0 9.1 %collective-permute-done.1 = bf16[1,40,1024]{2,1,0:T(8,128)(2,1)S(1)} collective-permute-done((bf16[1,40,1024]{2,1,0:T(8,128)(2,1)S(1)}, bf16[1,40,1024]{2,1,0:T(8,128)(2,1)S(1)}, u32[]{:S(2)}, u32[]{:S(2)}) %collective-permute-start.1) | collective-permute-done | bytes 81952 | tf_op jit(solution)/shard_map/ppermute | solution.py:251
  219.2 7.8 %collective-permute-done.2 = bf16[1,40,1024]{2,1,0:T(8,128)(2,1)S(1)} collective-permute-done((bf16[1,40,1024]{2,1,0:T(8,128)(2,1)S(1)}, bf16[1,40,1024]{2,1,0:T(8,128)(2,1)S(1)}, u32[]{:S(2)}, u32[]{:S(2)}) %collective-permute-start.2) | collective-permute-done | bytes 81952 | tf_op jit(solution)/shard_map/ppermute | solution.py:251
  227.0 6.9 %collective-permute-done.3 = bf16[1,40,1024]{2,1,0:T(8,128)(2,1)S(1)} collective-permute-done((bf16[1,40,1024]{2,1,0:T(8,128)(2,1)S(1)}, bf16[1,40,1024]{2,1,0:T(8,128)(2,1)S(1)}, u32[]{:S(2)}, u32[]{:S(2)}) %collective-permute-start.3) | collective-permute-done | bytes 81952 | tf_op jit(solution)/shard_map/ppermute | solution.py:251
  233.9 6.6 %collective-permute-done.4 = bf16[1,40,1024]{2,1,0:T(8,128)(2,1)S(1)} collective-permute-done((bf16[1,40,1024]{2,1,0:T(8,128)(2,1)S(1)}, bf16[1,40,1024]{2,1,0:T(8,128)(2,1)S(1)}, u32[]{:S(2)}, u32[]{:S(2)}) %collective-permute-start.4) | collective-permute-done | bytes 81952 | tf_op jit(solution)/shard_map/ppermute | solution.py:251
  240.9 6.5 %collective-permute-done.5 = bf16[1,40,1024]{2,1,0:T(8,128)(2,1)S(1)} collective-permute-done((bf16[1,40,1024]{2,1,0:T(8,128)(2,1)S(1)}, bf16[1,40,1024]{2,1,0:T(8,128)(2,1)S(1)}, u32[]{:S(2)}, u32[]{:S(2)}) %collective-permute-start.5) | collective-permute-done | bytes 81952 | tf_op jit(solution)/shard_map/ppermute | solution.py:251
  247.4 1.9 collective-permute-start.6
  249.3 3.8 collective-permute-done.6
  253.1 4.5 collective-permute-done.7
  257.6 3.2 collective-permute-start.30
  260.9 2.9 collective-permute-start.28
  264.1 6.5 %collective-permute-start.12 = (bf16[1,40,1024]{2,1,0:T(8,128)(2,1)S(1)}, bf16[1,40,1024]{2,1,0:T(8,128)(2,1)S(1)}, u32[]{:S(2)}, u32[]{:S(2)}) collective-permute-start(bf16[1,40,1024]{2,1,0:T(8,128)(2,1)S(1)} %get-tuple-element.32), channel_id=1, source_target_pairs={{0,52},{4,56},{8,60},{12,64},{16,68},{20,72},{24,76},{28,80},{32,8... | collective-permute-start | bytes 245768 | tf_op jit(solution)/shard_map/ppermute | solution.py:251
  272.1 3.7 collective-permute-start.13
  275.8 3.8 collective-permute-done.13
  279.6 3.5 collective-permute-start.14
  283.1 3.7 collective-permute-done.14
  287.6 4.3 collective-permute-done.15
  292.0 3.4 collective-permute-start.16
  295.4 5.0 %collective-permute-done.16 = bf16[1,40,1024]{2,1,0:T(8,128)(2,1)S(1)} collective-permute-done((bf16[1,40,1024]{2,1,0:T(8,128)(2,1)S(1)}, bf16[1,40,1024]{2,1,0:T(8,128)(2,1)S(1)}, u32[]{:S(2)}, u32[]{:S(2)}) %collective-permute-start.16) | collective-permute-done | bytes 81952 | tf_op jit(solution)/shard_map/ppermute | solution.py:251
  300.4 3.3 collective-permute-start.17
  303.7 4.8 %collective-permute-done.17 = bf16[1,40,1024]{2,1,0:T(8,128)(2,1)S(1)} collective-permute-done((bf16[1,40,1024]{2,1,0:T(8,128)(2,1)S(1)}, bf16[1,40,1024]{2,1,0:T(8,128)(2,1)S(1)}, u32[]{:S(2)}, u32[]{:S(2)}) %collective-permute-start.17) | collective-permute-done | bytes 81952 | tf_op jit(solution)/shard_map/ppermute | solution.py:251
  308.5 4.4 collective-permute-start.18
  312.9 2.5 collective-permute-done.18
  315.4 8.1 %collective-permute-start.19 = (bf16[1,40,1024]{2,1,0:T(8,128)(2,1)S(1)}, bf16[1,40,1024]{2,1,0:T(8,128)(2,1)S(1)}, u32[]{:S(2)}, u32[]{:S(2)}) collective-permute-start(bf16[1,40,1024]{2,1,0:T(8,128)(2,1)S(1)} %get-tuple-element.25), channel_id=1, source_target_pairs={{0,80},{4,84},{8,88},{12,92},{16,96},{20,100},{24,104},{28,108},{3... | collective-permute-start | bytes 245768 | tf_op jit(solution)/shard_map/ppermute | solution.py:251
  325.1 1.8 collective-permute-start.20
  326.8 3.6 collective-permute-done.20
  330.5 4.2 collective-permute-start.21
  336.2 9.1 %collective-permute-start.22 = (bf16[1,40,1024]{2,1,0:T(8,128)(2,1)S(1)}, bf16[1,40,1024]{2,1,0:T(8,128)(2,1)S(1)}, u32[]{:S(2)}, u32[]{:S(2)}) collective-permute-start(bf16[1,40,1024]{2,1,0:T(8,128)(2,1)S(1)} %get-tuple-element.22), channel_id=1, source_target_pairs={{0,92},{4,96},{8,100},{12,104},{16,108},{20,112},{24,116},{28,120}... | collective-permute-start | bytes 245768 | tf_op jit(solution)/shard_map/ppermute | solution.py:251
  346.7 5.1 %collective-permute-start.23 = (bf16[1,40,1024]{2,1,0:T(8,128)(2,1)S(1)}, bf16[1,40,1024]{2,1,0:T(8,128)(2,1)S(1)}, u32[]{:S(2)}, u32[]{:S(2)}) collective-permute-start(bf16[1,40,1024]{2,1,0:T(8,128)(2,1)S(1)} %get-tuple-element.21), channel_id=1, source_target_pairs={{0,96},{4,100},{8,104},{12,108},{16,112},{20,116},{24,120},{28,124... | collective-permute-start | bytes 245768 | tf_op jit(solution)/shard_map/ppermute | solution.py:251
  353.3 8.7 %collective-permute-done.24 = bf16[1,40,1024]{2,1,0:T(8,128)(2,1)S(1)} collective-permute-done((bf16[1,40,1024]{2,1,0:T(8,128)(2,1)S(1)}, bf16[1,40,1024]{2,1,0:T(8,128)(2,1)S(1)}, u32[]{:S(2)}, u32[]{:S(2)}) %collective-permute-start.24) | collective-permute-done | bytes 81952 | tf_op jit(solution)/shard_map/ppermute | solution.py:251
  362.1 7.2 %collective-permute-done.25 = bf16[1,40,1024]{2,1,0:T(8,128)(2,1)S(1)} collective-permute-done((bf16[1,40,1024]{2,1,0:T(8,128)(2,1)S(1)}, bf16[1,40,1024]{2,1,0:T(8,128)(2,1)S(1)}, u32[]{:S(2)}, u32[]{:S(2)}) %collective-permute-start.25) | collective-permute-done | bytes 81952 | tf_op jit(solution)/shard_map/ppermute | solution.py:251
  369.6 5.4 %collective-permute-done.26 = bf16[1,40,1024]{2,1,0:T(8,128)(2,1)S(1)} collective-permute-done((bf16[1,40,1024]{2,1,0:T(8,128)(2,1)S(1)}, bf16[1,40,1024]{2,1,0:T(8,128)(2,1)S(1)}, u32[]{:S(2)}, u32[]{:S(2)}) %collective-permute-start.26) | collective-permute-done | bytes 81952 | tf_op jit(solution)/shard_map/ppermute | solution.py:251
  375.1 2.3 fusion.7
  377.4 3.3 fusion.23
  380.7 4.1 gather_fusion.3
  384.8 4.1 fusion.1
  388.9 10.4 %all-to-all-start.2 = ((bf16[32,1,40,1024]{3,2,1,0:T(8,128)(2,1)}), bf16[32,1,40,1024]{3,2,1,0:T(8,128)(2,1)}, u32[]{:S(2)}, u32[]{:S(2)}) async-start(bf16[32,1,40,1024]{3,2,1,0:T(8,128)(2,1)} %fusion.1), calls=%async_computation.2 | async-start | bytes 5242880 | tf_op jit(solution)/shard_map/all_to_all | solution.py:257
  400.1 4.6 gather_fusion.4
  405.6 14.6 %all-to-all-done.2 = bf16[32,1,40,1024]{3,2,1,0:T(8,128)(2,1)} async-done(((bf16[32,1,40,1024]{3,2,1,0:T(8,128)(2,1)}), bf16[32,1,40,1024]{3,2,1,0:T(8,128)(2,1)}, u32[]{:S(2)}, u32[]{:S(2)}) %all-to-all-start.2) | async-done | bytes 2621472 | tf_op jit(solution)/shard_map/all_to_all | solution.py:257
  420.3 4.0 convolution_convert_fusion
  425.1 36.5 %all-to-all-start.3 = ((bf16[4,256,256]{2,1,0:T(8,128)(2,1)}), bf16[4,256,256]{2,1,0:T(8,128)(2,1)S(1)}, u32[]{:S(2)}, u32[]{:S(2)}) async-start(bf16[4,256,256]{2,1,0:T(8,128)(2,1)} %bitcast.283), calls=%async_computation.3 | async-start | bytes 1048576 | tf_op jit(solution)/shard_map/all_to_all | solution.py:277
  462.5 7.0 %all-to-all-done.3 = bf16[4,256,256]{2,1,0:T(8,128)(2,1)S(1)} async-done(((bf16[4,256,256]{2,1,0:T(8,128)(2,1)}), bf16[4,256,256]{2,1,0:T(8,128)(2,1)S(1)}, u32[]{:S(2)}, u32[]{:S(2)}) %all-to-all-start.3) | async-done | bytes 524320 | tf_op jit(solution)/shard_map/all_to_all | solution.py:277
  (145 shorter events, 45.0 us)
Async XLA Ops:
  7.2 367.9 %copy-start = (bf16[1,1024,2,352]{1,3,2,0:T(8,128)(2,1)S(1)}, bf16[1,1024,2,352]{1,3,2,0:T(8,128)(2,1)}, u32[]{:S(2)}) copy-start(bf16[1,1024,2,352]{1,3,2,0:T(8,128)(2,1)} %param.24) | copy-start | bytes 4325380
  10.7 11.5 %copy-start.11 = (s32[4]{0:T(128)S(1)}, s32[4]{0:T(128)}, u32[]{:S(2)}) copy-start(s32[4]{0:T(128)} %param.16) | copy-start | bytes 52
  10.7 39.4 %all-to-all-start = ((bf16[32,64,2,256]{3,1,2,0:T(8,128)(2,1)}), bf16[32,64,2,256]{3,1,2,0:T(8,128)(2,1)S(1)}, u32[]{:S(2)}, u32[]{:S(2)}) async-start(bf16[32,64,2,256]{3,1,2,0:T(8,128)(2,1)} %copy.259), calls=%async_computation | async-start | bytes 4194304 | tf_op jit(solution)/shard_map/all_to_all | solution.py:213
  22.1 134.7 %all-gather.2.cloned.1.call-start = ((), (), s32[]{:S(2)}) async-start(), calls=%async_computation.4 | async-start | bytes 8650752 | tf_op jit(solution)/shard_map/all_gather | solution.py:215
  55.8 5.9 %copy-start.6 = (s32[256,2]{0,1:T(2,128)S(1)}, s32[256,2]{0,1:T(2,128)}, u32[]{:S(2)}) copy-start(s32[256,2]{0,1:T(2,128)} %param.23) | copy-start | bytes 6148
  55.8 8.8 %copy-start.12 = (s32[1,4]{1,0:T(1,128)S(1)}, s32[1,4]{1,0:T(1,128)}, u32[]{:S(2)}) copy-start(s32[1,4]{1,0:T(1,128)} %param.14) | copy-start | bytes 52
  55.8 126.4 %all-to-all-start.1 = ((bf16[4,256,1024]{2,1,0:T(8,128)(2,1)}), bf16[4,256,1024]{2,1,0:T(8,128)(2,1)S(1)}, u32[]{:S(2)}, u32[]{:S(2)}) async-start(bf16[4,256,1024]{2,1,0:T(8,128)(2,1)} %broadcast_in_dim.87), calls=%async_computation.1 | async-start | bytes 4194304 | tf_op jit(solution)/shard_map/all_to_all | solution.py:222
  97.2 0.8 copy-start.2
  184.2 1.0 copy-start.1
  186.0 0.8 copy-start.3
  191.6 4.1 copy-start.9
  198.0 9.6 %collective-permute-start = (bf16[1,40,1024]{2,1,0:T(8,128)(2,1)S(1)}, bf16[1,40,1024]{2,1,0:T(8,128)(2,1)S(1)}, u32[]{:S(2)}, u32[]{:S(2)}) collective-permute-start(bf16[1,40,1024]{2,1,0:T(8,128)(2,1)S(1)} %get-tuple-element.44), channel_id=1, source_target_pairs={{0,4},{4,8},{8,12},{12,16},{16,20},{20,24},{24,28},{28,32},{32,36}... | collective-permute-start | bytes 245768 | tf_op jit(solution)/shard_map/ppermute | solution.py:251
  199.0 65.1 %collective-permute-start.11 = (bf16[1,40,1024]{2,1,0:T(8,128)(2,1)S(1)}, bf16[1,40,1024]{2,1,0:T(8,128)(2,1)S(1)}, u32[]{:S(2)}, u32[]{:S(2)}) collective-permute-start(bf16[1,40,1024]{2,1,0:T(8,128)(2,1)S(1)} %get-tuple-element.33), channel_id=1, source_target_pairs={{0,48},{4,52},{8,56},{12,60},{16,64},{20,68},{24,72},{28,76},{32,8... | collective-permute-start | bytes 245768 | tf_op jit(solution)/shard_map/ppermute | solution.py:251
  200.8 63.1 %collective-permute-start.10 = (bf16[1,40,1024]{2,1,0:T(8,128)(2,1)S(1)}, bf16[1,40,1024]{2,1,0:T(8,128)(2,1)S(1)}, u32[]{:S(2)}, u32[]{:S(2)}) collective-permute-start(bf16[1,40,1024]{2,1,0:T(8,128)(2,1)S(1)} %get-tuple-element.34), channel_id=1, source_target_pairs={{0,44},{4,48},{8,52},{12,56},{16,60},{20,64},{24,68},{28,72},{32,7... | collective-permute-start | bytes 245768 | tf_op jit(solution)/shard_map/ppermute | solution.py:251
  205.8 55.1 %collective-permute-start.9 = (bf16[1,40,1024]{2,1,0:T(8,128)(2,1)S(1)}, bf16[1,40,1024]{2,1,0:T(8,128)(2,1)S(1)}, u32[]{:S(2)}, u32[]{:S(2)}) collective-permute-start(bf16[1,40,1024]{2,1,0:T(8,128)(2,1)S(1)} %get-tuple-element.35), channel_id=1, source_target_pairs={{0,40},{4,44},{8,48},{12,52},{16,56},{20,60},{24,64},{28,68},{32,7... | collective-permute-start | bytes 245768 | tf_op jit(solution)/shard_map/ppermute | solution.py:251
  206.6 54.2 %collective-permute-start.8 = (bf16[1,40,1024]{2,1,0:T(8,128)(2,1)S(1)}, bf16[1,40,1024]{2,1,0:T(8,128)(2,1)S(1)}, u32[]{:S(2)}, u32[]{:S(2)}) collective-permute-start(bf16[1,40,1024]{2,1,0:T(8,128)(2,1)S(1)} %get-tuple-element.36), channel_id=1, source_target_pairs={{0,36},{4,40},{8,44},{12,48},{16,52},{20,56},{24,60},{28,64},{32,6... | collective-permute-start | bytes 245768 | tf_op jit(solution)/shard_map/ppermute | solution.py:251
  207.6 11.6 %collective-permute-start.1 = (bf16[1,40,1024]{2,1,0:T(8,128)(2,1)S(1)}, bf16[1,40,1024]{2,1,0:T(8,128)(2,1)S(1)}, u32[]{:S(2)}, u32[]{:S(2)}) collective-permute-start(bf16[1,40,1024]{2,1,0:T(8,128)(2,1)S(1)} %get-tuple-element.43), channel_id=1, source_target_pairs={{0,8},{4,12},{8,16},{12,20},{16,24},{20,28},{24,32},{28,36},{32,40... | collective-permute-start | bytes 245768 | tf_op jit(solution)/shard_map/ppermute | solution.py:251
  219.2 7.8 %collective-permute-start.2 = (bf16[1,40,1024]{2,1,0:T(8,128)(2,1)S(1)}, bf16[1,40,1024]{2,1,0:T(8,128)(2,1)S(1)}, u32[]{:S(2)}, u32[]{:S(2)}) collective-permute-start(bf16[1,40,1024]{2,1,0:T(8,128)(2,1)S(1)} %get-tuple-element.42), channel_id=1, source_target_pairs={{0,12},{4,16},{8,20},{12,24},{16,28},{20,32},{24,36},{28,40},{32,4... | collective-permute-start | bytes 245768 | tf_op jit(solution)/shard_map/ppermute | solution.py:251
  227.0 6.9 %collective-permute-start.3 = (bf16[1,40,1024]{2,1,0:T(8,128)(2,1)S(1)}, bf16[1,40,1024]{2,1,0:T(8,128)(2,1)S(1)}, u32[]{:S(2)}, u32[]{:S(2)}) collective-permute-start(bf16[1,40,1024]{2,1,0:T(8,128)(2,1)S(1)} %get-tuple-element.41), channel_id=1, source_target_pairs={{0,16},{4,20},{8,24},{12,28},{16,32},{20,36},{24,40},{28,44},{32,4... | collective-permute-start | bytes 245768 | tf_op jit(solution)/shard_map/ppermute | solution.py:251
  233.9 6.6 %collective-permute-start.4 = (bf16[1,40,1024]{2,1,0:T(8,128)(2,1)S(1)}, bf16[1,40,1024]{2,1,0:T(8,128)(2,1)S(1)}, u32[]{:S(2)}, u32[]{:S(2)}) collective-permute-start(bf16[1,40,1024]{2,1,0:T(8,128)(2,1)S(1)} %get-tuple-element.40), channel_id=1, source_target_pairs={{0,20},{4,24},{8,28},{12,32},{16,36},{20,40},{24,44},{28,48},{32,5... | collective-permute-start | bytes 245768 | tf_op jit(solution)/shard_map/ppermute | solution.py:251
  240.5 6.9 %collective-permute-start.5 = (bf16[1,40,1024]{2,1,0:T(8,128)(2,1)S(1)}, bf16[1,40,1024]{2,1,0:T(8,128)(2,1)S(1)}, u32[]{:S(2)}, u32[]{:S(2)}) collective-permute-start(bf16[1,40,1024]{2,1,0:T(8,128)(2,1)S(1)} %get-tuple-element.39), channel_id=1, source_target_pairs={{0,24},{4,28},{8,32},{12,36},{16,40},{20,44},{24,48},{28,52},{32,5... | collective-permute-start | bytes 245768 | tf_op jit(solution)/shard_map/ppermute | solution.py:251
  247.4 5.7 %collective-permute-start.6 = (bf16[1,40,1024]{2,1,0:T(8,128)(2,1)S(1)}, bf16[1,40,1024]{2,1,0:T(8,128)(2,1)S(1)}, u32[]{:S(2)}, u32[]{:S(2)}) collective-permute-start(bf16[1,40,1024]{2,1,0:T(8,128)(2,1)S(1)} %get-tuple-element.38), channel_id=1, source_target_pairs={{0,28},{4,32},{8,36},{12,40},{16,44},{20,48},{24,52},{28,56},{32,6... | collective-permute-start | bytes 245768 | tf_op jit(solution)/shard_map/ppermute | solution.py:251
  253.1 4.5 collective-permute-start.7
  257.6 117.5 %collective-permute-start.30 = (bf16[1,40,1024]{2,1,0:T(8,128)(2,1)S(1)}, bf16[1,40,1024]{2,1,0:T(8,128)(2,1)S(1)}, u32[]{:S(2)}, u32[]{:S(2)}) collective-permute-start(bf16[1,40,1024]{2,1,0:T(8,128)(2,1)S(1)} %get-tuple-element.14), channel_id=1, source_target_pairs={{0,124},{4,0},{8,4},{12,8},{16,12},{20,16},{24,20},{28,24},{32,28}... | collective-permute-start | bytes 245768 | tf_op jit(solution)/shard_map/ppermute | solution.py:251
  260.8 114.2 %collective-permute-start.29 = (bf16[1,40,1024]{2,1,0:T(8,128)(2,1)S(1)}, bf16[1,40,1024]{2,1,0:T(8,128)(2,1)S(1)}, u32[]{:S(2)}, u32[]{:S(2)}) collective-permute-start(bf16[1,40,1024]{2,1,0:T(8,128)(2,1)S(1)} %get-tuple-element.15), channel_id=1, source_target_pairs={{0,120},{4,124},{8,0},{12,4},{16,8},{20,12},{24,16},{28,20},{32,24... | collective-permute-start | bytes 245768 | tf_op jit(solution)/shard_map/ppermute | solution.py:251
  260.9 114.1 %collective-permute-start.28 = (bf16[1,40,1024]{2,1,0:T(8,128)(2,1)S(1)}, bf16[1,40,1024]{2,1,0:T(8,128)(2,1)S(1)}, u32[]{:S(2)}, u32[]{:S(2)}) collective-permute-start(bf16[1,40,1024]{2,1,0:T(8,128)(2,1)S(1)} %get-tuple-element.16), channel_id=1, source_target_pairs={{0,116},{4,120},{8,124},{12,0},{16,4},{20,8},{24,12},{28,16},{32,2... | collective-permute-start | bytes 245768 | tf_op jit(solution)/shard_map/ppermute | solution.py:251
  263.8 111.2 %collective-permute-start.27 = (bf16[1,40,1024]{2,1,0:T(8,128)(2,1)S(1)}, bf16[1,40,1024]{2,1,0:T(8,128)(2,1)S(1)}, u32[]{:S(2)}, u32[]{:S(2)}) collective-permute-start(bf16[1,40,1024]{2,1,0:T(8,128)(2,1)S(1)} %get-tuple-element.17), channel_id=1, source_target_pairs={{0,112},{4,116},{8,120},{12,124},{16,0},{20,4},{24,8},{28,12},{32,... | collective-permute-start | bytes 245768 | tf_op jit(solution)/shard_map/ppermute | solution.py:251
  264.1 8.0 %collective-permute-start.12 = (bf16[1,40,1024]{2,1,0:T(8,128)(2,1)S(1)}, bf16[1,40,1024]{2,1,0:T(8,128)(2,1)S(1)}, u32[]{:S(2)}, u32[]{:S(2)}) collective-permute-start(bf16[1,40,1024]{2,1,0:T(8,128)(2,1)S(1)} %get-tuple-element.32), channel_id=1, source_target_pairs={{0,52},{4,56},{8,60},{12,64},{16,68},{20,72},{24,76},{28,80},{32,8... | collective-permute-start | bytes 245768 | tf_op jit(solution)/shard_map/ppermute | solution.py:251
  272.1 7.4 %collective-permute-start.13 = (bf16[1,40,1024]{2,1,0:T(8,128)(2,1)S(1)}, bf16[1,40,1024]{2,1,0:T(8,128)(2,1)S(1)}, u32[]{:S(2)}, u32[]{:S(2)}) collective-permute-start(bf16[1,40,1024]{2,1,0:T(8,128)(2,1)S(1)} %get-tuple-element.31), channel_id=1, source_target_pairs={{0,56},{4,60},{8,64},{12,68},{16,72},{20,76},{24,80},{28,84},{32,8... | collective-permute-start | bytes 245768 | tf_op jit(solution)/shard_map/ppermute | solution.py:251
  279.6 7.2 %collective-permute-start.14 = (bf16[1,40,1024]{2,1,0:T(8,128)(2,1)S(1)}, bf16[1,40,1024]{2,1,0:T(8,128)(2,1)S(1)}, u32[]{:S(2)}, u32[]{:S(2)}) collective-permute-start(bf16[1,40,1024]{2,1,0:T(8,128)(2,1)S(1)} %get-tuple-element.30), channel_id=1, source_target_pairs={{0,60},{4,64},{8,68},{12,72},{16,76},{20,80},{24,84},{28,88},{32,9... | collective-permute-start | bytes 245768 | tf_op jit(solution)/shard_map/ppermute | solution.py:251
  286.7 5.3 %collective-permute-start.15 = (bf16[1,40,1024]{2,1,0:T(8,128)(2,1)S(1)}, bf16[1,40,1024]{2,1,0:T(8,128)(2,1)S(1)}, u32[]{:S(2)}, u32[]{:S(2)}) collective-permute-start(bf16[1,40,1024]{2,1,0:T(8,128)(2,1)S(1)} %get-tuple-element.29), channel_id=1, source_target_pairs={{0,64},{4,68},{8,72},{12,76},{16,80},{20,84},{24,88},{28,92},{32,9... | collective-permute-start | bytes 245768 | tf_op jit(solution)/shard_map/ppermute | solution.py:251
  292.0 8.5 %collective-permute-start.16 = (bf16[1,40,1024]{2,1,0:T(8,128)(2,1)S(1)}, bf16[1,40,1024]{2,1,0:T(8,128)(2,1)S(1)}, u32[]{:S(2)}, u32[]{:S(2)}) collective-permute-start(bf16[1,40,1024]{2,1,0:T(8,128)(2,1)S(1)} %get-tuple-element.28), channel_id=1, source_target_pairs={{0,68},{4,72},{8,76},{12,80},{16,84},{20,88},{24,92},{28,96},{32,1... | collective-permute-start | bytes 245768 | tf_op jit(solution)/shard_map/ppermute | solution.py:251
  300.4 8.1 %collective-permute-start.17 = (bf16[1,40,1024]{2,1,0:T(8,128)(2,1)S(1)}, bf16[1,40,1024]{2,1,0:T(8,128)(2,1)S(1)}, u32[]{:S(2)}, u32[]{:S(2)}) collective-permute-start(bf16[1,40,1024]{2,1,0:T(8,128)(2,1)S(1)} %get-tuple-element.27), channel_id=1, source_target_pairs={{0,72},{4,76},{8,80},{12,84},{16,88},{20,92},{24,96},{28,100},{32,... | collective-permute-start | bytes 245768 | tf_op jit(solution)/shard_map/ppermute | solution.py:251
  308.5 6.9 %collective-permute-start.18 = (bf16[1,40,1024]{2,1,0:T(8,128)(2,1)S(1)}, bf16[1,40,1024]{2,1,0:T(8,128)(2,1)S(1)}, u32[]{:S(2)}, u32[]{:S(2)}) collective-permute-start(bf16[1,40,1024]{2,1,0:T(8,128)(2,1)S(1)} %get-tuple-element.26), channel_id=1, source_target_pairs={{0,76},{4,80},{8,84},{12,88},{16,92},{20,96},{24,100},{28,104},{32... | collective-permute-start | bytes 245768 | tf_op jit(solution)/shard_map/ppermute | solution.py:251
  315.4 9.6 %collective-permute-start.19 = (bf16[1,40,1024]{2,1,0:T(8,128)(2,1)S(1)}, bf16[1,40,1024]{2,1,0:T(8,128)(2,1)S(1)}, u32[]{:S(2)}, u32[]{:S(2)}) collective-permute-start(bf16[1,40,1024]{2,1,0:T(8,128)(2,1)S(1)} %get-tuple-element.25), channel_id=1, source_target_pairs={{0,80},{4,84},{8,88},{12,92},{16,96},{20,100},{24,104},{28,108},{3... | collective-permute-start | bytes 245768 | tf_op jit(solution)/shard_map/ppermute | solution.py:251
  325.1 5.4 %collective-permute-start.20 = (bf16[1,40,1024]{2,1,0:T(8,128)(2,1)S(1)}, bf16[1,40,1024]{2,1,0:T(8,128)(2,1)S(1)}, u32[]{:S(2)}, u32[]{:S(2)}) collective-permute-start(bf16[1,40,1024]{2,1,0:T(8,128)(2,1)S(1)} %get-tuple-element.24), channel_id=1, source_target_pairs={{0,84},{4,88},{8,92},{12,96},{16,100},{20,104},{24,108},{28,112},{... | collective-permute-start | bytes 245768 | tf_op jit(solution)/shard_map/ppermute | solution.py:251
  330.5 5.7 %collective-permute-start.21 = (bf16[1,40,1024]{2,1,0:T(8,128)(2,1)S(1)}, bf16[1,40,1024]{2,1,0:T(8,128)(2,1)S(1)}, u32[]{:S(2)}, u32[]{:S(2)}) collective-permute-start(bf16[1,40,1024]{2,1,0:T(8,128)(2,1)S(1)} %get-tuple-element.23), channel_id=1, source_target_pairs={{0,88},{4,92},{8,96},{12,100},{16,104},{20,108},{24,112},{28,116},... | collective-permute-start | bytes 245768 | tf_op jit(solution)/shard_map/ppermute | solution.py:251
  336.2 10.5 %collective-permute-start.22 = (bf16[1,40,1024]{2,1,0:T(8,128)(2,1)S(1)}, bf16[1,40,1024]{2,1,0:T(8,128)(2,1)S(1)}, u32[]{:S(2)}, u32[]{:S(2)}) collective-permute-start(bf16[1,40,1024]{2,1,0:T(8,128)(2,1)S(1)} %get-tuple-element.22), channel_id=1, source_target_pairs={{0,92},{4,96},{8,100},{12,104},{16,108},{20,112},{24,116},{28,120}... | collective-permute-start | bytes 245768 | tf_op jit(solution)/shard_map/ppermute | solution.py:251
  346.7 6.6 %collective-permute-start.23 = (bf16[1,40,1024]{2,1,0:T(8,128)(2,1)S(1)}, bf16[1,40,1024]{2,1,0:T(8,128)(2,1)S(1)}, u32[]{:S(2)}, u32[]{:S(2)}) collective-permute-start(bf16[1,40,1024]{2,1,0:T(8,128)(2,1)S(1)} %get-tuple-element.21), channel_id=1, source_target_pairs={{0,96},{4,100},{8,104},{12,108},{16,112},{20,116},{24,120},{28,124... | collective-permute-start | bytes 245768 | tf_op jit(solution)/shard_map/ppermute | solution.py:251
  353.3 8.7 %collective-permute-start.24 = (bf16[1,40,1024]{2,1,0:T(8,128)(2,1)S(1)}, bf16[1,40,1024]{2,1,0:T(8,128)(2,1)S(1)}, u32[]{:S(2)}, u32[]{:S(2)}) collective-permute-start(bf16[1,40,1024]{2,1,0:T(8,128)(2,1)S(1)} %get-tuple-element.20), channel_id=1, source_target_pairs={{0,100},{4,104},{8,108},{12,112},{16,116},{20,120},{24,124},{28,0}... | collective-permute-start | bytes 245768 | tf_op jit(solution)/shard_map/ppermute | solution.py:251
  362.1 7.2 %collective-permute-start.25 = (bf16[1,40,1024]{2,1,0:T(8,128)(2,1)S(1)}, bf16[1,40,1024]{2,1,0:T(8,128)(2,1)S(1)}, u32[]{:S(2)}, u32[]{:S(2)}) collective-permute-start(bf16[1,40,1024]{2,1,0:T(8,128)(2,1)S(1)} %get-tuple-element.19), channel_id=1, source_target_pairs={{0,104},{4,108},{8,112},{12,116},{16,120},{20,124},{24,0},{28,4},{... | collective-permute-start | bytes 245768 | tf_op jit(solution)/shard_map/ppermute | solution.py:251
  369.3 5.7 %collective-permute-start.26 = (bf16[1,40,1024]{2,1,0:T(8,128)(2,1)S(1)}, bf16[1,40,1024]{2,1,0:T(8,128)(2,1)S(1)}, u32[]{:S(2)}, u32[]{:S(2)}) collective-permute-start(bf16[1,40,1024]{2,1,0:T(8,128)(2,1)S(1)} %get-tuple-element.18), channel_id=1, source_target_pairs={{0,108},{4,112},{8,116},{12,120},{16,124},{20,0},{24,4},{28,8},{32... | collective-permute-start | bytes 245768 | tf_op jit(solution)/shard_map/ppermute | solution.py:251
  375.1 2.3 copy-start.10
  380.7 4.1 copy-start.8
  388.9 11.0 %copy-start.4 = (bf16[256,1024]{1,0:T(8,128)(2,1)S(1)}, bf16[256,1024]{1,0:T(8,128)(2,1)}, u32[]{:S(2)}) copy-start(bf16[256,1024]{1,0:T(8,128)(2,1)} %copy-done.3) | copy-start | bytes 1572868
  388.9 11.0 %copy-start.7 = (bf16[1024,16]{0,1:T(8,128)(2,1)S(1)}, bf16[1024,16]{0,1:T(8,128)(2,1)}, u32[]{:S(2)}) copy-start(bf16[1024,16]{0,1:T(8,128)(2,1)} %param.22) | copy-start | bytes 98308
  388.9 31.4 %all-to-all-start.2 = ((bf16[32,1,40,1024]{3,2,1,0:T(8,128)(2,1)}), bf16[32,1,40,1024]{3,2,1,0:T(8,128)(2,1)}, u32[]{:S(2)}, u32[]{:S(2)}) async-start(bf16[32,1,40,1024]{3,2,1,0:T(8,128)(2,1)} %fusion.1), calls=%async_computation.2 | async-start | bytes 5242880 | tf_op jit(solution)/shard_map/all_to_all | solution.py:257
  420.3 41.3 %copy-start.5 = (bf16[256,768]{0,1:T(8,128)(2,1)S(1)}, bf16[256,768]{0,1:T(8,128)(2,1)}, u32[]{:S(2)}) copy-start(bf16[256,768]{0,1:T(8,128)(2,1)} %copy.254) | copy-start | bytes 1179652
  425.1 44.3 %all-to-all-start.3 = ((bf16[4,256,256]{2,1,0:T(8,128)(2,1)}), bf16[4,256,256]{2,1,0:T(8,128)(2,1)S(1)}, u32[]{:S(2)}, u32[]{:S(2)}) async-start(bf16[4,256,256]{2,1,0:T(8,128)(2,1)} %bitcast.283), calls=%async_computation.3 | async-start | bytes 1048576 | tf_op jit(solution)/shard_map/all_to_all | solution.py:277
Sparse Core Ops, SparseCore 0:
  53.2 103.5 all-gather.1

commit v12 on v7

--- a/solution.py
+++ b/solution.py
@@ -258,7 +258,7 @@
     mixture = jnp.dot(
         selection,
         returned.reshape(block_count * CAP, out_columns).astype(jnp.float32),
-        precision=lax.Precision.HIGHEST,
+        precision=lax.Precision.HIGH,
         preferred_element_type=jnp.float32,
     )
     blocks = jnp.transpose(

time: 303 us -> 302 us (level)
  no operation moved by 1% of the time
where the time goes in v12:
time: 302 us; the launch traced here: 301 us
  waiting for transfers between devices  103 us (34%)
  blocking collectives  67.9 us (22%)
  local copies, waits for them, and re-layouts  42.2 us (14%)
  starting transfers between devices  28.5 us (9%)
  Pallas kernels  16.8 us (6%)
  between operations  14.3 us (5%)
  other arithmetic  14.2 us (5%)
  matrix products  14 us (5%)
    all_gather x1, waiting for transfers between devices, shards(): cached = lax.all_gather(owned, 'req', axis=1, tiled=True)  41.1 us
    all_to_all x1, blocking collectives, shards(): lax.all_to_all(outgoing_rows, 'req', split_axis=0, concat_axis=0, tiled=T...  40.6 us
    all_to_all x1, waiting for transfers between devices, shards(): lax.all_to_all(pieces, 'req', split_axis=0, concat_axis=0, tiled=True)  27.8 us
    all_to_all x1, waiting for transfers between devices, shards(): lax.all_to_all(partial_out.astype(jnp.bfloat16), 'req', split_axis=0, con...  27.4 us
    all_gather x1, blocking collectives, shards(): rows_whole = lax.all_gather(tokens, 'exp', axis=1, tiled=True)  18.8 us
    pallas_call x1, Pallas kernels, attention(): pl.pallas_call(attention_kernel, grid_spec=grid_spec, out_shape=jax.Shape...  16.8 us
    unnamed x30, local copies, waits for them, and re-layouts  11.7 us
    all_to_all x1, starting transfers between devices, shards(): lax.all_to_all(pieces, 'req', split_axis=0, concat_axis=0, tiled=True)  11.5 us
  transfers between devices with their start and end apart: 5, of which 4 were waited for; matrix products, arithmetic and copies ran while one was open for 15% of the time, Pallas kernels for 6%

profile of v12, /device:TPU:1, one launch (start us, length us, event | category | flops | bytes accessed | tf_op | source)
XLA Modules:
  0.0 301.1 jit_solution(4710863570318245658)
XLA Ops:
  7.2 3.5 %copy.104 = bf16[32,64,2,256]{3,1,2,0:T(8,128)(2,1)} copy(bf16[32,64,2,256]{3,2,1,0:T(2,128)(2,1)} %bitcast.96) | data formatting | bytes 4194304 | tf_op jit(solution)/shard_map/reshape;squeeze | solution.py:212
  10.7 11.5 %all-to-all-start = ((bf16[32,64,2,256]{3,1,2,0:T(8,128)(2,1)}), bf16[32,64,2,256]{3,1,2,0:T(8,128)(2,1)S(1)}, u32[]{:S(2)}, u32[]{:S(2)}) async-start(bf16[32,64,2,256]{3,1,2,0:T(8,128)(2,1)} %copy.104), calls=%async_computation | async-start | bytes 4194304 | tf_op jit(solution)/shard_map/all_to_all | solution.py:213
  22.2 27.8 %all-to-all-done = bf16[32,64,2,256]{3,1,2,0:T(8,128)(2,1)S(1)} async-done(((bf16[32,64,2,256]{3,1,2,0:T(8,128)(2,1)}), bf16[32,64,2,256]{3,1,2,0:T(8,128)(2,1)S(1)}, u32[]{:S(2)}, u32[]{:S(2)}) %all-to-all-start) | async-done | bytes 2097184 | tf_op jit(solution)/shard_map/all_to_all | solution.py:213
  50.1 1.3 gather_fusion
  51.3 1.7 broadcast_select_fusion
  53.1 2.7 broadcast_in_dim.67
  55.8 5.9 %all-to-all-start.1 = ((bf16[4,256,1024]{2,1,0:T(8,128)(2,1)}), bf16[4,256,1024]{2,1,0:T(8,128)(2,1)S(1)}, u32[]{:S(2)}, u32[]{:S(2)}) async-start(bf16[4,256,1024]{2,1,0:T(8,128)(2,1)} %broadcast_in_dim.67), calls=%async_computation.1 | async-start | bytes 4194304 | tf_op jit(solution)/shard_map/all_to_all | solution.py:222
  61.7 0.8 copy.105
  62.5 1.0 eq.43
  63.5 1.0 eq.39
  64.6 0.7 reduce-window.19
  65.3 0.6 fusion.33
  66.0 3.1 %reduce-window.20 = s32[16,4,128]{2,0,1:T(8,128)} reduce-window(s32[16,4,128]{2,0,1:T(8,128)} %fusion.33, s32[]{:T(128)} %constant.31.clone.1), window={size=1x1x128 pad=0_0x0_0x127_0}, to_apply=%region_2.3 | reduce-window | flops 1040384 | bytes 65540 | tf_op jit(solution)/shard_map/reduce-window.1
  69.1 1.0 slice_reduce_fusion
  70.1 0.9 fusion.32
  71.0 0.8 min.28
  71.8 1.0 copy.108
  72.7 0.6 broadcast_multiply_fusion
  73.3 1.5 copy.112
  74.8 1.0 mul.126
  75.8 2.6 copy.98
  78.4 18.8 %all_gather.9 = bf16[256,1024]{1,0:T(8,128)(2,1)S(1)} all-gather(bf16[256,256]{1,0:T(8,128)(2,1)} %param.13), channel_id=1, replica_groups=mesh['req'=32,'exp'=4] {'exp'}, dimensions={1}, use_global_device_ids=true | all-gather | bytes 655360 | tf_op jit(solution)/shard_map/all_gather | solution.py:196
  97.2 0.2 fusion.18
  97.4 0.6 copy-done.2
  98.1 2.9 convolution_convert_fusion.1
  100.9 1.9 copy.99
  102.8 1.8 fusion.44
  104.6 1.7 copy.121
  106.3 1.7 copy.120
  107.9 1.7 copy.119
  109.6 0.6 compare_select_fusion
  110.2 0.6 add_select_fusion
  110.8 2.6 scatter_custom_fusion
  113.4 1.2 clamp_bitcast_fusion.group_ref
  114.6 1.2 bitcast_subtract_fusion.start_ref
  115.9 41.1 %all-gather.2.cloned.1.call-done = bf16[4,2048,2,256]{3,1,2,0:T(8,128)(2,1)} async-done(((bf16[4,64,2,256]{3,1,2,0:T(8,128)(2,1)}), bf16[4,2048,2,256]{3,1,2,0:T(8,128)(2,1)}) %all-gather.2.cloned.1.call-update) | async-done | bytes 8388624 | tf_op jit(solution)/shard_map/all_gather | solution.py:215
  156.9 16.8 %shard_map.140 = bf16[256,256]{1,0:T(8,128)(2,1)} custom-call(s32[4]{0:T(128)} %clamp_bitcast_fusion.group_ref, s32[4]{0:T(128)} %bitcast_subtract_fusion.start_ref, s32[4]{0:T(128)} %bitcast.105, bf16[256,256]{1,0:T(8,128)(2,1)} %bitcast.101, bf16[256,256]{1,0:T(8,128)(2,1)} %bitcast.100, bf16[256,256]{1,0:T(8,128)(2,1)} %bitcast.99, ...), custom_call_target="tpu_custom_call" | custom-call | flops 5171576832 | bytes 8912896 | tf_op jit(solution)/shard_map/pallas_call | solution.py:134
  173.7 8.5 %all_gather.11 = bf16[256,1024]{1,0:T(8,128)(2,1)} all-gather(bf16[256,256]{1,0:T(8,128)(2,1)} %shard_map.140), channel_id=1, replica_groups=mesh['req'=32,'exp'=4] {'exp'}, dimensions={1}, use_global_device_ids=true | all-gather | bytes 655360 | tf_op jit(solution)/shard_map/all_gather | solution.py:220
  182.2 2.0 multiply_reduce_fusion
  184.2 1.0 copy-done.1
  185.2 0.2 multiply_convert_fusion
  185.4 0.8 copy-done.3
  186.2 2.8 gather_fusion.1
  189.1 0.4 broadcast_in_dim.76
  189.5 40.6 %all_to_all.25 = bf16[32,1,40,1024]{3,2,1,0:T(8,128)(2,1)S(1)} all-to-all(bf16[32,1,40,1024]{3,2,1,0:T(8,128)(2,1)S(1)} %bitcast.91), channel_id=1, replica_groups=mesh['req'=32,'exp'=4] {'req'}, dimensions={0} | all-to-all | bytes 5242880 | tf_op jit(solution)/shard_map/all_to_all | solution.py:246
  230.1 2.3 fusion.5
  232.4 3.3 %convert_bitcast_fusion = bf16[32,1,40,1024]{3,2,1,0:T(8,128)(2,1)} fusion(f32[32,1,40,2,352]{4,2,3,0,1:T(8,128)S(1)} %fusion.5, bf16[1,352,1024]{2,1,0:T(8,128)(2,1)S(1)} %copy-done.9), kind=kOutput, calls=%fused_computation.7 | convolution fusion | flops 928563200 | bytes 6946816 | tf_op jit(solution)/shard_map/slch,lhd->slcd/dot_general | solution.py:178
  235.7 5.4 %all-to-all-start.3 = ((bf16[32,1,40,1024]{3,2,1,0:T(8,128)(2,1)}), bf16[32,1,40,1024]{3,2,1,0:T(8,128)(2,1)}, u32[]{:S(2)}, u32[]{:S(2)}) async-start(bf16[32,1,40,1024]{3,2,1,0:T(8,128)(2,1)} %convert_bitcast_fusion), calls=%async_computation.3 | async-start | bytes 5242880 | tf_op jit(solution)/shard_map/all_to_all | solution.py:248
  241.1 0.1 copy.109
  241.3 0.1 reshape.245
  241.4 0.2 lt.57
  241.6 0.1 copy.111
  241.7 0.2 fusion.45
  242.0 4.6 %gather_fusion.2 = f32[512]{0:T(512)S(1)} fusion(f32[256,16]{0,1:T(8,128)S(1)} %fusion.45, s32[512]{0:T(512)S(1)} %reshape.245), kind=kCustom, calls=%fused_computation.2 | custom fusion | bytes 8192 | tf_op jit(solution)/shard_map/jit(take_along_axis)/gather | solution.py:235
  246.5 0.1 reshape.248
  246.7 0.1 copy.110
  246.8 0.7 select_reduce_fusion
  247.5 27.4 %all-to-all-done.3 = bf16[32,1,40,1024]{3,2,1,0:T(8,128)(2,1)} async-done(((bf16[32,1,40,1024]{3,2,1,0:T(8,128)(2,1)}), bf16[32,1,40,1024]{3,2,1,0:T(8,128)(2,1)}, u32[]{:S(2)}, u32[]{:S(2)}) %all-to-all-start.3) | async-done | bytes 2621472 | tf_op jit(solution)/shard_map/all_to_all | solution.py:248
  274.9 3.3 %convolution_convert_fusion = bf16[256,1024]{1,0:T(8,128)(2,1)S(1)} fusion(f32[256,1280]{1,0:T(8,128)S(1)} %select_reduce_fusion, bf16[1280,1024]{1,0:T(8,128)(2,1)} %bitcast.35), kind=kOutput, calls=%fused_computation.27 | convolution fusion | flops 2013528064 | bytes 4456448 | tf_op jit(solution)/shard_map/dot_general | solution.py:258
  278.2 0.8 copy.126
  279.0 5.7 %all-to-all-start.4 = ((bf16[4,256,256]{2,1,0:T(8,128)(2,1)}), bf16[4,256,256]{2,1,0:T(8,128)(2,1)S(1)}, u32[]{:S(2)}, u32[]{:S(2)}) async-start(bf16[4,256,256]{2,1,0:T(8,128)(2,1)} %bitcast.89), calls=%async_computation.4 | async-start | bytes 1048576 | tf_op jit(solution)/shard_map/all_to_all | solution.py:268
  284.7 0.9 copy.115
  285.6 7.0 %all-to-all-done.4 = bf16[4,256,256]{2,1,0:T(8,128)(2,1)S(1)} async-done(((bf16[4,256,256]{2,1,0:T(8,128)(2,1)}), bf16[4,256,256]{2,1,0:T(8,128)(2,1)S(1)}, u32[]{:S(2)}, u32[]{:S(2)}) %all-to-all-start.4) | async-done | bytes 524320 | tf_op jit(solution)/shard_map/all_to_all | solution.py:268
  292.6 1.7 add_convert_fusion
  (40 shorter events, 0.3 us)
Async XLA Ops:
  7.2 222.9 %copy-start = (bf16[1,1024,2,352]{1,3,2,0:T(8,128)(2,1)S(1)}, bf16[1,1024,2,352]{1,3,2,0:T(8,128)(2,1)}, u32[]{:S(2)}) copy-start(bf16[1,1024,2,352]{1,3,2,0:T(8,128)(2,1)} %param.24) | copy-start | bytes 4325380
  10.7 11.5 %copy-start.10 = (s32[4]{0:T(128)S(1)}, s32[4]{0:T(128)}, u32[]{:S(2)}) copy-start(s32[4]{0:T(128)} %param.16) | copy-start | bytes 52
  10.7 39.4 %all-to-all-start = ((bf16[32,64,2,256]{3,1,2,0:T(8,128)(2,1)}), bf16[32,64,2,256]{3,1,2,0:T(8,128)(2,1)S(1)}, u32[]{:S(2)}, u32[]{:S(2)}) async-start(bf16[32,64,2,256]{3,1,2,0:T(8,128)(2,1)} %copy.104), calls=%async_computation | async-start | bytes 4194304 | tf_op jit(solution)/shard_map/all_to_all | solution.py:213
  22.1 134.8 %all-gather.2.cloned.1.call-start = ((), (), s32[]{:S(2)}) async-start(), calls=%async_computation.5 | async-start | bytes 8650752 | tf_op jit(solution)/shard_map/all_gather | solution.py:215
  55.8 5.9 %copy-start.6 = (s32[256,2]{0,1:T(2,128)S(1)}, s32[256,2]{0,1:T(2,128)}, u32[]{:S(2)}) copy-start(s32[256,2]{0,1:T(2,128)} %param.23) | copy-start | bytes 6148
  55.8 8.8 %copy-start.11 = (s32[1,4]{1,0:T(1,128)S(1)}, s32[1,4]{1,0:T(1,128)}, u32[]{:S(2)}) copy-start(s32[1,4]{1,0:T(1,128)} %param.14) | copy-start | bytes 52
  55.8 126.4 %all-to-all-start.1 = ((bf16[4,256,1024]{2,1,0:T(8,128)(2,1)}), bf16[4,256,1024]{2,1,0:T(8,128)(2,1)S(1)}, u32[]{:S(2)}, u32[]{:S(2)}) async-start(bf16[4,256,1024]{2,1,0:T(8,128)(2,1)} %broadcast_in_dim.67), calls=%async_computation.1 | async-start | bytes 4194304 | tf_op jit(solution)/shard_map/all_to_all | solution.py:222
  97.2 0.8 copy-start.2
  182.2 3.0 %copy-start.8 = (f32[1024]{0:T(1024)S(1)}, f32[1024]{0:T(1024)}, u32[]{:S(2)}) copy-start(f32[1024]{0:T(1024)} %param.21) | copy-start | bytes 12292
  184.2 1.0 copy-start.1
  185.4 0.8 copy-start.3
  230.1 2.3 copy-start.9
  235.7 6.0 %copy-start.4 = (bf16[256,1024]{1,0:T(8,128)(2,1)S(1)}, bf16[256,1024]{1,0:T(8,128)(2,1)}, u32[]{:S(2)}) copy-start(bf16[256,1024]{1,0:T(8,128)(2,1)} %copy-done.3) | copy-start | bytes 1572868
  235.7 6.0 %copy-start.7 = (bf16[1024,16]{0,1:T(8,128)(2,1)S(1)}, bf16[1024,16]{0,1:T(8,128)(2,1)}, u32[]{:S(2)}) copy-start(bf16[1024,16]{0,1:T(8,128)(2,1)} %param.22) | copy-start | bytes 98308
  235.7 39.2 %all-to-all-start.3 = ((bf16[32,1,40,1024]{3,2,1,0:T(8,128)(2,1)}), bf16[32,1,40,1024]{3,2,1,0:T(8,128)(2,1)}, u32[]{:S(2)}, u32[]{:S(2)}) async-start(bf16[32,1,40,1024]{3,2,1,0:T(8,128)(2,1)} %convert_bitcast_fusion), calls=%async_computation.3 | async-start | bytes 5242880 | tf_op jit(solution)/shard_map/all_to_all | solution.py:248
  278.1 6.5 %copy-start.5 = (bf16[256,768]{0,1:T(8,128)(2,1)S(1)}, bf16[256,768]{0,1:T(8,128)(2,1)}, u32[]{:S(2)}) copy-start(bf16[256,768]{0,1:T(8,128)(2,1)} %copy.99) | copy-start | bytes 1179652
  279.0 13.6 %all-to-all-start.4 = ((bf16[4,256,256]{2,1,0:T(8,128)(2,1)}), bf16[4,256,256]{2,1,0:T(8,128)(2,1)S(1)}, u32[]{:S(2)}, u32[]{:S(2)}) async-start(bf16[4,256,256]{2,1,0:T(8,128)(2,1)} %bitcast.89), calls=%async_computation.4 | async-start | bytes 1048576 | tf_op jit(solution)/shard_map/all_to_all | solution.py:268
Sparse Core Ops, SparseCore 0:
  53.2 103.6 all-gather.1

commit v13 on v12

--- a/solution.py
+++ b/solution.py
@@ -88,13 +88,11 @@
     context = jnp.zeros((rows, width), jnp.float32)
     for head in range(width // HEAD_DIM):
         in_head = lane_head == head
-        query_h = jnp.where(in_head, query, jnp.zeros_like(query))
+        query_h = jnp.where(in_head, query * jnp.asarray(scale, query.dtype), jnp.zeros_like(query))
         score_pre = lax.dot_general(
             query_h, prefix_keys, contract, preferred_element_type=jnp.float32
-        ) * scale
-        score_suf = lax.dot_general(
-            query_h, keys, contract, preferred_element_type=jnp.float32
-        ) * scale
+        )
+        score_suf = lax.dot_general(query_h, keys, contract, preferred_element_type=jnp.float32)
         score_suf = jnp.where(suffix_ok, score_suf, -1e30)
         highest = jnp.maximum(
             jnp.max(score_pre, axis=1, keepdims=True), jnp.max(score_suf, axis=1, keepdims=True)

time: 302 us -> 302 us (level)
  no operation moved by 1% of the time
where the time goes in v13:
time: 302 us; the launch traced here: 301 us
  waiting for transfers between devices  103 us (34%)
  blocking collectives  67.9 us (22%)
  local copies, waits for them, and re-layouts  42.2 us (14%)
  starting transfers between devices  28.5 us (9%)
  Pallas kernels  16.7 us (6%)
  between operations  14.3 us (5%)
  other arithmetic  14.2 us (5%)
  matrix products  14 us (5%)
    all_gather x1, waiting for transfers between devices, shards(): cached = lax.all_gather(owned, 'req', axis=1, tiled=True)  41.1 us
    all_to_all x1, blocking collectives, shards(): lax.all_to_all(outgoing_rows, 'req', split_axis=0, concat_axis=0, tiled=T...  40.6 us
    all_to_all x1, waiting for transfers between devices, shards(): lax.all_to_all(pieces, 'req', split_axis=0, concat_axis=0, tiled=True)  27.8 us
    all_to_all x1, waiting for transfers between devices, shards(): lax.all_to_all(partial_out.astype(jnp.bfloat16), 'req', split_axis=0, con...  27.4 us
    all_gather x1, blocking collectives, shards(): rows_whole = lax.all_gather(tokens, 'exp', axis=1, tiled=True)  18.8 us
    pallas_call x1, Pallas kernels, attention(): pl.pallas_call(attention_kernel, grid_spec=grid_spec, out_shape=jax.Shape...  16.7 us
    unnamed x30, local copies, waits for them, and re-layouts  11.7 us
    all_to_all x1, starting transfers between devices, shards(): lax.all_to_all(pieces, 'req', split_axis=0, concat_axis=0, tiled=True)  11.5 us
  transfers between devices with their start and end apart: 5, of which 4 were waited for; matrix products, arithmetic and copies ran while one was open for 15% of the time, Pallas kernels for 6%

profile of v13, /device:TPU:1, one launch (start us, length us, event | category | flops | bytes accessed | tf_op | source)
XLA Modules:
  0.0 301.0 jit_solution(12765132763272664142)
XLA Ops:
  7.2 3.5 %copy.104 = bf16[32,64,2,256]{3,1,2,0:T(8,128)(2,1)} copy(bf16[32,64,2,256]{3,2,1,0:T(2,128)(2,1)} %bitcast.96) | data formatting | bytes 4194304 | tf_op jit(solution)/shard_map/reshape;squeeze | solution.py:210
  10.7 11.5 %all-to-all-start = ((bf16[32,64,2,256]{3,1,2,0:T(8,128)(2,1)}), bf16[32,64,2,256]{3,1,2,0:T(8,128)(2,1)S(1)}, u32[]{:S(2)}, u32[]{:S(2)}) async-start(bf16[32,64,2,256]{3,1,2,0:T(8,128)(2,1)} %copy.104), calls=%async_computation | async-start | bytes 4194304 | tf_op jit(solution)/shard_map/all_to_all | solution.py:211
  22.2 27.8 %all-to-all-done = bf16[32,64,2,256]{3,1,2,0:T(8,128)(2,1)S(1)} async-done(((bf16[32,64,2,256]{3,1,2,0:T(8,128)(2,1)}), bf16[32,64,2,256]{3,1,2,0:T(8,128)(2,1)S(1)}, u32[]{:S(2)}, u32[]{:S(2)}) %all-to-all-start) | async-done | bytes 2097184 | tf_op jit(solution)/shard_map/all_to_all | solution.py:211
  50.1 1.3 gather_fusion
  51.3 1.7 broadcast_select_fusion
  53.1 2.7 broadcast_in_dim.67
  55.8 5.9 %all-to-all-start.1 = ((bf16[4,256,1024]{2,1,0:T(8,128)(2,1)}), bf16[4,256,1024]{2,1,0:T(8,128)(2,1)S(1)}, u32[]{:S(2)}, u32[]{:S(2)}) async-start(bf16[4,256,1024]{2,1,0:T(8,128)(2,1)} %broadcast_in_dim.67), calls=%async_computation.1 | async-start | bytes 4194304 | tf_op jit(solution)/shard_map/all_to_all | solution.py:220
  61.7 0.8 copy.105
  62.5 1.0 eq.43
  63.5 1.0 eq.39
  64.6 0.7 reduce-window.19
  65.3 0.6 fusion.33
  66.0 3.1 %reduce-window.20 = s32[16,4,128]{2,0,1:T(8,128)} reduce-window(s32[16,4,128]{2,0,1:T(8,128)} %fusion.33, s32[]{:T(128)} %constant.31.clone.1), window={size=1x1x128 pad=0_0x0_0x127_0}, to_apply=%region_2.3 | reduce-window | flops 1040384 | bytes 65540 | tf_op jit(solution)/shard_map/reduce-window.1
  69.1 1.0 slice_reduce_fusion
  70.1 0.9 fusion.32
  71.0 0.8 min.28
  71.8 1.0 copy.108
  72.7 0.6 broadcast_multiply_fusion
  73.3 1.5 copy.112
  74.8 1.0 mul.126
  75.8 2.6 copy.98
  78.4 18.8 %all_gather.9 = bf16[256,1024]{1,0:T(8,128)(2,1)S(1)} all-gather(bf16[256,256]{1,0:T(8,128)(2,1)} %param.13), channel_id=1, replica_groups=mesh['req'=32,'exp'=4] {'exp'}, dimensions={1}, use_global_device_ids=true | all-gather | bytes 655360 | tf_op jit(solution)/shard_map/all_gather | solution.py:194
  97.2 0.2 fusion.18
  97.4 0.6 copy-done.2
  98.1 2.9 convolution_convert_fusion.1
  100.9 1.9 copy.99
  102.8 1.8 fusion.44
  104.6 1.7 copy.121
  106.3 1.7 copy.120
  107.9 1.7 copy.119
  109.6 0.6 compare_select_fusion
  110.2 0.6 add_select_fusion
  110.8 2.6 scatter_custom_fusion
  113.4 1.2 clamp_bitcast_fusion.group_ref
  114.6 1.2 bitcast_subtract_fusion.start_ref
  115.9 41.1 %all-gather.2.cloned.1.call-done = bf16[4,2048,2,256]{3,1,2,0:T(8,128)(2,1)} async-done(((bf16[4,64,2,256]{3,1,2,0:T(8,128)(2,1)}), bf16[4,2048,2,256]{3,1,2,0:T(8,128)(2,1)}) %all-gather.2.cloned.1.call-update) | async-done | bytes 8388624 | tf_op jit(solution)/shard_map/all_gather | solution.py:213
  156.9 16.7 %shard_map.140 = bf16[256,256]{1,0:T(8,128)(2,1)} custom-call(s32[4]{0:T(128)} %clamp_bitcast_fusion.group_ref, s32[4]{0:T(128)} %bitcast_subtract_fusion.start_ref, s32[4]{0:T(128)} %bitcast.105, bf16[256,256]{1,0:T(8,128)(2,1)} %bitcast.101, bf16[256,256]{1,0:T(8,128)(2,1)} %bitcast.100, bf16[256,256]{1,0:T(8,128)(2,1)} %bitcast.99, ...), custom_call_target="tpu_custom_call" | custom-call | flops 5171576832 | bytes 8912896 | tf_op jit(solution)/shard_map/pallas_call | solution.py:132
  173.6 8.5 %all_gather.11 = bf16[256,1024]{1,0:T(8,128)(2,1)} all-gather(bf16[256,256]{1,0:T(8,128)(2,1)} %shard_map.140), channel_id=1, replica_groups=mesh['req'=32,'exp'=4] {'exp'}, dimensions={1}, use_global_device_ids=true | all-gather | bytes 655360 | tf_op jit(solution)/shard_map/all_gather | solution.py:218
  182.1 2.0 multiply_reduce_fusion
  184.1 1.0 copy-done.1
  185.1 0.2 multiply_convert_fusion
  185.3 0.8 copy-done.3
  186.2 2.8 gather_fusion.1
  189.0 0.4 broadcast_in_dim.76
  189.4 40.6 %all_to_all.25 = bf16[32,1,40,1024]{3,2,1,0:T(8,128)(2,1)S(1)} all-to-all(bf16[32,1,40,1024]{3,2,1,0:T(8,128)(2,1)S(1)} %bitcast.91), channel_id=1, replica_groups=mesh['req'=32,'exp'=4] {'req'}, dimensions={0} | all-to-all | bytes 5242880 | tf_op jit(solution)/shard_map/all_to_all | solution.py:244
  229.9 2.3 fusion.5
  232.3 3.3 %convert_bitcast_fusion = bf16[32,1,40,1024]{3,2,1,0:T(8,128)(2,1)} fusion(f32[32,1,40,2,352]{4,2,3,0,1:T(8,128)S(1)} %fusion.5, bf16[1,352,1024]{2,1,0:T(8,128)(2,1)S(1)} %copy-done.9), kind=kOutput, calls=%fused_computation.7 | convolution fusion | flops 928563200 | bytes 6946816 | tf_op jit(solution)/shard_map/slch,lhd->slcd/dot_general | solution.py:176
  235.5 5.4 %all-to-all-start.3 = ((bf16[32,1,40,1024]{3,2,1,0:T(8,128)(2,1)}), bf16[32,1,40,1024]{3,2,1,0:T(8,128)(2,1)}, u32[]{:S(2)}, u32[]{:S(2)}) async-start(bf16[32,1,40,1024]{3,2,1,0:T(8,128)(2,1)} %convert_bitcast_fusion), calls=%async_computation.3 | async-start | bytes 5242880 | tf_op jit(solution)/shard_map/all_to_all | solution.py:246
  241.0 0.1 copy.109
  241.2 0.1 reshape.245
  241.3 0.2 lt.57
  241.5 0.1 copy.111
  241.6 0.2 fusion.45
  241.8 4.6 %gather_fusion.2 = f32[512]{0:T(512)S(1)} fusion(f32[256,16]{0,1:T(8,128)S(1)} %fusion.45, s32[512]{0:T(512)S(1)} %reshape.245), kind=kCustom, calls=%fused_computation.2 | custom fusion | bytes 8192 | tf_op jit(solution)/shard_map/jit(take_along_axis)/gather | solution.py:233
  246.4 0.1 reshape.248
  246.6 0.1 copy.110
  246.7 0.7 select_reduce_fusion
  247.4 27.4 %all-to-all-done.3 = bf16[32,1,40,1024]{3,2,1,0:T(8,128)(2,1)} async-done(((bf16[32,1,40,1024]{3,2,1,0:T(8,128)(2,1)}), bf16[32,1,40,1024]{3,2,1,0:T(8,128)(2,1)}, u32[]{:S(2)}, u32[]{:S(2)}) %all-to-all-start.3) | async-done | bytes 2621472 | tf_op jit(solution)/shard_map/all_to_all | solution.py:246
  274.7 3.3 %convolution_convert_fusion = bf16[256,1024]{1,0:T(8,128)(2,1)S(1)} fusion(f32[256,1280]{1,0:T(8,128)S(1)} %select_reduce_fusion, bf16[1280,1024]{1,0:T(8,128)(2,1)} %bitcast.35), kind=kOutput, calls=%fused_computation.27 | convolution fusion | flops 2013528064 | bytes 4456448 | tf_op jit(solution)/shard_map/dot_general | solution.py:256
  278.0 0.8 copy.126
  278.9 5.7 %all-to-all-start.4 = ((bf16[4,256,256]{2,1,0:T(8,128)(2,1)}), bf16[4,256,256]{2,1,0:T(8,128)(2,1)S(1)}, u32[]{:S(2)}, u32[]{:S(2)}) async-start(bf16[4,256,256]{2,1,0:T(8,128)(2,1)} %bitcast.89), calls=%async_computation.4 | async-start | bytes 1048576 | tf_op jit(solution)/shard_map/all_to_all | solution.py:266
  284.6 0.9 copy.115
  285.5 7.0 %all-to-all-done.4 = bf16[4,256,256]{2,1,0:T(8,128)(2,1)S(1)} async-done(((bf16[4,256,256]{2,1,0:T(8,128)(2,1)}), bf16[4,256,256]{2,1,0:T(8,128)(2,1)S(1)}, u32[]{:S(2)}, u32[]{:S(2)}) %all-to-all-start.4) | async-done | bytes 524320 | tf_op jit(solution)/shard_map/all_to_all | solution.py:266
  292.5 1.7 add_convert_fusion
  (40 shorter events, 0.3 us)
Async XLA Ops:
  7.2 222.8 %copy-start = (bf16[1,1024,2,352]{1,3,2,0:T(8,128)(2,1)S(1)}, bf16[1,1024,2,352]{1,3,2,0:T(8,128)(2,1)}, u32[]{:S(2)}) copy-start(bf16[1,1024,2,352]{1,3,2,0:T(8,128)(2,1)} %param.24) | copy-start | bytes 4325380
  10.7 11.5 %copy-start.10 = (s32[4]{0:T(128)S(1)}, s32[4]{0:T(128)}, u32[]{:S(2)}) copy-start(s32[4]{0:T(128)} %param.16) | copy-start | bytes 52
  10.7 39.4 %all-to-all-start = ((bf16[32,64,2,256]{3,1,2,0:T(8,128)(2,1)}), bf16[32,64,2,256]{3,1,2,0:T(8,128)(2,1)S(1)}, u32[]{:S(2)}, u32[]{:S(2)}) async-start(bf16[32,64,2,256]{3,1,2,0:T(8,128)(2,1)} %copy.104), calls=%async_computation | async-start | bytes 4194304 | tf_op jit(solution)/shard_map/all_to_all | solution.py:211
  22.1 134.8 %all-gather.2.cloned.1.call-start = ((), (), s32[]{:S(2)}) async-start(), calls=%async_computation.5 | async-start | bytes 8650752 | tf_op jit(solution)/shard_map/all_gather | solution.py:213
  55.8 5.9 %copy-start.6 = (s32[256,2]{0,1:T(2,128)S(1)}, s32[256,2]{0,1:T(2,128)}, u32[]{:S(2)}) copy-start(s32[256,2]{0,1:T(2,128)} %param.23) | copy-start | bytes 6148
  55.8 8.8 %copy-start.11 = (s32[1,4]{1,0:T(1,128)S(1)}, s32[1,4]{1,0:T(1,128)}, u32[]{:S(2)}) copy-start(s32[1,4]{1,0:T(1,128)} %param.14) | copy-start | bytes 52
  55.8 126.3 %all-to-all-start.1 = ((bf16[4,256,1024]{2,1,0:T(8,128)(2,1)}), bf16[4,256,1024]{2,1,0:T(8,128)(2,1)S(1)}, u32[]{:S(2)}, u32[]{:S(2)}) async-start(bf16[4,256,1024]{2,1,0:T(8,128)(2,1)} %broadcast_in_dim.67), calls=%async_computation.1 | async-start | bytes 4194304 | tf_op jit(solution)/shard_map/all_to_all | solution.py:220
  97.2 0.8 copy-start.2
  182.1 3.0 %copy-start.8 = (f32[1024]{0:T(1024)S(1)}, f32[1024]{0:T(1024)}, u32[]{:S(2)}) copy-start(f32[1024]{0:T(1024)} %param.21) | copy-start | bytes 12292
  184.1 1.0 copy-start.1
  185.3 0.8 copy-start.3
  229.9 2.3 copy-start.9
  235.5 6.0 %copy-start.4 = (bf16[256,1024]{1,0:T(8,128)(2,1)S(1)}, bf16[256,1024]{1,0:T(8,128)(2,1)}, u32[]{:S(2)}) copy-start(bf16[256,1024]{1,0:T(8,128)(2,1)} %copy-done.3) | copy-start | bytes 1572868
  235.5 6.0 %copy-start.7 = (bf16[1024,16]{0,1:T(8,128)(2,1)S(1)}, bf16[1024,16]{0,1:T(8,128)(2,1)}, u32[]{:S(2)}) copy-start(bf16[1024,16]{0,1:T(8,128)(2,1)} %param.22) | copy-start | bytes 98308
  235.5 39.2 %all-to-all-start.3 = ((bf16[32,1,40,1024]{3,2,1,0:T(8,128)(2,1)}), bf16[32,1,40,1024]{3,2,1,0:T(8,128)(2,1)}, u32[]{:S(2)}, u32[]{:S(2)}) async-start(bf16[32,1,40,1024]{3,2,1,0:T(8,128)(2,1)} %convert_bitcast_fusion), calls=%async_computation.3 | async-start | bytes 5242880 | tf_op jit(solution)/shard_map/all_to_all | solution.py:246
  278.0 6.5 %copy-start.5 = (bf16[256,768]{0,1:T(8,128)(2,1)S(1)}, bf16[256,768]{0,1:T(8,128)(2,1)}, u32[]{:S(2)}) copy-start(bf16[256,768]{0,1:T(8,128)(2,1)} %copy.99) | copy-start | bytes 1179652
  278.9 13.6 %all-to-all-start.4 = ((bf16[4,256,256]{2,1,0:T(8,128)(2,1)}), bf16[4,256,256]{2,1,0:T(8,128)(2,1)S(1)}, u32[]{:S(2)}, u32[]{:S(2)}) async-start(bf16[4,256,256]{2,1,0:T(8,128)(2,1)} %bitcast.89), calls=%async_computation.4 | async-start | bytes 1048576 | tf_op jit(solution)/shard_map/all_to_all | solution.py:266
Sparse Core Ops, SparseCore 0:
  53.2 103.6 all-gather.1
